TPU v7x, 512 devices: a whole 4x4x16 slice. The times are simulated.
512 devices in a mesh: ref: 16 (over y_hi, x, core), dom: 32 (over y_lo, z).
Axes of the slice: x: 4, y: 4 (y_hi: 2, y_lo: 2; y = y_hi * 2 + y_lo), z: 16, core: 2. Of those that a mesh axis runs over, the one named last changes fastest.
Arguments:
- particles: bfloat16 [16384, 4096], P(('ref', 'dom'))
- inv_noise: float32 [16384], P(('ref', 'dom')), may hold values from 1 to 6
- candidates: int32 [16384, 8], P(('ref', 'dom')), may hold values from 0 to 127, as said below
- offsets: int32 [9, 2], replicated, may hold values from -2 to 2, as said below
- references: bfloat16 [128, 4096], P('ref')
Outputs:
- refreshed: bfloat16 [128, 4096], P('ref', 'dom')
- log_evidence: float32 [16384], P(('ref', 'dom'))
Inputs may be any that keep to these rules, and one draw needn't show every extreme that they name: `candidates`: each row names 8 different classes; class loads are uneven. `offsets`: 9 different shifts.
All inputs are finite; a program needn't handle non-finite values.
Results may differ from a plain program's by a relative error of at most 0.0038.
Values may be sent and summed in bfloat16 or wider, within the bound.
No kernel may reach another device: no remote copies, remote signals or barrier semaphores. Data moves between devices by JAX's collectives and lax.ppermute only.
A program may use at most 64 MiB of HBM per device.

v0:
```python
import jax
import jax.numpy as jnp
from jax import lax
from jax.sharding import Mesh
from jax.sharding import PartitionSpec as P

SIDE = 64
REF = ("yh", "x", "c")
DOM = ("yl", "z")
ALL = REF + DOM
HALVING = (
    ("c", 2, 1),
    ("yl", 2, 1),
    ("x", 4, 1),
    ("yh", 2, 1),
    ("x", 4, 2),
)


def shift_matrices(moves):
    line = jnp.arange(SIDE, dtype=jnp.int32)
    source = jnp.mod(line[None, :, None] - moves[:, None, None], SIDE)
    return (line[None, None, :] == source).astype(jnp.bfloat16)


def roll_set(images, offsets, sign):
    grid = images.reshape(images.shape[0], SIDE, SIDE)
    rows = shift_matrices(sign * offsets[:, 0])
    cols = shift_matrices(sign * offsets[:, 1])
    moved = jnp.einsum("sai,nij->snaj", rows, grid, preferred_element_type=jnp.float32).astype(jnp.bfloat16)
    moved = jnp.einsum("snaj,sbj->snab", moved, cols, preferred_element_type=jnp.float32).astype(jnp.bfloat16)
    return moved.reshape(offsets.shape[0], images.shape[0], SIDE * SIDE)


def partner(axis, size, bit):
    return [(i, i ^ bit) for i in range(size)]


def reduce_blocks(partial):
    t = partial.reshape(2, 2, 2, 2, 8, 2, 2, 2, 2, 2, 128)
    t = t.transpose(3, 5, 2, 0, 1, 6, 7, 8, 9, 4, 10)
    for axis, size, bit in HALVING:
        mine = (lax.axis_index(axis) // bit) % 2
        keep = lax.dynamic_index_in_dim(t, mine, 0, keepdims=False)
        send = lax.dynamic_index_in_dim(t, 1 - mine, 0, keepdims=False)
        t = keep + lax.ppermute(send, axis, partner(axis, size, bit))
    t = t.reshape(-1, *t.shape[-2:])
    return jnp.sum(lax.all_to_all(t, "z", 0, 0, tiled=True), axis=0)


def gather_rows(rows):
    copies = jnp.broadcast_to(rows[None], (16, *rows.shape))
    return lax.all_to_all(copies, REF, 0, 0, tiled=True).reshape(-1, rows.shape[1])


def per_device(particles, inv_noise, candidates, offsets, references):
    tile_size = references.shape[0]
    all_classes = tile_size * 16
    stacked = roll_set(particles, offsets, -1)
    tile_rows = gather_rows(references)
    tile_float = tile_rows.astype(jnp.float32)
    norms = jnp.sum(tile_float * tile_float, axis=1)
    match_score = jnp.einsum(
        "spi,ji->psj", stacked, tile_rows, preferred_element_type=jnp.float32
    )
    update = match_score - 0.5 * norms[None, None, :]
    score = inv_noise[:, None, None] * update
    classes = jnp.arange(all_classes, dtype=jnp.int32)
    permitted_mask = jnp.any(candidates[:, :, None] == classes[None, None, :], axis=1)
    masked = jnp.where(permitted_mask[:, None, :], score, -1e30)
    peak_val = jnp.max(masked, axis=(1, 2))
    denom_sum = jnp.sum(jnp.exp(masked - peak_val[:, None, None]), axis=(1, 2))
    evidence = peak_val + jnp.log(denom_sum)
    weight = jnp.where(
        permitted_mask[:, None, :], jnp.exp(masked - evidence[:, None, None]), 0.0
    ).astype(jnp.bfloat16)
    partial = jnp.einsum("psk,spq->kq", weight, stacked, preferred_element_type=jnp.float32)
    shares = reduce_blocks(partial)
    row_power = jnp.sum(shares * shares, axis=1)
    row_power = row_power + lax.ppermute(row_power, "yl", partner("yl", 2, 1))
    row_power = jnp.broadcast_to(row_power[None], (16, row_power.shape[0]))
    row_power = jnp.sum(lax.all_to_all(row_power, "z", 0, 0, tiled=True), axis=0)
    refreshed = (shares / jnp.sqrt(row_power[:, None] / (SIDE * SIDE) + 1e-06)).astype(jnp.bfloat16)
    return (refreshed, evidence)


def solution(mesh):
    assert mesh.devices.shape == (16, 32)
    fine = Mesh(mesh.devices.reshape(2, 4, 2, 2, 16), ALL)
    in_specs = (
        P(ALL, None),
        P(ALL),
        P(ALL, None),
        P(),
        P(REF, None),
    )
    out_specs = (P(REF, DOM), P(ALL))
    return jax.shard_map(
        per_device, mesh=fine, in_specs=in_specs, out_specs=out_specs, check_vma=False
    )
```

profile of v0, /device:TPU:6, one launch (start us, length us, event | category | flops | bytes accessed | tf_op | source)
XLA Modules:
  0.0 127.2 jit_solution(3782910056180237824)
XLA Ops:
  0.6 2.0 %broadcast_in_dim.30 = bf16[16,8,4096]{2,1,0:T(8,128)(2,1)} broadcast(bf16[8,4096]{1,0:T(8,128)(2,1)} %param.9), dimensions={1,2} | broadcast | bytes 1114112 | tf_op jit(solution)/shard_map/broadcast_in_dim | solution.py:52
  2.6 9.3 %all-to-all-start = ((bf16[16,8,4096]{2,1,0:T(8,128)(2,1)}), bf16[16,8,4096]{2,1,0:T(8,128)(2,1)S(1)}, u32[]{:S(2)}, u32[]{:S(2)}) async-start(bf16[16,8,4096]{2,1,0:T(8,128)(2,1)} %broadcast_in_dim.30), calls=%async_computation | async-start | bytes 2097152 | tf_op jit(solution)/shard_map/all_to_all | solution.py:53
  12.0 0.5 reshape.155
  12.6 4.4 %fusion.5 = bf16[9,32,64,64]{3,2,1,0:T(8,128)(2,1)} fusion(bf16[32,64,64,1]{2,1,0,3:T(8,128)(2,1)S(1)} %reshape.155, s32[9,64]{1,0:T(8,128)S(1)} %get-tuple-element.6, s32[9,64]{1,0:T(8,128)S(1)} %get-tuple-element.7), kind=kOutput, calls=%fused_computation.4 | convolution fusion | flops 304422912 | bytes 2626048 | tf_op jit(solution)/shard_map/snaj,sbj->snab/dot_general | solution.py:31
  17.0 6.1 %reshape.151 = bf16[9,32,4096]{2,1,0:T(8,128)(2,1)S(1)} reshape(bf16[9,32,64,64]{3,2,1,0:T(8,128)(2,1)} %fusion.5) | data formatting | bytes 4718592 | tf_op jit(solution)/shard_map/reshape | solution.py:32
  23.1 2.9 %dot_general.23 = bf16[2,2,2,2,2,128,32,9]{5,4,3,2,1,0,6,7:T(2,128)(2,1)} reshape(bf16[4096,32,9]{0,1,2:T(8,128)(2,1)S(1)} %bitcast.79) | data formatting | bytes 4718592 | tf_op jit(solution)/shard_map/psk,spq->kq/dot_general | solution.py:77
  26.1 0.1 fusion.28
  26.2 0.3 all-to-all-done
  26.4 0.3 multiply_reduce_fusion
  26.8 0.9 select_reduce_fusion
  27.7 0.2 exponential_reduce_fusion
  28.0 0.1 fusion.24
  28.1 0.2 copy.21
  28.3 2.6 %fusion.10 = f32[2,2,2,2,8,2,2,2,2,2,128]{10,4,9,8,7,6,5,3,2,1,0:T(8,128)S(1)} fusion(bf16[2,2,2,2,2,128,32,9,1,1,1,1]{5,4,3,2,1,0,6,7,11,10,9,8:T(2,128)(2,1)} %bitcast.80, bf16[2,2,2,2,8,32,9,1,1,1,1,1]{5,4,3,2,1,0,6,11,10,9,8,7:T(8,128)(2,1)S(1)} %bitcast.81), kind=kOutput, calls=%fused_computation.8 | convolution fusion | flops 301989888 | bytes 4530176 | tf_op jit(solution)/shard_map/psk,spq->kq/dot_general | solution.py:77
  30.9 0.1 dynamic-slice_bitcast_fusion
  31.1 2.8 %collective-permute-start = (f32[2,2,2,2,2,2,2,2,8,128]{9,8,7,6,5,4,0,1,3,2:T(8,128)S(1)}, f32[2,2,2,2,2,2,2,2,8,128]{9,8,7,6,5,4,0,1,3,2:T(8,128)}, u32[]{:S(2)}, u32[]{:S(2)}) collective-permute-start(f32[2,2,2,2,2,2,2,2,8,128]{9,8,7,6,5,4,0,1,3,2:T(8,128)S(1)} %dynamic-slice_bitcast_fusion), channel_id=1, source_target_pairs={{0,32},{32,0},{1,33},{33,1},{2,34},{34,2},{3,35},{35,3},{4,36},{36... | collective-permute-start | bytes 3145736 | tf_op jit(solution)/shard_map/ppermute | solution.py:46
  33.9 2.4 %collective-permute-done = f32[2,2,2,2,2,2,2,2,8,128]{9,8,7,6,5,4,0,1,3,2:T(8,128)} collective-permute-done((f32[2,2,2,2,2,2,2,2,8,128]{9,8,7,6,5,4,0,1,3,2:T(8,128)S(1)}, f32[2,2,2,2,2,2,2,2,8,128]{9,8,7,6,5,4,0,1,3,2:T(8,128)}, u32[]{:S(2)}, u32[]{:S(2)}) %collective-permute-start) | collective-permute-done | bytes 1048608 | tf_op jit(solution)/shard_map/ppermute | solution.py:46
  36.2 1.4 %bitcast_add_fusion = f32[2,2,2,2,2,2,2,2,8,128]{9,8,7,6,5,4,0,1,3,2:T(8,128)S(1)} fusion(f32[2,2,2,2,2,2,2,2,8,128]{9,8,7,6,5,4,0,1,3,2:T(8,128)} %collective-permute-done, f32[2,2,2,2,8,2,2,2,2,2,128]{10,4,9,8,7,6,5,3,2,1,0:T(8,128)S(1)} %fusion.10, s32[]{:T(128)S(6)} %select_n.104), kind=kLoop, calls=%fused_computation.11 | loop fusion | flops 262144 | bytes 3145732 | tf_op jit(solution)/shard_map/add | solution.py:46
  37.7 1.9 %collective-permute-start.1 = (f32[2,2,2,2,2,2,2,8,128]{8,7,6,5,4,3,0,2,1:T(8,128)S(1)}, f32[2,2,2,2,2,2,2,8,128]{8,7,6,5,4,3,0,2,1:T(8,128)S(1)}, u32[]{:S(2)}, u32[]{:S(2)}) collective-permute-start(f32[2,2,2,2,2,2,2,8,128]{8,7,6,5,4,3,0,2,1:T(8,128)S(1)} %dynamic-slice_bitcast_fusion.1), channel_id=1, source_target_pairs={{0,16},{16,0},{1,17},{17,1},{2,18},{18,2},{3,19},{19,3},{4,20},{20... | collective-permute-start | bytes 1572872 | tf_op jit(solution)/shard_map/ppermute | solution.py:46
  39.7 14.1 %collective-permute-done.1 = f32[2,2,2,2,2,2,2,8,128]{8,7,6,5,4,3,0,2,1:T(8,128)S(1)} collective-permute-done((f32[2,2,2,2,2,2,2,8,128]{8,7,6,5,4,3,0,2,1:T(8,128)S(1)}, f32[2,2,2,2,2,2,2,8,128]{8,7,6,5,4,3,0,2,1:T(8,128)S(1)}, u32[]{:S(2)}, u32[]{:S(2)}) %collective-permute-start.1) | collective-permute-done | bytes 524320 | tf_op jit(solution)/shard_map/ppermute | solution.py:46
  54.0 2.6 %collective-permute-start.2 = (f32[2,2,2,2,2,2,8,128]{7,6,5,4,3,2,1,0:T(8,128)S(1)}, f32[2,2,2,2,2,2,8,128]{7,6,5,4,3,2,1,0:T(8,128)S(1)}, u32[]{:S(2)}, u32[]{:S(2)}) collective-permute-start(f32[2,2,2,2,2,2,8,128]{7,6,5,4,3,2,1,0:T(8,128)S(1)} %dynamic-slice_bitcast_fusion.2), channel_id=1, source_target_pairs={{0,64},{64,0},{128,192},{192,128},{1,65},{65,1},{129,193},{193,129... | collective-permute-start | bytes 786440 | tf_op jit(solution)/shard_map/ppermute | solution.py:46
  56.6 7.0 %collective-permute-done.2 = f32[2,2,2,2,2,2,8,128]{7,6,5,4,3,2,1,0:T(8,128)S(1)} collective-permute-done((f32[2,2,2,2,2,2,8,128]{7,6,5,4,3,2,1,0:T(8,128)S(1)}, f32[2,2,2,2,2,2,8,128]{7,6,5,4,3,2,1,0:T(8,128)S(1)}, u32[]{:S(2)}, u32[]{:S(2)}) %collective-permute-start.2) | collective-permute-done | bytes 262176 | tf_op jit(solution)/shard_map/ppermute | solution.py:46
  63.7 3.7 %collective-permute-start.3 = (f32[2,2,2,2,2,8,128]{6,5,4,3,2,1,0:T(8,128)S(1)}, f32[2,2,2,2,2,8,128]{6,5,4,3,2,1,0:T(8,128)S(1)}, u32[]{:S(2)}, u32[]{:S(2)}) collective-permute-start(f32[2,2,2,2,2,8,128]{6,5,4,3,2,1,0:T(8,128)S(1)} %dynamic-slice_bitcast_fusion.3), channel_id=1, source_target_pairs={{0,256},{256,0},{1,257},{257,1},{2,258},{258,2},{3,259},{259,3},{4... | collective-permute-start | bytes 393224 | tf_op jit(solution)/shard_map/ppermute | solution.py:46
  67.4 4.6 %collective-permute-done.3 = f32[2,2,2,2,2,8,128]{6,5,4,3,2,1,0:T(8,128)S(1)} collective-permute-done((f32[2,2,2,2,2,8,128]{6,5,4,3,2,1,0:T(8,128)S(1)}, f32[2,2,2,2,2,8,128]{6,5,4,3,2,1,0:T(8,128)S(1)}, u32[]{:S(2)}, u32[]{:S(2)}) %collective-permute-start.3) | collective-permute-done | bytes 131104 | tf_op jit(solution)/shard_map/ppermute | solution.py:46
  72.1 4.3 %collective-permute-start.4 = (f32[2,2,2,2,8,128]{5,4,3,2,1,0:T(8,128)S(1)}, f32[2,2,2,2,8,128]{5,4,3,2,1,0:T(8,128)S(1)}, u32[]{:S(2)}, u32[]{:S(2)}) collective-permute-start(f32[2,2,2,2,8,128]{5,4,3,2,1,0:T(8,128)S(1)} %dynamic-slice_bitcast_fusion.4), channel_id=1, source_target_pairs={{0,128},{64,192},{128,0},{192,64},{1,129},{65,193},{129,1},{193,65... | collective-permute-start | bytes 196616 | tf_op jit(solution)/shard_map/ppermute | solution.py:46
  76.3 3.4 %collective-permute-done.4 = f32[2,2,2,2,8,128]{5,4,3,2,1,0:T(8,128)S(1)} collective-permute-done((f32[2,2,2,2,8,128]{5,4,3,2,1,0:T(8,128)S(1)}, f32[2,2,2,2,8,128]{5,4,3,2,1,0:T(8,128)S(1)}, u32[]{:S(2)}, u32[]{:S(2)}) %collective-permute-start.4) | collective-permute-done | bytes 65568 | tf_op jit(solution)/shard_map/ppermute | solution.py:46
  79.7 26.0 %all_to_all.16 = f32[16,8,128]{2,1,0:T(8,128)S(1)} all-to-all(f32[16,8,128]{2,1,0:T(8,128)S(1)} %bitcast.82), channel_id=1, replica_groups=mesh['yh'=2,'x'=4,'c'=2,'yl'=2,'z'=16] {'z'}, dimensions={0} | all-to-all | bytes 131072 | tf_op jit(solution)/shard_map/all_to_all | solution.py:48
  105.7 0.1 multiply_reduce_fusion.1
  105.8 2.6 %collective-permute-start.5 = (f32[8]{0:T(128)S(1)}, f32[8]{0:T(128)S(1)}, u32[]{:S(2)}, u32[]{:S(2)}) collective-permute-start(f32[8]{0:T(128)S(1)} %multiply_reduce_fusion.1), channel_id=1, source_target_pairs={{0,16},{16,0},{1,17},{17,1},{2,18},{18,2},{3,19},{19,3},{4,20},{20... | collective-permute-start | bytes 104 | tf_op jit(solution)/shard_map/ppermute | solution.py:80
  108.4 2.9 %collective-permute-done.5 = f32[8]{0:T(128)S(1)} collective-permute-done((f32[8]{0:T(128)S(1)}, f32[8]{0:T(128)S(1)}, u32[]{:S(2)}, u32[]{:S(2)}) %collective-permute-start.5) | collective-permute-done | bytes 64 | tf_op jit(solution)/shard_map/ppermute | solution.py:80
  111.3 15.1 %all_to_all.17 = f32[16,1,8]{2,1,0:T(1,128)S(1)} all-to-all(f32[16,1,8]{2,1,0:T(1,128)S(1)} %broadcast_in_dim.58), channel_id=1, replica_groups=mesh['yh'=2,'x'=4,'c'=2,'yl'=2,'z'=16] {'z'}, dimensions={0} | all-to-all | bytes 1024 | tf_op jit(solution)/shard_map/all_to_all | solution.py:82
  126.5 0.7 divide_convert_fusion
  (29 shorter events, 0.6 us)
Async XLA Ops:
  0.6 11.3 %copy-start = (bf16[32,4096]{1,0:T(8,128)(2,1)S(1)}, bf16[32,4096]{1,0:T(8,128)(2,1)}, u32[]{:S(2)}) copy-start(bf16[32,4096]{1,0:T(8,128)(2,1)} %param.5) | copy-start | bytes 786436
  0.6 11.9 %copy-start.2 = (s32[9,2]{0,1:T(2,128)S(1)}, s32[9,2]{0,1:T(2,128)}, u32[]{:S(2)}) copy-start(s32[9,2]{0,1:T(2,128)} %param.8) | copy-start | bytes 220
  2.6 23.8 %all-to-all-start = ((bf16[16,8,4096]{2,1,0:T(8,128)(2,1)}), bf16[16,8,4096]{2,1,0:T(8,128)(2,1)S(1)}, u32[]{:S(2)}, u32[]{:S(2)}) async-start(bf16[16,8,4096]{2,1,0:T(8,128)(2,1)} %broadcast_in_dim.30), calls=%async_computation | async-start | bytes 2097152 | tf_op jit(solution)/shard_map/all_to_all | solution.py:53
  23.1 2.9 %copy-start.1 = (s32[32,8]{0,1:T(8,128)S(1)}, s32[32,8]{0,1:T(8,128)}, u32[]{:S(2)}) copy-start(s32[32,8]{0,1:T(8,128)} %param.7) | copy-start | bytes 3076
  23.1 3.8 %copy-start.3 = (f32[32]{0:T(128)S(1)}, f32[32]{0:T(128)}, u32[]{:S(2)}) copy-start(f32[32]{0:T(128)} %param.6) | copy-start | bytes 388
  27.9 3.0 %copy-start.4 = (f32[32]{0:T(128)}, f32[32]{0:T(128)S(1)}, u32[]{:S(2)}) copy-start(f32[32]{0:T(128)S(1)} %log_add_fusion) | copy-start | bytes 388
  31.1 5.2 %collective-permute-start = (f32[2,2,2,2,2,2,2,2,8,128]{9,8,7,6,5,4,0,1,3,2:T(8,128)S(1)}, f32[2,2,2,2,2,2,2,2,8,128]{9,8,7,6,5,4,0,1,3,2:T(8,128)}, u32[]{:S(2)}, u32[]{:S(2)}) collective-permute-start(f32[2,2,2,2,2,2,2,2,8,128]{9,8,7,6,5,4,0,1,3,2:T(8,128)S(1)} %dynamic-slice_bitcast_fusion), channel_id=1, source_target_pairs={{0,32},{32,0},{1,33},{33,1},{2,34},{34,2},{3,35},{35,3},{4,36},{36... | collective-permute-start | bytes 3145736 | tf_op jit(solution)/shard_map/ppermute | solution.py:46
  37.7 16.1 %collective-permute-start.1 = (f32[2,2,2,2,2,2,2,8,128]{8,7,6,5,4,3,0,2,1:T(8,128)S(1)}, f32[2,2,2,2,2,2,2,8,128]{8,7,6,5,4,3,0,2,1:T(8,128)S(1)}, u32[]{:S(2)}, u32[]{:S(2)}) collective-permute-start(f32[2,2,2,2,2,2,2,8,128]{8,7,6,5,4,3,0,2,1:T(8,128)S(1)} %dynamic-slice_bitcast_fusion.1), channel_id=1, source_target_pairs={{0,16},{16,0},{1,17},{17,1},{2,18},{18,2},{3,19},{19,3},{4,20},{20... | collective-permute-start | bytes 1572872 | tf_op jit(solution)/shard_map/ppermute | solution.py:46
  54.0 9.6 %collective-permute-start.2 = (f32[2,2,2,2,2,2,8,128]{7,6,5,4,3,2,1,0:T(8,128)S(1)}, f32[2,2,2,2,2,2,8,128]{7,6,5,4,3,2,1,0:T(8,128)S(1)}, u32[]{:S(2)}, u32[]{:S(2)}) collective-permute-start(f32[2,2,2,2,2,2,8,128]{7,6,5,4,3,2,1,0:T(8,128)S(1)} %dynamic-slice_bitcast_fusion.2), channel_id=1, source_target_pairs={{0,64},{64,0},{128,192},{192,128},{1,65},{65,1},{129,193},{193,129... | collective-permute-start | bytes 786440 | tf_op jit(solution)/shard_map/ppermute | solution.py:46
  63.7 8.4 %collective-permute-start.3 = (f32[2,2,2,2,2,8,128]{6,5,4,3,2,1,0:T(8,128)S(1)}, f32[2,2,2,2,2,8,128]{6,5,4,3,2,1,0:T(8,128)S(1)}, u32[]{:S(2)}, u32[]{:S(2)}) collective-permute-start(f32[2,2,2,2,2,8,128]{6,5,4,3,2,1,0:T(8,128)S(1)} %dynamic-slice_bitcast_fusion.3), channel_id=1, source_target_pairs={{0,256},{256,0},{1,257},{257,1},{2,258},{258,2},{3,259},{259,3},{4... | collective-permute-start | bytes 393224 | tf_op jit(solution)/shard_map/ppermute | solution.py:46
  72.1 7.7 %collective-permute-start.4 = (f32[2,2,2,2,8,128]{5,4,3,2,1,0:T(8,128)S(1)}, f32[2,2,2,2,8,128]{5,4,3,2,1,0:T(8,128)S(1)}, u32[]{:S(2)}, u32[]{:S(2)}) collective-permute-start(f32[2,2,2,2,8,128]{5,4,3,2,1,0:T(8,128)S(1)} %dynamic-slice_bitcast_fusion.4), channel_id=1, source_target_pairs={{0,128},{64,192},{128,0},{192,64},{1,129},{65,193},{129,1},{193,65... | collective-permute-start | bytes 196616 | tf_op jit(solution)/shard_map/ppermute | solution.py:46
  105.8 5.5 %collective-permute-start.5 = (f32[8]{0:T(128)S(1)}, f32[8]{0:T(128)S(1)}, u32[]{:S(2)}, u32[]{:S(2)}) collective-permute-start(f32[8]{0:T(128)S(1)} %multiply_reduce_fusion.1), channel_id=1, source_target_pairs={{0,16},{16,0},{1,17},{17,1},{2,18},{18,2},{3,19},{19,3},{4,20},{20... | collective-permute-start | bytes 104 | tf_op jit(solution)/shard_map/ppermute | solution.py:80
where the time goes:
time: 129 us; the launch traced here: 127 us
  blocking collectives  41.1 us (32%)
  waiting for transfers between devices  34.6 us (27%)
  starting transfers between devices  27.2 us (21%)
  local copies, waits for them, and re-layouts  12.2 us (9%)
  matrix products  7.88 us (6%)
  other arithmetic  3.25 us (3%)
    ppermute x5, waiting for transfers between devices, reduce_blocks(): t = keep + lax.ppermute(send, axis, partner(axis, size, bit))  31.5 us
    all_to_all x1, blocking collectives, reduce_blocks(): return jnp.sum(lax.all_to_all(t, 'z', 0, 0, tiled=True), axis=0)  26 us
    ppermute x5, starting transfers between devices, reduce_blocks(): t = keep + lax.ppermute(send, axis, partner(axis, size, bit))  15.3 us
    all_to_all x1, blocking collectives, per_device(): lax.all_to_all(row_power, 'z', 0, 0, tiled=True)  15.1 us
    all_to_all x1, starting transfers between devices, gather_rows(): lax.all_to_all(copies, REF, 0, 0, tiled=True).reshape(-1, rows.shape[1])  9.3 us
    reshape x1, local copies, waits for them, and re-layouts, roll_set(): return moved.reshape(offsets.shape[0], images.shape[0], SIDE * SIDE)  6.09 us
    dot_general x1, matrix products, roll_set(): jnp.einsum('snaj,sbj->snab', moved, cols, preferred_element_type=jnp.floa...  4.35 us
    dot_general x1, local copies, waits for them, and re-layouts, per_device(): jnp.einsum('psk,spq->kq', weight, stacked, preferred_element_type=jnp.flo...  2.9 us
  transfers between devices with their start and end apart: 7, of which 7 were waited for; matrix products, arithmetic and copies ran while one was open for 11% of the time, Pallas kernels for 0%

commit v1 on v0

--- a/solution.py
+++ b/solution.py
@@ -8,13 +8,6 @@
 REF = ("yh", "x", "c")
 DOM = ("yl", "z")
 ALL = REF + DOM
-HALVING = (
-    ("c", 2, 1),
-    ("yl", 2, 1),
-    ("x", 4, 1),
-    ("yh", 2, 1),
-    ("x", 4, 2),
-)
 
 
 def shift_matrices(moves):
@@ -36,15 +29,26 @@
     return [(i, i ^ bit) for i in range(size)]
 
 
+def halve(t, axis, size, bit, dim):
+    mine = (lax.axis_index(axis) // bit) % 2
+    keep = lax.dynamic_index_in_dim(t, mine, dim, keepdims=False)
+    send = lax.dynamic_index_in_dim(t, 1 - mine, dim, keepdims=False)
+    return keep + lax.ppermute(send, axis, partner(axis, size, bit))
+
+
+def halve_pair(t, first, second):
+    mid = t.shape[2] // 2
+    a = halve(halve(lax.slice_in_dim(t, 0, mid, axis=2), *first, 0), *second, 0)
+    b = halve(halve(lax.slice_in_dim(t, mid, t.shape[2], axis=2), *second, 1), *first, 0)
+    return jnp.concatenate([a, b], axis=0)
+
+
 def reduce_blocks(partial):
-    t = partial.reshape(2, 2, 2, 2, 8, 2, 2, 2, 2, 2, 128)
-    t = t.transpose(3, 5, 2, 0, 1, 6, 7, 8, 9, 4, 10)
-    for axis, size, bit in HALVING:
-        mine = (lax.axis_index(axis) // bit) % 2
-        keep = lax.dynamic_index_in_dim(t, mine, 0, keepdims=False)
-        send = lax.dynamic_index_in_dim(t, 1 - mine, 0, keepdims=False)
-        t = keep + lax.ppermute(send, axis, partner(axis, size, bit))
-    t = t.reshape(-1, *t.shape[-2:])
+    t = partial.reshape(2, 2, 2, 2, 8, 2, 16, 128)
+    t = t.transpose(3, 5, 2, 0, 1, 6, 4, 7)
+    t = halve(t, "c", 2, 1, 0)
+    t = halve_pair(t, ("yl", 2, 1), ("x", 4, 1))
+    t = halve_pair(t, ("yh", 2, 1), ("x", 4, 2))
     return jnp.sum(lax.all_to_all(t, "z", 0, 0, tiled=True), axis=0)
 
 

time: 129 us -> 126 us (0.977); the launches traced: 127 us -> 126 us
  waiting for transfers between devices: 34.6 us -> 21.2 us
  starting transfers between devices: 27.2 us -> 39.9 us
    ppermute x5 -> x9, waiting for transfers between devices: 31.5 us -> 17.1 us  [halve(): return keep + lax.ppermute(send, axis, partner(axis, size, bit))]
    ppermute x5 -> x9, starting transfers between devices: 15.3 us -> 28 us  [halve(): return keep + lax.ppermute(send, axis, partner(axis, size, bit))]
    dot_general x1 -> x0, local copies, waits for them, and re-layouts: 2.9 us -> none  [per_device(): jnp.einsum('psk,spq->kq', weight, stacked, preferred_element_type=jnp.flo...]
    unnamed x11 -> x12, local copies, waits for them, and re-layouts: 0.1 us -> 2.02 us
  transfers between devices with their start and end apart: 7 -> 11, of which waited for: 7 -> 8; matrix products, arithmetic and copies ran while one was open for 11% -> 11% of each run, Pallas kernels for 0% -> 0%
where the time goes in v1:
time: 126 us
  blocking collectives  41.1 us (33%)
  starting transfers between devices  39.9 us (32%)
  waiting for transfers between devices  21.2 us (17%)
  local copies, waits for them, and re-layouts  11.3 us (9%)
  matrix products  7.89 us (6%)
  other arithmetic  3.19 us (3%)
    ppermute x9, starting transfers between devices, halve(): return keep + lax.ppermute(send, axis, partner(axis, size, bit))  28 us
    all_to_all x1, blocking collectives, reduce_blocks(): return jnp.sum(lax.all_to_all(t, 'z', 0, 0, tiled=True), axis=0)  25.9 us
    ppermute x9, waiting for transfers between devices, halve(): return keep + lax.ppermute(send, axis, partner(axis, size, bit))  17.1 us
    all_to_all x1, blocking collectives, per_device(): lax.all_to_all(row_power, 'z', 0, 0, tiled=True)  15.2 us
    all_to_all x1, starting transfers between devices, gather_rows(): lax.all_to_all(copies, REF, 0, 0, tiled=True).reshape(-1, rows.shape[1])  9.3 us
    reshape x1, local copies, waits for them, and re-layouts, roll_set(): return moved.reshape(offsets.shape[0], images.shape[0], SIDE * SIDE)  6.1 us
    dot_general x1, matrix products, roll_set(): jnp.einsum('snaj,sbj->snab', moved, cols, preferred_element_type=jnp.floa...  4.37 us
    ppermute x1, waiting for transfers between devices, per_device(): row_power = row_power + lax.ppermute(row_power, 'yl', partner('yl', 2, 1))  2.87 us
  transfers between devices with their start and end apart: 11, of which 8 were waited for; matrix products, arithmetic and copies ran while one was open for 11% of the time, Pallas kernels for 0%

profile of v1, /device:TPU:6, one launch (start us, length us, event | category | flops | bytes accessed | tf_op | source)
XLA Modules:
  0.0 125.6 jit_solution(8391002087048108264)
XLA Ops:
  0.6 2.0 %broadcast_in_dim.30 = bf16[16,8,4096]{2,1,0:T(8,128)(2,1)} broadcast(bf16[8,4096]{1,0:T(8,128)(2,1)} %param.9), dimensions={1,2} | broadcast | bytes 1114112 | tf_op jit(solution)/shard_map/broadcast_in_dim | solution.py:56
  2.6 9.3 %all-to-all-start = ((bf16[16,8,4096]{2,1,0:T(8,128)(2,1)}), bf16[16,8,4096]{2,1,0:T(8,128)(2,1)S(1)}, u32[]{:S(2)}, u32[]{:S(2)}) async-start(bf16[16,8,4096]{2,1,0:T(8,128)(2,1)} %broadcast_in_dim.30), calls=%async_computation | async-start | bytes 2097152 | tf_op jit(solution)/shard_map/all_to_all | solution.py:57
  11.9 0.5 reshape.151
  12.6 4.4 %fusion.5 = bf16[9,32,64,64]{3,2,1,0:T(8,128)(2,1)} fusion(bf16[32,64,64,1]{2,1,0,3:T(8,128)(2,1)S(1)} %reshape.151, s32[9,64]{1,0:T(8,128)S(1)} %get-tuple-element.8, s32[9,64]{1,0:T(8,128)S(1)} %get-tuple-element.9), kind=kOutput, calls=%fused_computation.4 | convolution fusion | flops 304422912 | bytes 2626048 | tf_op jit(solution)/shard_map/snaj,sbj->snab/dot_general | solution.py:24
  17.0 6.1 %reshape.148 = bf16[9,32,4096]{2,1,0:T(8,128)(2,1)S(1)} reshape(bf16[9,32,64,64]{3,2,1,0:T(8,128)(2,1)} %fusion.5) | data formatting | bytes 4718592 | tf_op jit(solution)/shard_map/reshape | solution.py:25
  23.2 1.9 %copy.37 = bf16[36,8,32,128]{3,2,1,0:T(8,128)(2,1)} copy(bf16[36,8,32,128]{3,1,2,0:T(8,128)(2,1)S(1)} %bitcast.101) | data formatting | bytes 4718592
  25.2 1.2 all-to-all-done
  26.4 0.3 multiply_reduce_fusion
  26.8 0.9 select_reduce_fusion
  28.0 0.2 copy.21
  28.3 2.6 %fusion.10 = f32[2,2,2,2,8,2,16,128]{7,4,6,5,3,2,1,0:T(8,128)S(1)} fusion(bf16[2,16,128,32,9,1,1,1,1]{2,1,0,3,4,8,7,6,5:T(8,128)(2,1)} %bitcast.102, bf16[2,2,2,2,8,32,9,1,1]{5,4,3,2,1,0,6,8,7:T(8,128)(2,1)S(1)} %bitcast.103), kind=kOutput, calls=%fused_computation.8 | convolution fusion | flops 301989888 | bytes 4530176 | tf_op jit(solution)/shard_map/psk,spq->kq/dot_general | solution.py:81
  31.0 2.8 %collective-permute-start = (f32[2,2,2,2,16,8,128]{6,5,4,0,1,3,2:T(8,128)S(1)}, f32[2,2,2,2,16,8,128]{6,5,4,0,1,3,2:T(8,128)}, u32[]{:S(2)}, u32[]{:S(2)}) collective-permute-start(f32[2,2,2,2,16,8,128]{6,5,4,0,1,3,2:T(8,128)S(1)} %dynamic-slice_bitcast_fusion), channel_id=1, source_target_pairs={{0,32},{32,0},{1,33},{33,1},{2,34},{34,2},{3,35},{35,3},{4,36},{36... | collective-permute-start | bytes 3145736 | tf_op jit(solution)/shard_map/ppermute | solution.py:36
  33.9 2.4 %collective-permute-done = f32[2,2,2,2,16,8,128]{6,5,4,0,1,3,2:T(8,128)} collective-permute-done((f32[2,2,2,2,16,8,128]{6,5,4,0,1,3,2:T(8,128)S(1)}, f32[2,2,2,2,16,8,128]{6,5,4,0,1,3,2:T(8,128)}, u32[]{:S(2)}, u32[]{:S(2)}) %collective-permute-start) | collective-permute-done | bytes 1048608 | tf_op jit(solution)/shard_map/ppermute | solution.py:36
  36.2 1.3 %bitcast_add_fusion = f32[2,2,2,2,16,8,128]{6,5,4,0,1,3,2:T(8,128)S(1)} fusion(f32[2,2,2,2,16,8,128]{6,5,4,0,1,3,2:T(8,128)} %collective-permute-done, f32[2,2,2,2,8,2,16,128]{7,4,6,5,3,2,1,0:T(8,128)S(1)} %fusion.10, s32[]{:T(128)S(6)} %select_n.126), kind=kLoop, calls=%fused_computation.11 | loop fusion | flops 262144 | bytes 3145732 | tf_op jit(solution)/shard_map/add | solution.py:36
  37.7 2.6 %collective-permute-start.3 = (f32[2,1,2,16,8,128]{5,4,3,0,2,1:T(8,128)S(1)}, f32[2,1,2,16,8,128]{5,4,3,0,2,1:T(8,128)S(1)}, u32[]{:S(2)}, u32[]{:S(2)}) collective-permute-start(f32[2,1,2,16,8,128]{5,4,3,0,2,1:T(8,128)S(1)} %dynamic-slice_bitcast_fusion.1), channel_id=1, source_target_pairs={{0,64},{64,0},{128,192},{192,128},{1,65},{65,1},{129,193},{193,129... | collective-permute-start | bytes 786440 | tf_op jit(solution)/shard_map/ppermute | solution.py:36
  40.5 1.9 %collective-permute-start.1 = (f32[2,1,2,16,8,128]{5,4,3,0,2,1:T(8,128)S(1)}, f32[2,1,2,16,8,128]{5,4,3,0,2,1:T(8,128)S(1)}, u32[]{:S(2)}, u32[]{:S(2)}) collective-permute-start(f32[2,1,2,16,8,128]{5,4,3,0,2,1:T(8,128)S(1)} %dynamic-slice_bitcast_fusion.2), channel_id=1, source_target_pairs={{0,16},{16,0},{1,17},{17,1},{2,18},{18,2},{3,19},{19,3},{4,20},{20... | collective-permute-start | bytes 786440 | tf_op jit(solution)/shard_map/ppermute | solution.py:36
  42.4 5.8 %collective-permute-done.3 = f32[2,1,2,16,8,128]{5,4,3,0,2,1:T(8,128)S(1)} collective-permute-done((f32[2,1,2,16,8,128]{5,4,3,0,2,1:T(8,128)S(1)}, f32[2,1,2,16,8,128]{5,4,3,0,2,1:T(8,128)S(1)}, u32[]{:S(2)}, u32[]{:S(2)}) %collective-permute-start.3) | collective-permute-done | bytes 262176 | tf_op jit(solution)/shard_map/ppermute | solution.py:36
  48.2 1.9 %collective-permute-start.4 = (f32[1,2,16,8,128]{4,3,2,1,0:T(8,128)S(1)}, f32[1,2,16,8,128]{4,3,2,1,0:T(8,128)S(1)}, u32[]{:S(2)}, u32[]{:S(2)}) collective-permute-start(f32[1,2,16,8,128]{4,3,2,1,0:T(8,128)S(1)} %dynamic-slice_bitcast_fusion.3), channel_id=1, source_target_pairs={{0,16},{16,0},{1,17},{17,1},{2,18},{18,2},{3,19},{19,3},{4,20},{20... | collective-permute-start | bytes 393224 | tf_op jit(solution)/shard_map/ppermute | solution.py:36
  50.2 0.5 collective-permute-done.1
  50.7 3.2 %collective-permute-start.2 = (f32[1,2,16,8,128]{4,3,2,1,0:T(8,128)S(1)}, f32[1,2,16,8,128]{4,3,2,1,0:T(8,128)S(1)}, u32[]{:S(2)}, u32[]{:S(2)}) collective-permute-start(f32[1,2,16,8,128]{4,3,2,1,0:T(8,128)S(1)} %dynamic-slice_bitcast_fusion.4), channel_id=1, source_target_pairs={{0,64},{64,0},{128,192},{192,128},{1,65},{65,1},{129,193},{193,129... | collective-permute-start | bytes 393224 | tf_op jit(solution)/shard_map/ppermute | solution.py:36
  53.9 1.2 collective-permute-done.4
  55.1 2.5 %collective-permute-done.2 = f32[1,2,16,8,128]{4,3,2,1,0:T(8,128)S(1)} collective-permute-done((f32[1,2,16,8,128]{4,3,2,1,0:T(8,128)S(1)}, f32[1,2,16,8,128]{4,3,2,1,0:T(8,128)S(1)}, u32[]{:S(2)}, u32[]{:S(2)}) %collective-permute-start.2) | collective-permute-done | bytes 131104 | tf_op jit(solution)/shard_map/ppermute | solution.py:36
  57.6 3.1 %collective-permute-start.5 = (f32[2,8,8,128]{3,2,1,0:T(8,128)S(1)}, f32[2,8,8,128]{3,2,1,0:T(8,128)S(1)}, u32[]{:S(2)}, u32[]{:S(2)}) collective-permute-start(f32[2,8,8,128]{3,2,1,0:T(8,128)S(1)} %dynamic-slice_bitcast_fusion.5), channel_id=1, source_target_pairs={{0,256},{256,0},{1,257},{257,1},{2,258},{258,2},{3,259},{259,3},{4... | collective-permute-start | bytes 196616 | tf_op jit(solution)/shard_map/ppermute | solution.py:36
  60.8 4.8 %collective-permute-start.7 = (f32[2,8,8,128]{3,2,1,0:T(8,128)S(1)}, f32[2,8,8,128]{3,2,1,0:T(8,128)S(1)}, u32[]{:S(2)}, u32[]{:S(2)}) collective-permute-start(f32[2,8,8,128]{3,2,1,0:T(8,128)S(1)} %fusion.31), channel_id=1, source_target_pairs={{0,128},{64,192},{128,0},{192,64},{1,129},{65,193},{129,1},{193,65... | collective-permute-start | bytes 196616 | tf_op jit(solution)/shard_map/ppermute | solution.py:36
  65.7 5.2 %collective-permute-start.6 = (f32[8,8,128]{2,1,0:T(8,128)S(1)}, f32[8,8,128]{2,1,0:T(8,128)S(1)}, u32[]{:S(2)}, u32[]{:S(2)}) collective-permute-start(f32[8,8,128]{2,1,0:T(8,128)S(1)} %dynamic-slice_bitcast_fusion.7), channel_id=1, source_target_pairs={{0,128},{64,192},{128,0},{192,64},{1,129},{65,193},{129,1},{193,65... | collective-permute-start | bytes 98312 | tf_op jit(solution)/shard_map/ppermute | solution.py:36
  70.9 2.4 %collective-permute-start.8 = (f32[8,8,128]{2,1,0:T(8,128)S(1)}, f32[8,8,128]{2,1,0:T(8,128)S(1)}, u32[]{:S(2)}, u32[]{:S(2)}) collective-permute-start(f32[8,8,128]{2,1,0:T(8,128)S(1)} %dynamic-slice_bitcast_fusion.6), channel_id=1, source_target_pairs={{0,256},{256,0},{1,257},{257,1},{2,258},{258,2},{3,259},{259,3},{4... | collective-permute-start | bytes 98312 | tf_op jit(solution)/shard_map/ppermute | solution.py:36
  73.4 4.9 %collective-permute-done.8 = f32[8,8,128]{2,1,0:T(8,128)S(1)} collective-permute-done((f32[8,8,128]{2,1,0:T(8,128)S(1)}, f32[8,8,128]{2,1,0:T(8,128)S(1)}, u32[]{:S(2)}, u32[]{:S(2)}) %collective-permute-start.8) | collective-permute-done | bytes 32800 | tf_op jit(solution)/shard_map/ppermute | solution.py:36
  78.3 25.9 %all_to_all.16 = f32[16,8,128]{2,1,0:T(8,128)S(1)} all-to-all(f32[16,8,128]{2,1,0:T(8,128)S(1)} %pad_maximum_fusion), channel_id=1, replica_groups=mesh['yh'=2,'x'=4,'c'=2,'yl'=2,'z'=16] {'z'}, dimensions={0} | all-to-all | bytes 131072 | tf_op jit(solution)/shard_map/all_to_all | solution.py:52
  104.3 2.6 %collective-permute-start.9 = (f32[8]{0:T(128)S(1)}, f32[8]{0:T(128)S(1)}, u32[]{:S(2)}, u32[]{:S(2)}) collective-permute-start(f32[8]{0:T(128)S(1)} %multiply_reduce_fusion.1), channel_id=1, source_target_pairs={{0,16},{16,0},{1,17},{17,1},{2,18},{18,2},{3,19},{19,3},{4,20},{20... | collective-permute-start | bytes 104 | tf_op jit(solution)/shard_map/ppermute | solution.py:84
  106.9 2.9 %collective-permute-done.9 = f32[8]{0:T(128)S(1)} collective-permute-done((f32[8]{0:T(128)S(1)}, f32[8]{0:T(128)S(1)}, u32[]{:S(2)}, u32[]{:S(2)}) %collective-permute-start.9) | collective-permute-done | bytes 64 | tf_op jit(solution)/shard_map/ppermute | solution.py:84
  109.8 15.2 %all_to_all.17 = f32[16,1,8]{2,1,0:T(1,128)S(1)} all-to-all(f32[16,1,8]{2,1,0:T(1,128)S(1)} %broadcast_in_dim.58), channel_id=1, replica_groups=mesh['yh'=2,'x'=4,'c'=2,'yl'=2,'z'=16] {'z'}, dimensions={0} | all-to-all | bytes 1024 | tf_op jit(solution)/shard_map/all_to_all | solution.py:86
  125.0 0.7 divide_convert_fusion
  (48 shorter events, 1.4 us)
Async XLA Ops:
  0.6 11.3 %copy-start = (bf16[32,4096]{1,0:T(8,128)(2,1)S(1)}, bf16[32,4096]{1,0:T(8,128)(2,1)}, u32[]{:S(2)}) copy-start(bf16[32,4096]{1,0:T(8,128)(2,1)} %param.5) | copy-start | bytes 786436
  0.6 11.9 %copy-start.2 = (s32[9,2]{0,1:T(2,128)S(1)}, s32[9,2]{0,1:T(2,128)}, u32[]{:S(2)}) copy-start(s32[9,2]{0,1:T(2,128)} %param.8) | copy-start | bytes 220
  2.6 23.8 %all-to-all-start = ((bf16[16,8,4096]{2,1,0:T(8,128)(2,1)}), bf16[16,8,4096]{2,1,0:T(8,128)(2,1)S(1)}, u32[]{:S(2)}, u32[]{:S(2)}) async-start(bf16[16,8,4096]{2,1,0:T(8,128)(2,1)} %broadcast_in_dim.30), calls=%async_computation | async-start | bytes 2097152 | tf_op jit(solution)/shard_map/all_to_all | solution.py:57
  17.0 6.1 %copy-start.1 = (s32[32,8]{0,1:T(8,128)S(1)}, s32[32,8]{0,1:T(8,128)}, u32[]{:S(2)}) copy-start(s32[32,8]{0,1:T(8,128)} %param.7) | copy-start | bytes 3076
  23.2 3.7 %copy-start.3 = (f32[32]{0:T(128)S(1)}, f32[32]{0:T(128)}, u32[]{:S(2)}) copy-start(f32[32]{0:T(128)} %param.6) | copy-start | bytes 388
  27.9 3.0 %copy-start.4 = (f32[32]{0:T(128)}, f32[32]{0:T(128)S(1)}, u32[]{:S(2)}) copy-start(f32[32]{0:T(128)S(1)} %log_add_fusion) | copy-start | bytes 388
  31.0 5.2 %collective-permute-start = (f32[2,2,2,2,16,8,128]{6,5,4,0,1,3,2:T(8,128)S(1)}, f32[2,2,2,2,16,8,128]{6,5,4,0,1,3,2:T(8,128)}, u32[]{:S(2)}, u32[]{:S(2)}) collective-permute-start(f32[2,2,2,2,16,8,128]{6,5,4,0,1,3,2:T(8,128)S(1)} %dynamic-slice_bitcast_fusion), channel_id=1, source_target_pairs={{0,32},{32,0},{1,33},{33,1},{2,34},{34,2},{3,35},{35,3},{4,36},{36... | collective-permute-start | bytes 3145736 | tf_op jit(solution)/shard_map/ppermute | solution.py:36
  37.7 10.5 %collective-permute-start.3 = (f32[2,1,2,16,8,128]{5,4,3,0,2,1:T(8,128)S(1)}, f32[2,1,2,16,8,128]{5,4,3,0,2,1:T(8,128)S(1)}, u32[]{:S(2)}, u32[]{:S(2)}) collective-permute-start(f32[2,1,2,16,8,128]{5,4,3,0,2,1:T(8,128)S(1)} %dynamic-slice_bitcast_fusion.1), channel_id=1, source_target_pairs={{0,64},{64,0},{128,192},{192,128},{1,65},{65,1},{129,193},{193,129... | collective-permute-start | bytes 786440 | tf_op jit(solution)/shard_map/ppermute | solution.py:36
  40.5 10.2 %collective-permute-start.1 = (f32[2,1,2,16,8,128]{5,4,3,0,2,1:T(8,128)S(1)}, f32[2,1,2,16,8,128]{5,4,3,0,2,1:T(8,128)S(1)}, u32[]{:S(2)}, u32[]{:S(2)}) collective-permute-start(f32[2,1,2,16,8,128]{5,4,3,0,2,1:T(8,128)S(1)} %dynamic-slice_bitcast_fusion.2), channel_id=1, source_target_pairs={{0,16},{16,0},{1,17},{17,1},{2,18},{18,2},{3,19},{19,3},{4,20},{20... | collective-permute-start | bytes 786440 | tf_op jit(solution)/shard_map/ppermute | solution.py:36
  48.2 6.9 %collective-permute-start.4 = (f32[1,2,16,8,128]{4,3,2,1,0:T(8,128)S(1)}, f32[1,2,16,8,128]{4,3,2,1,0:T(8,128)S(1)}, u32[]{:S(2)}, u32[]{:S(2)}) collective-permute-start(f32[1,2,16,8,128]{4,3,2,1,0:T(8,128)S(1)} %dynamic-slice_bitcast_fusion.3), channel_id=1, source_target_pairs={{0,16},{16,0},{1,17},{17,1},{2,18},{18,2},{3,19},{19,3},{4,20},{20... | collective-permute-start | bytes 393224 | tf_op jit(solution)/shard_map/ppermute | solution.py:36
  50.7 6.9 %collective-permute-start.2 = (f32[1,2,16,8,128]{4,3,2,1,0:T(8,128)S(1)}, f32[1,2,16,8,128]{4,3,2,1,0:T(8,128)S(1)}, u32[]{:S(2)}, u32[]{:S(2)}) collective-permute-start(f32[1,2,16,8,128]{4,3,2,1,0:T(8,128)S(1)} %dynamic-slice_bitcast_fusion.4), channel_id=1, source_target_pairs={{0,64},{64,0},{128,192},{192,128},{1,65},{65,1},{129,193},{193,129... | collective-permute-start | bytes 393224 | tf_op jit(solution)/shard_map/ppermute | solution.py:36
  57.6 8.0 %collective-permute-start.5 = (f32[2,8,8,128]{3,2,1,0:T(8,128)S(1)}, f32[2,8,8,128]{3,2,1,0:T(8,128)S(1)}, u32[]{:S(2)}, u32[]{:S(2)}) collective-permute-start(f32[2,8,8,128]{3,2,1,0:T(8,128)S(1)} %dynamic-slice_bitcast_fusion.5), channel_id=1, source_target_pairs={{0,256},{256,0},{1,257},{257,1},{2,258},{258,2},{3,259},{259,3},{4... | collective-permute-start | bytes 196616 | tf_op jit(solution)/shard_map/ppermute | solution.py:36
  60.8 10.1 %collective-permute-start.7 = (f32[2,8,8,128]{3,2,1,0:T(8,128)S(1)}, f32[2,8,8,128]{3,2,1,0:T(8,128)S(1)}, u32[]{:S(2)}, u32[]{:S(2)}) collective-permute-start(f32[2,8,8,128]{3,2,1,0:T(8,128)S(1)} %fusion.31), channel_id=1, source_target_pairs={{0,128},{64,192},{128,0},{192,64},{1,129},{65,193},{129,1},{193,65... | collective-permute-start | bytes 196616 | tf_op jit(solution)/shard_map/ppermute | solution.py:36
  65.7 7.7 %collective-permute-start.6 = (f32[8,8,128]{2,1,0:T(8,128)S(1)}, f32[8,8,128]{2,1,0:T(8,128)S(1)}, u32[]{:S(2)}, u32[]{:S(2)}) collective-permute-start(f32[8,8,128]{2,1,0:T(8,128)S(1)} %dynamic-slice_bitcast_fusion.7), channel_id=1, source_target_pairs={{0,128},{64,192},{128,0},{192,64},{1,129},{65,193},{129,1},{193,65... | collective-permute-start | bytes 98312 | tf_op jit(solution)/shard_map/ppermute | solution.py:36
  70.9 7.3 %collective-permute-start.8 = (f32[8,8,128]{2,1,0:T(8,128)S(1)}, f32[8,8,128]{2,1,0:T(8,128)S(1)}, u32[]{:S(2)}, u32[]{:S(2)}) collective-permute-start(f32[8,8,128]{2,1,0:T(8,128)S(1)} %dynamic-slice_bitcast_fusion.6), channel_id=1, source_target_pairs={{0,256},{256,0},{1,257},{257,1},{2,258},{258,2},{3,259},{259,3},{4... | collective-permute-start | bytes 98312 | tf_op jit(solution)/shard_map/ppermute | solution.py:36
  104.3 5.5 %collective-permute-start.9 = (f32[8]{0:T(128)S(1)}, f32[8]{0:T(128)S(1)}, u32[]{:S(2)}, u32[]{:S(2)}) collective-permute-start(f32[8]{0:T(128)S(1)} %multiply_reduce_fusion.1), channel_id=1, source_target_pairs={{0,16},{16,0},{1,17},{17,1},{2,18},{18,2},{3,19},{19,3},{4,20},{20... | collective-permute-start | bytes 104 | tf_op jit(solution)/shard_map/ppermute | solution.py:84

commit v2 on v1

--- a/solution.py
+++ b/solution.py
@@ -8,6 +8,7 @@
 REF = ("yh", "x", "c")
 DOM = ("yl", "z")
 ALL = REF + DOM
+SPREAD = ("yh", "x", "yl", "z")
 
 
 def shift_matrices(moves):
@@ -45,11 +46,10 @@
 
 def reduce_blocks(partial):
     t = partial.reshape(2, 2, 2, 2, 8, 2, 16, 128)
-    t = t.transpose(3, 5, 2, 0, 1, 6, 4, 7)
+    t = t.transpose(3, 0, 1, 2, 5, 6, 4, 7)
     t = halve(t, "c", 2, 1, 0)
-    t = halve_pair(t, ("yl", 2, 1), ("x", 4, 1))
-    t = halve_pair(t, ("yh", 2, 1), ("x", 4, 2))
-    return jnp.sum(lax.all_to_all(t, "z", 0, 0, tiled=True), axis=0)
+    t = t.reshape(-1, *t.shape[-2:])
+    return jnp.sum(lax.all_to_all(t, SPREAD, 0, 0, tiled=True), axis=0)
 
 
 def gather_rows(rows):
@@ -81,9 +81,8 @@
     partial = jnp.einsum("psk,spq->kq", weight, stacked, preferred_element_type=jnp.float32)
     shares = reduce_blocks(partial)
     row_power = jnp.sum(shares * shares, axis=1)
-    row_power = row_power + lax.ppermute(row_power, "yl", partner("yl", 2, 1))
-    row_power = jnp.broadcast_to(row_power[None], (16, row_power.shape[0]))
-    row_power = jnp.sum(lax.all_to_all(row_power, "z", 0, 0, tiled=True), axis=0)
+    row_power = jnp.broadcast_to(row_power[None], (32, row_power.shape[0]))
+    row_power = jnp.sum(lax.all_to_all(row_power, DOM, 0, 0, tiled=True), axis=0)
     refreshed = (shares / jnp.sqrt(row_power[:, None] / (SIDE * SIDE) + 1e-06)).astype(jnp.bfloat16)
     return (refreshed, evidence)
 

time: 126 us -> 133 us (1.056); the launches traced: 126 us -> 131 us
  blocking collectives: 41.1 us -> 92.4 us
  starting transfers between devices: 39.9 us -> 12.1 us
  waiting for transfers between devices: 21.2 us -> 3.62 us
    all_to_all x2, blocking collectives: 41.1 us -> 92.4 us  [the longest x1 74.6 us: reduce_blocks(): return jnp.sum(lax.all_to_all(t, SPREAD, 0, 0, tiled=True), axis=0)]
    ppermute x9 -> x1, starting transfers between devices: 28 us -> 2.79 us  [halve(): return keep + lax.ppermute(send, axis, partner(axis, size, bit))]
    ppermute x9 -> x1, waiting for transfers between devices: 17.1 us -> 2.39 us  [halve(): return keep + lax.ppermute(send, axis, partner(axis, size, bit))]
    ppermute x1 -> x0, waiting for transfers between devices: 2.87 us -> none  [per_device(): row_power = row_power + lax.ppermute(row_power, 'yl', partner('yl', 2, 1))]
    ppermute x1 -> x0, starting transfers between devices: 2.58 us -> none  [per_device(): row_power = row_power + lax.ppermute(row_power, 'yl', partner('yl', 2, 1))]
  transfers between devices with their start and end apart: 11 -> 2, of which waited for: 8 -> 2; matrix products, arithmetic and copies ran while one was open for 11% -> 10% of each run, Pallas kernels for 0% -> 0%
where the time goes in v2:
time: 133 us; the launch traced here: 131 us
  blocking collectives  92.4 us (69%)
  starting transfers between devices  12.1 us (9%)
  local copies, waits for them, and re-layouts  11.1 us (8%)
  matrix products  7.88 us (6%)
  waiting for transfers between devices  3.62 us (3%)
  other arithmetic  3.27 us (2%)
    all_to_all x1, blocking collectives, reduce_blocks(): return jnp.sum(lax.all_to_all(t, SPREAD, 0, 0, tiled=True), axis=0)  74.6 us
    all_to_all x1, blocking collectives, per_device(): lax.all_to_all(row_power, DOM, 0, 0, tiled=True)  17.8 us
    all_to_all x1, starting transfers between devices, gather_rows(): lax.all_to_all(copies, REF, 0, 0, tiled=True).reshape(-1, rows.shape[1])  9.3 us
    reshape x1, local copies, waits for them, and re-layouts, roll_set(): return moved.reshape(offsets.shape[0], images.shape[0], SIDE * SIDE)  6.09 us
    dot_general x1, matrix products, roll_set(): jnp.einsum('snaj,sbj->snab', moved, cols, preferred_element_type=jnp.floa...  4.35 us
    ppermute x1, starting transfers between devices, halve(): return keep + lax.ppermute(send, axis, partner(axis, size, bit))  2.79 us
  transfers between devices with their start and end apart: 2, of which 2 were waited for; matrix products, arithmetic and copies ran while one was open for 10% of the time, Pallas kernels for 0%

profile of v2, /device:TPU:6, one launch (start us, length us, event | category | flops | bytes accessed | tf_op | source)
XLA Modules:
  0.0 131.1 jit_solution(3054765651455602257)
XLA Ops:
  0.6 0.0 copy-start
  0.6 0.0 copy-start.2
  0.6 2.0 %broadcast_in_dim.30 = bf16[16,8,4096]{2,1,0:T(8,128)(2,1)} broadcast(bf16[8,4096]{1,0:T(8,128)(2,1)} %param.9), dimensions={1,2} | broadcast | bytes 1114112 | tf_op jit(solution)/shard_map/broadcast_in_dim | solution.py:56
  2.6 9.3 %all-to-all-start = ((bf16[16,8,4096]{2,1,0:T(8,128)(2,1)}), bf16[16,8,4096]{2,1,0:T(8,128)(2,1)S(1)}, u32[]{:S(2)}, u32[]{:S(2)}) async-start(bf16[16,8,4096]{2,1,0:T(8,128)(2,1)} %broadcast_in_dim.30), calls=%async_computation | async-start | bytes 2097152 | tf_op jit(solution)/shard_map/all_to_all | solution.py:57
  12.0 0.5 reshape.155
  12.5 0.1 add_select_fusion
  12.6 4.4 %fusion.5 = bf16[9,32,64,64]{3,2,1,0:T(8,128)(2,1)} fusion(bf16[32,64,64,1]{2,1,0,3:T(8,128)(2,1)S(1)} %reshape.155, s32[9,64]{1,0:T(8,128)S(1)} %get-tuple-element.6, s32[9,64]{1,0:T(8,128)S(1)} %get-tuple-element.7), kind=kOutput, calls=%fused_computation.4 | convolution fusion | flops 304422912 | bytes 2626048 | tf_op jit(solution)/shard_map/snaj,sbj->snab/dot_general | solution.py:25
  17.0 6.1 %reshape.151 = bf16[9,32,4096]{2,1,0:T(8,128)(2,1)S(1)} reshape(bf16[9,32,64,64]{3,2,1,0:T(8,128)(2,1)} %fusion.5) | data formatting | bytes 4718592 | tf_op jit(solution)/shard_map/reshape | solution.py:26
  23.1 0.0 copy-start.1
  23.1 0.0 copy-start.3
  23.1 1.9 %copy.37 = bf16[36,8,32,128]{3,2,1,0:T(8,128)(2,1)} copy(bf16[36,8,32,128]{3,1,2,0:T(8,128)(2,1)S(1)} %bitcast.68) | data formatting | bytes 4718592
  25.0 0.1 copy.20
  25.1 0.1 fusion.28
  25.2 1.2 all-to-all-done
  26.4 0.3 multiply_reduce_fusion
  26.7 0.1 mul.62
  26.8 0.9 select_reduce_fusion
  27.7 0.2 exponential_reduce_fusion
  27.9 0.0 copy-start.4
  28.0 0.1 fusion.24
  28.1 0.2 copy.21
  28.3 2.6 %fusion.10 = f32[2,2,2,2,8,2,16,128]{7,4,6,5,3,2,1,0:T(8,128)S(1)} fusion(bf16[2,16,128,32,9,1,1,1,1]{2,1,0,3,4,8,7,6,5:T(8,128)(2,1)} %bitcast.70, bf16[2,2,2,2,8,32,9,1,1]{5,4,3,2,1,0,6,8,7:T(8,128)(2,1)S(1)} %bitcast.71), kind=kOutput, calls=%fused_computation.8 | convolution fusion | flops 301989888 | bytes 4530176 | tf_op jit(solution)/shard_map/psk,spq->kq/dot_general | solution.py:81
  30.9 0.1 dynamic-slice_bitcast_fusion
  31.0 2.8 %collective-permute-start = (f32[2,2,2,2,16,8,128]{6,5,4,3,2,1,0:T(8,128)S(1)}, f32[2,2,2,2,16,8,128]{6,5,4,3,2,1,0:T(8,128)}, u32[]{:S(2)}, u32[]{:S(2)}) collective-permute-start(f32[2,2,2,2,16,8,128]{6,5,4,3,2,1,0:T(8,128)S(1)} %dynamic-slice_bitcast_fusion), channel_id=1, source_target_pairs={{0,32},{32,0},{1,33},{33,1},{2,34},{34,2},{3,35},{35,3},{4,36},{36... | collective-permute-start | bytes 3145736 | tf_op jit(solution)/shard_map/ppermute | solution.py:37
  33.9 2.4 %collective-permute-done = f32[2,2,2,2,16,8,128]{6,5,4,3,2,1,0:T(8,128)} collective-permute-done((f32[2,2,2,2,16,8,128]{6,5,4,3,2,1,0:T(8,128)S(1)}, f32[2,2,2,2,16,8,128]{6,5,4,3,2,1,0:T(8,128)}, u32[]{:S(2)}, u32[]{:S(2)}) %collective-permute-start) | collective-permute-done | bytes 1048608 | tf_op jit(solution)/shard_map/ppermute | solution.py:37
  36.2 1.3 %bitcast_add_fusion = f32[2,2,2,2,16,8,128]{6,5,4,3,2,1,0:T(8,128)S(1)} fusion(f32[2,2,2,2,16,8,128]{6,5,4,3,2,1,0:T(8,128)} %collective-permute-done, f32[2,2,2,2,8,2,16,128]{7,4,6,5,3,2,1,0:T(8,128)S(1)} %fusion.10, s32[]{:T(128)S(6)} %select_n.54), kind=kLoop, calls=%fused_computation.11 | loop fusion | flops 262144 | bytes 3145732 | tf_op jit(solution)/shard_map/add | solution.py:37
  37.6 74.6 %all_to_all.16 = f32[256,8,128]{2,1,0:T(8,128)S(1)} all-to-all(f32[256,8,128]{2,1,0:T(8,128)S(1)} %bitcast.69), channel_id=1, replica_groups=mesh['yh'=2,'x'=4,'c'=2,'yl'=2,'z'=16] {'yh','x','yl','z'}, dimensions={0} | all-to-all | bytes 2097152 | tf_op jit(solution)/shard_map/all_to_all | solution.py:52
  112.2 0.3 reduce_sum.47
  112.5 0.1 multiply_reduce_fusion.1
  112.6 17.8 %all_to_all.17 = f32[32,1,8]{2,1,0:T(1,128)S(1)} all-to-all(f32[32,1,8]{2,1,0:T(1,128)S(1)} %broadcast_in_dim.58), channel_id=1, replica_groups=mesh['yh'=2,'x'=4,'c'=2,'yl'=2,'z'=16] {'yl','z'}, dimensions={0} | all-to-all | bytes 2048 | tf_op jit(solution)/shard_map/all_to_all | solution.py:85
  130.4 0.1 reduce_sum.49
  130.4 0.7 divide_convert_fusion
  (10 shorter events, 0.1 us)
Async XLA Ops:
  0.6 11.3 %copy-start = (bf16[32,4096]{1,0:T(8,128)(2,1)S(1)}, bf16[32,4096]{1,0:T(8,128)(2,1)}, u32[]{:S(2)}) copy-start(bf16[32,4096]{1,0:T(8,128)(2,1)} %param.5) | copy-start | bytes 786436
  0.6 11.9 %copy-start.2 = (s32[9,2]{0,1:T(2,128)S(1)}, s32[9,2]{0,1:T(2,128)}, u32[]{:S(2)}) copy-start(s32[9,2]{0,1:T(2,128)} %param.8) | copy-start | bytes 220
  2.6 23.8 %all-to-all-start = ((bf16[16,8,4096]{2,1,0:T(8,128)(2,1)}), bf16[16,8,4096]{2,1,0:T(8,128)(2,1)S(1)}, u32[]{:S(2)}, u32[]{:S(2)}) async-start(bf16[16,8,4096]{2,1,0:T(8,128)(2,1)} %broadcast_in_dim.30), calls=%async_computation | async-start | bytes 2097152 | tf_op jit(solution)/shard_map/all_to_all | solution.py:57
  23.1 2.0 %copy-start.1 = (s32[32,8]{0,1:T(8,128)S(1)}, s32[32,8]{0,1:T(8,128)}, u32[]{:S(2)}) copy-start(s32[32,8]{0,1:T(8,128)} %param.7) | copy-start | bytes 3076
  23.1 3.8 %copy-start.3 = (f32[32]{0:T(128)S(1)}, f32[32]{0:T(128)}, u32[]{:S(2)}) copy-start(f32[32]{0:T(128)} %param.6) | copy-start | bytes 388
  27.9 3.0 %copy-start.4 = (f32[32]{0:T(128)}, f32[32]{0:T(128)S(1)}, u32[]{:S(2)}) copy-start(f32[32]{0:T(128)S(1)} %log_add_fusion) | copy-start | bytes 388
  31.0 5.2 %collective-permute-start = (f32[2,2,2,2,16,8,128]{6,5,4,3,2,1,0:T(8,128)S(1)}, f32[2,2,2,2,16,8,128]{6,5,4,3,2,1,0:T(8,128)}, u32[]{:S(2)}, u32[]{:S(2)}) collective-permute-start(f32[2,2,2,2,16,8,128]{6,5,4,3,2,1,0:T(8,128)S(1)} %dynamic-slice_bitcast_fusion), channel_id=1, source_target_pairs={{0,32},{32,0},{1,33},{33,1},{2,34},{34,2},{3,35},{35,3},{4,36},{36... | collective-permute-start | bytes 3145736 | tf_op jit(solution)/shard_map/ppermute | solution.py:37

commit v3 on v1

--- a/solution.py
+++ b/solution.py
@@ -10,19 +10,28 @@
 ALL = REF + DOM
 
 
-def shift_matrices(moves):
-    line = jnp.arange(SIDE, dtype=jnp.int32)
-    source = jnp.mod(line[None, :, None] - moves[:, None, None], SIDE)
-    return (line[None, None, :] == source).astype(jnp.bfloat16)
-
-
 def roll_set(images, offsets, sign):
-    grid = images.reshape(images.shape[0], SIDE, SIDE)
-    rows = shift_matrices(sign * offsets[:, 0])
-    cols = shift_matrices(sign * offsets[:, 1])
-    moved = jnp.einsum("sai,nij->snaj", rows, grid, preferred_element_type=jnp.float32).astype(jnp.bfloat16)
-    moved = jnp.einsum("snaj,sbj->snab", moved, cols, preferred_element_type=jnp.float32).astype(jnp.bfloat16)
-    return moved.reshape(offsets.shape[0], images.shape[0], SIDE * SIDE)
+    n = images.shape[0]
+    grid = images.reshape(n, SIDE // 2, 2 * SIDE)
+    row_move = sign * offsets[:, 0]
+    col_move = sign * offsets[:, 1]
+    half = jnp.arange(2, dtype=jnp.int32)
+    to_half = jnp.mod(half[None, :] + row_move[:, None], 2)
+    to_row = (half[None, :] + row_move[:, None] - to_half) // 2
+    lane = jnp.arange(2 * SIDE, dtype=jnp.int32)
+    lane_half, column = lane // SIDE, lane % SIDE
+    moved_column = jnp.mod(column[None, :] + col_move[:, None], SIDE)
+    lanes = (
+        (lane_half[None, None, :, None] == half[None, :, None, None])
+        & (lane_half[None, None, None, :] == to_half[:, :, None, None])
+        & (column[None, None, None, :] == moved_column[:, None, :, None])
+    ).astype(jnp.bfloat16)
+    line = jnp.arange(SIDE // 2, dtype=jnp.int32)
+    rows = (
+        line[None, None, None, :] == jnp.mod(line[None, None, :, None] - to_row[:, :, None, None], SIDE // 2)
+    ).astype(jnp.bfloat16)
+    moved = jnp.einsum("nrl,shlm->shnrm", grid, lanes, preferred_element_type=jnp.float32).astype(jnp.bfloat16)
+    return jnp.einsum("shqr,shnrm->snqm", rows, moved, preferred_element_type=jnp.float32).astype(jnp.bfloat16)
 
 
 def partner(axis, size, bit):
@@ -65,7 +74,8 @@
     tile_float = tile_rows.astype(jnp.float32)
     norms = jnp.sum(tile_float * tile_float, axis=1)
     match_score = jnp.einsum(
-        "spi,ji->psj", stacked, tile_rows, preferred_element_type=jnp.float32
+        "sprl,jrl->psj", stacked, tile_rows.reshape(tile_rows.shape[0], *stacked.shape[2:]),
+        preferred_element_type=jnp.float32,
     )
     update = match_score - 0.5 * norms[None, None, :]
     score = inv_noise[:, None, None] * update
@@ -78,7 +88,7 @@
     weight = jnp.where(
         permitted_mask[:, None, :], jnp.exp(masked - evidence[:, None, None]), 0.0
     ).astype(jnp.bfloat16)
-    partial = jnp.einsum("psk,spq->kq", weight, stacked, preferred_element_type=jnp.float32)
+    partial = jnp.einsum("psk,sprl->krl", weight, stacked, preferred_element_type=jnp.float32)
     shares = reduce_blocks(partial)
     row_power = jnp.sum(shares * shares, axis=1)
     row_power = row_power + lax.ppermute(row_power, "yl", partner("yl", 2, 1))

time: 126 us -> 129 us (1.024)
  local copies, waits for them, and re-layouts: 11.3 us -> 4.4 us
  waiting for transfers between devices: 21.2 us -> 27.5 us
  other arithmetic: 3.19 us -> 5.94 us
    reshape x2 -> x0, local copies, waits for them, and re-layouts: 6.63 us -> none  [the longest x1 6.1 us: roll_set(): return moved.reshape(offsets.shape[0], images.shape[0], SIDE * SIDE)]
    all_to_all x1, waiting for transfers between devices: 1.22 us -> 7.5 us  [gather_rows(): lax.all_to_all(copies, REF, 0, 0, tiled=True).reshape(-1, rows.shape[1])]
    eq x0 -> x3, other arithmetic: none -> 1.4 us  [the longest x1 0.67 us: roll_set(): lane_half[None, None, None, :] == to_half[:, :, None, None]]
  transfers between devices with their start and end apart: 11 -> 11, of which waited for: 8 -> 8; matrix products, arithmetic and copies ran while one was open for 11% -> 6% of each run, Pallas kernels for 0% -> 0%
where the time goes in v3:
time: 129 us; the launch traced here: 128 us
  blocking collectives  41.1 us (32%)
  starting transfers between devices  39.9 us (31%)
  waiting for transfers between devices  27.5 us (21%)
  matrix products  8.31 us (6%)
  other arithmetic  5.94 us (5%)
  local copies, waits for them, and re-layouts  4.4 us (3%)
    ppermute x9, starting transfers between devices, halve(): return keep + lax.ppermute(send, axis, partner(axis, size, bit))  28 us
    all_to_all x1, blocking collectives, reduce_blocks(): return jnp.sum(lax.all_to_all(t, 'z', 0, 0, tiled=True), axis=0)  25.9 us
    ppermute x9, waiting for transfers between devices, halve(): return keep + lax.ppermute(send, axis, partner(axis, size, bit))  17.1 us
    all_to_all x1, blocking collectives, per_device(): lax.all_to_all(row_power, 'z', 0, 0, tiled=True)  15.2 us
    all_to_all x1, starting transfers between devices, gather_rows(): lax.all_to_all(copies, REF, 0, 0, tiled=True).reshape(-1, rows.shape[1])  9.3 us
    all_to_all x1, waiting for transfers between devices, gather_rows(): lax.all_to_all(copies, REF, 0, 0, tiled=True).reshape(-1, rows.shape[1])  7.5 us
    dot_general x1, matrix products, roll_set(): jnp.einsum('shqr,shnrm->snqm', rows, moved, preferred_element_type=jnp.fl...  3.14 us
    ppermute x1, waiting for transfers between devices, per_device(): row_power = row_power + lax.ppermute(row_power, 'yl', partner('yl', 2, 1))  2.86 us
  transfers between devices with their start and end apart: 11, of which 8 were waited for; matrix products, arithmetic and copies ran while one was open for 6% of the time, Pallas kernels for 0%

profile of v3, /device:TPU:6, one launch (start us, length us, event | category | flops | bytes accessed | tf_op | source)
XLA Modules:
  0.0 128.3 jit_solution(6264722670151039064)
XLA Ops:
  0.7 2.0 %broadcast_in_dim.22 = bf16[16,8,4096]{2,1,0:T(8,128)(2,1)} broadcast(bf16[8,4096]{1,0:T(8,128)(2,1)} %param.9), dimensions={1,2} | broadcast | bytes 1114112 | tf_op jit(solution)/shard_map/broadcast_in_dim | solution.py:65
  2.6 9.3 %all-to-all-start = ((bf16[16,8,4096]{2,1,0:T(8,128)(2,1)}), bf16[16,8,4096]{2,1,0:T(8,128)(2,1)S(1)}, u32[]{:S(2)}, u32[]{:S(2)}) async-start(bf16[16,8,4096]{2,1,0:T(8,128)(2,1)} %broadcast_in_dim.22), calls=%async_computation | async-start | bytes 2097152 | tf_op jit(solution)/shard_map/all_to_all | solution.py:66
  12.0 0.5 iota_compare_fusion.2
  12.7 0.7 fusion.44
  13.4 0.7 copy.35
  14.2 0.7 broadcast_compare_fusion.1
  14.8 0.7 and_select_fusion
  15.7 3.1 %fusion.5 = bf16[9,32,32,128]{3,2,1,0:T(8,128)(2,1)S(1)} fusion(pred[9,128,128]{2,1,0:T(8,128)(4,1)S(1)} %broadcast_compare_fusion, pred[9,2,128]{2,1,0:T(4,128)(4,1)} %broadcast_compare_fusion.1, pred[2,128]{1,0:T(4,128)(4,1)} %iota_compare_fusion.2, bf16[32,32,128,1,1]{2,1,0,3,4:T(8,128)(2,1)} %bitcast.110, s32[9,2,32]{2,1,0:T(2,128)} %and_select_fusion), kind=kOutput, calls=%fused_computation.5 | convolution fusion | flops 759121920 | bytes 2773760 | tf_op jit(solution)/shard_map/shqr,shnrm->snqm/dot_general | solution.py:34
  18.9 7.5 %all-to-all-done = bf16[16,8,4096]{2,1,0:T(8,128)(2,1)S(1)} async-done(((bf16[16,8,4096]{2,1,0:T(8,128)(2,1)}), bf16[16,8,4096]{2,1,0:T(8,128)(2,1)S(1)}, u32[]{:S(2)}, u32[]{:S(2)}) %all-to-all-start) | async-done | bytes 1048608 | tf_op jit(solution)/shard_map/all_to_all | solution.py:66
  26.4 1.2 copy.36
  28.0 2.3 %fusion.66 = (f32[32]{0:T(128)S(1)}, f32[9,32,128]{2,1,0:T(8,128)S(1)}) fusion(f32[128]{0:T(128)S(1)} %mul.47, bf16[128,32,128]{2,1,0:T(8,128)(2,1)} %bitcast.108, bf16[9,32,32,128]{3,2,1,0:T(8,128)(2,1)S(1)} %fusion.5, f32[32]{0:T(128)S(1)} %copy-done.6, pred[32,128]{1,0:T(8,128)(4,1)S(1)} %copy-done.2), kind=kOutput, calls=%fused_computation.107 | convolution fusion | flops 302137312 | bytes 3560192 | tf_op jit(solution)/shard_map/sprl,jrl->psj/dot_general | solution.py:76
  30.6 2.8 %fusion.6 = f32[128,32,128,1]{2,0,3,1:T(8,128)S(1)} fusion(bf16[9,32,32,128]{3,2,1,0:T(8,128)(2,1)} %copy-done, f32[9,32,128]{2,1,0:T(8,128)S(1)} %get-tuple-element.9, f32[32]{0:T(128)S(1)} %log_add_fusion, pred[32,128]{1,0:T(8,128)(4,1)S(1)} %copy-done.2), kind=kOutput, calls=%fused_computation.6 | convolution fusion | flops 302100480 | bytes 4608128 | tf_op jit(solution)/shard_map/psk,sprl->krl/dot_general | solution.py:91
  33.6 2.8 %collective-permute-start = (f32[2,2,2,2,16,8,128]{6,5,1,3,2,4,0:T(8,128)S(1)}, f32[2,2,2,2,16,8,128]{6,5,1,3,2,4,0:T(8,128)}, u32[]{:S(2)}, u32[]{:S(2)}) collective-permute-start(f32[2,2,2,2,16,8,128]{6,5,1,3,2,4,0:T(8,128)S(1)} %dynamic-slice_bitcast_fusion), channel_id=1, source_target_pairs={{0,32},{32,0},{1,33},{33,1},{2,34},{34,2},{3,35},{35,3},{4,36},{36... | collective-permute-start | bytes 3145736 | tf_op jit(solution)/shard_map/ppermute | solution.py:45
  36.4 2.4 %collective-permute-done = f32[2,2,2,2,16,8,128]{6,5,1,3,2,4,0:T(8,128)} collective-permute-done((f32[2,2,2,2,16,8,128]{6,5,1,3,2,4,0:T(8,128)S(1)}, f32[2,2,2,2,16,8,128]{6,5,1,3,2,4,0:T(8,128)}, u32[]{:S(2)}, u32[]{:S(2)}) %collective-permute-start) | collective-permute-done | bytes 1048608 | tf_op jit(solution)/shard_map/ppermute | solution.py:45
  38.8 1.4 %bitcast_add_fusion = f32[2,2,2,2,16,8,128]{6,5,1,3,2,4,0:T(8,128)S(1)} fusion(f32[2,2,2,2,16,8,128]{6,5,1,3,2,4,0:T(8,128)} %collective-permute-done, f32[2,2,2,2,8,2,16,128]{7,4,3,2,1,0,6,5:T(8,128)S(1)} %bitcast.107, s32[]{:T(128)S(6)} %select_n.179), kind=kLoop, calls=%fused_computation.18 | loop fusion | flops 262144 | bytes 3145732 | tf_op jit(solution)/shard_map/add | solution.py:45
  40.3 2.6 %collective-permute-start.3 = (f32[2,1,2,16,8,128]{5,4,2,3,0,1:T(8,128)S(1)}, f32[2,1,2,16,8,128]{5,4,2,3,0,1:T(8,128)S(1)}, u32[]{:S(2)}, u32[]{:S(2)}) collective-permute-start(f32[2,1,2,16,8,128]{5,4,2,3,0,1:T(8,128)S(1)} %dynamic-slice_bitcast_fusion.1), channel_id=1, source_target_pairs={{0,64},{64,0},{128,192},{192,128},{1,65},{65,1},{129,193},{193,129... | collective-permute-start | bytes 786440 | tf_op jit(solution)/shard_map/ppermute | solution.py:45
  43.1 1.9 %collective-permute-start.1 = (f32[2,1,2,16,8,128]{5,4,0,2,3,1:T(8,128)S(1)}, f32[2,1,2,16,8,128]{5,4,0,2,3,1:T(8,128)S(1)}, u32[]{:S(2)}, u32[]{:S(2)}) collective-permute-start(f32[2,1,2,16,8,128]{5,4,0,2,3,1:T(8,128)S(1)} %dynamic-slice_bitcast_fusion.2), channel_id=1, source_target_pairs={{0,16},{16,0},{1,17},{17,1},{2,18},{18,2},{3,19},{19,3},{4,20},{20... | collective-permute-start | bytes 786440 | tf_op jit(solution)/shard_map/ppermute | solution.py:45
  45.0 5.8 %collective-permute-done.3 = f32[2,1,2,16,8,128]{5,4,2,3,0,1:T(8,128)S(1)} collective-permute-done((f32[2,1,2,16,8,128]{5,4,2,3,0,1:T(8,128)S(1)}, f32[2,1,2,16,8,128]{5,4,2,3,0,1:T(8,128)S(1)}, u32[]{:S(2)}, u32[]{:S(2)}) %collective-permute-start.3) | collective-permute-done | bytes 262176 | tf_op jit(solution)/shard_map/ppermute | solution.py:45
  50.9 1.9 %collective-permute-start.4 = (f32[1,2,16,8,128]{4,3,1,2,0:T(8,128)S(1)}, f32[1,2,16,8,128]{4,3,1,2,0:T(8,128)S(1)}, u32[]{:S(2)}, u32[]{:S(2)}) collective-permute-start(f32[1,2,16,8,128]{4,3,1,2,0:T(8,128)S(1)} %dynamic-slice_bitcast_fusion.3), channel_id=1, source_target_pairs={{0,16},{16,0},{1,17},{17,1},{2,18},{18,2},{3,19},{19,3},{4,20},{20... | collective-permute-start | bytes 393224 | tf_op jit(solution)/shard_map/ppermute | solution.py:45
  53.4 3.2 %collective-permute-start.2 = (f32[1,2,16,8,128]{4,3,1,2,0:T(8,128)S(1)}, f32[1,2,16,8,128]{4,3,1,2,0:T(8,128)S(1)}, u32[]{:S(2)}, u32[]{:S(2)}) collective-permute-start(f32[1,2,16,8,128]{4,3,1,2,0:T(8,128)S(1)} %dynamic-slice_bitcast_fusion.4), channel_id=1, source_target_pairs={{0,64},{64,0},{128,192},{192,128},{1,65},{65,1},{129,193},{193,129... | collective-permute-start | bytes 393224 | tf_op jit(solution)/shard_map/ppermute | solution.py:45
  56.6 1.2 collective-permute-done.4
  57.8 2.4 %collective-permute-done.2 = f32[1,2,16,8,128]{4,3,1,2,0:T(8,128)S(1)} collective-permute-done((f32[1,2,16,8,128]{4,3,1,2,0:T(8,128)S(1)}, f32[1,2,16,8,128]{4,3,1,2,0:T(8,128)S(1)}, u32[]{:S(2)}, u32[]{:S(2)}) %collective-permute-start.2) | collective-permute-done | bytes 131104 | tf_op jit(solution)/shard_map/ppermute | solution.py:45
  60.3 3.1 %collective-permute-start.5 = (f32[2,8,8,128]{3,2,0,1:T(8,128)S(1)}, f32[2,8,8,128]{3,2,0,1:T(8,128)S(1)}, u32[]{:S(2)}, u32[]{:S(2)}) collective-permute-start(f32[2,8,8,128]{3,2,0,1:T(8,128)S(1)} %dynamic-slice_bitcast_fusion.5), channel_id=1, source_target_pairs={{0,256},{256,0},{1,257},{257,1},{2,258},{258,2},{3,259},{259,3},{4... | collective-permute-start | bytes 196616 | tf_op jit(solution)/shard_map/ppermute | solution.py:45
  63.4 4.8 %collective-permute-start.7 = (f32[2,8,8,128]{3,2,1,0:T(8,128)S(1)}, f32[2,8,8,128]{3,2,1,0:T(8,128)S(1)}, u32[]{:S(2)}, u32[]{:S(2)}) collective-permute-start(f32[2,8,8,128]{3,2,1,0:T(8,128)S(1)} %fusion.51), channel_id=1, source_target_pairs={{0,128},{64,192},{128,0},{192,64},{1,129},{65,193},{129,1},{193,65... | collective-permute-start | bytes 196616 | tf_op jit(solution)/shard_map/ppermute | solution.py:45
  68.3 5.2 %collective-permute-start.6 = (f32[8,8,128]{2,1,0:T(8,128)S(1)}, f32[8,8,128]{2,1,0:T(8,128)S(1)}, u32[]{:S(2)}, u32[]{:S(2)}) collective-permute-start(f32[8,8,128]{2,1,0:T(8,128)S(1)} %dynamic-slice_bitcast_fusion.7), channel_id=1, source_target_pairs={{0,128},{64,192},{128,0},{192,64},{1,129},{65,193},{129,1},{193,65... | collective-permute-start | bytes 98312 | tf_op jit(solution)/shard_map/ppermute | solution.py:45
  73.5 2.4 %collective-permute-start.8 = (f32[8,8,128]{2,1,0:T(8,128)S(1)}, f32[8,8,128]{2,1,0:T(8,128)S(1)}, u32[]{:S(2)}, u32[]{:S(2)}) collective-permute-start(f32[8,8,128]{2,1,0:T(8,128)S(1)} %dynamic-slice_bitcast_fusion.6), channel_id=1, source_target_pairs={{0,256},{256,0},{1,257},{257,1},{2,258},{258,2},{3,259},{259,3},{4... | collective-permute-start | bytes 98312 | tf_op jit(solution)/shard_map/ppermute | solution.py:45
  76.0 4.9 %collective-permute-done.8 = f32[8,8,128]{2,1,0:T(8,128)S(1)} collective-permute-done((f32[8,8,128]{2,1,0:T(8,128)S(1)}, f32[8,8,128]{2,1,0:T(8,128)S(1)}, u32[]{:S(2)}, u32[]{:S(2)}) %collective-permute-start.8) | collective-permute-done | bytes 32800 | tf_op jit(solution)/shard_map/ppermute | solution.py:45
  80.9 25.9 %all_to_all.16 = f32[16,8,128]{2,1,0:T(8,128)S(1)} all-to-all(f32[16,8,128]{2,1,0:T(8,128)S(1)} %pad_maximum_fusion), channel_id=1, replica_groups=mesh['yh'=2,'x'=4,'c'=2,'yl'=2,'z'=16] {'z'}, dimensions={0} | all-to-all | bytes 131072 | tf_op jit(solution)/shard_map/all_to_all | solution.py:61
  106.9 2.6 %collective-permute-start.9 = (f32[8]{0:T(128)S(1)}, f32[8]{0:T(128)S(1)}, u32[]{:S(2)}, u32[]{:S(2)}) collective-permute-start(f32[8]{0:T(128)S(1)} %multiply_reduce_fusion.1), channel_id=1, source_target_pairs={{0,16},{16,0},{1,17},{17,1},{2,18},{18,2},{3,19},{19,3},{4,20},{20... | collective-permute-start | bytes 104 | tf_op jit(solution)/shard_map/ppermute | solution.py:94
  109.5 2.9 %collective-permute-done.9 = f32[8]{0:T(128)S(1)} collective-permute-done((f32[8]{0:T(128)S(1)}, f32[8]{0:T(128)S(1)}, u32[]{:S(2)}, u32[]{:S(2)}) %collective-permute-start.9) | collective-permute-done | bytes 64 | tf_op jit(solution)/shard_map/ppermute | solution.py:94
  112.4 15.2 %all_to_all.17 = f32[16,1,8]{2,1,0:T(1,128)S(1)} all-to-all(f32[16,1,8]{2,1,0:T(1,128)S(1)} %broadcast_in_dim.25), channel_id=1, replica_groups=mesh['yh'=2,'x'=4,'c'=2,'yl'=2,'z'=16] {'z'}, dimensions={0} | all-to-all | bytes 1024 | tf_op jit(solution)/shard_map/all_to_all | solution.py:96
  127.6 0.7 divide_convert_fusion
  (55 shorter events, 2.3 us)
Async XLA Ops:
  0.6 11.3 %copy-start.4 = (s32[9,2]{0,1:T(2,128)S(1)}, s32[9,2]{0,1:T(2,128)}, u32[]{:S(2)}) copy-start(s32[9,2]{0,1:T(2,128)} %param.8) | copy-start | bytes 220
  0.6 11.9 %copy-start.3 = (s32[32,8]{0,1:T(8,128)S(1)}, s32[32,8]{0,1:T(8,128)}, u32[]{:S(2)}) copy-start(s32[32,8]{0,1:T(8,128)} %param.7) | copy-start | bytes 3076
  0.7 12.8 %copy-start.1 = (bf16[32,4096]{1,0:T(8,128)(2,1)S(1)}, bf16[32,4096]{1,0:T(8,128)(2,1)}, u32[]{:S(2)}) copy-start(bf16[32,4096]{1,0:T(8,128)(2,1)} %param.5) | copy-start | bytes 786436
  2.6 23.8 %all-to-all-start = ((bf16[16,8,4096]{2,1,0:T(8,128)(2,1)}), bf16[16,8,4096]{2,1,0:T(8,128)(2,1)S(1)}, u32[]{:S(2)}, u32[]{:S(2)}) async-start(bf16[16,8,4096]{2,1,0:T(8,128)(2,1)} %broadcast_in_dim.22), calls=%async_computation | async-start | bytes 2097152 | tf_op jit(solution)/shard_map/all_to_all | solution.py:66
  18.9 11.5 %copy-start = (bf16[9,32,32,128]{3,2,1,0:T(8,128)(2,1)}, bf16[9,32,32,128]{3,2,1,0:T(8,128)(2,1)S(1)}, u32[]{:S(2)}) copy-start(bf16[9,32,32,128]{3,2,1,0:T(8,128)(2,1)S(1)} %fusion.5) | copy-start | bytes 7077892
  18.9 9.1 %copy-start.2 = (pred[32,128]{1,0:T(8,128)(4,1)S(1)}, pred[32,128]{1,0:T(8,128)(4,1)}, u32[]{:S(2)}) copy-start(pred[32,128]{1,0:T(8,128)(4,1)} %fusion.44) | copy-start | bytes 12292
  18.9 9.1 %copy-start.6 = (f32[32]{0:T(128)S(1)}, f32[32]{0:T(128)}, u32[]{:S(2)}) copy-start(f32[32]{0:T(128)} %param.6) | copy-start | bytes 388
  30.6 3.0 %copy-start.5 = (f32[32]{0:T(128)}, f32[32]{0:T(128)S(1)}, u32[]{:S(2)}) copy-start(f32[32]{0:T(128)S(1)} %log_add_fusion) | copy-start | bytes 388
  33.6 5.2 %collective-permute-start = (f32[2,2,2,2,16,8,128]{6,5,1,3,2,4,0:T(8,128)S(1)}, f32[2,2,2,2,16,8,128]{6,5,1,3,2,4,0:T(8,128)}, u32[]{:S(2)}, u32[]{:S(2)}) collective-permute-start(f32[2,2,2,2,16,8,128]{6,5,1,3,2,4,0:T(8,128)S(1)} %dynamic-slice_bitcast_fusion), channel_id=1, source_target_pairs={{0,32},{32,0},{1,33},{33,1},{2,34},{34,2},{3,35},{35,3},{4,36},{36... | collective-permute-start | bytes 3145736 | tf_op jit(solution)/shard_map/ppermute | solution.py:45
  40.3 10.5 %collective-permute-start.3 = (f32[2,1,2,16,8,128]{5,4,2,3,0,1:T(8,128)S(1)}, f32[2,1,2,16,8,128]{5,4,2,3,0,1:T(8,128)S(1)}, u32[]{:S(2)}, u32[]{:S(2)}) collective-permute-start(f32[2,1,2,16,8,128]{5,4,2,3,0,1:T(8,128)S(1)} %dynamic-slice_bitcast_fusion.1), channel_id=1, source_target_pairs={{0,64},{64,0},{128,192},{192,128},{1,65},{65,1},{129,193},{193,129... | collective-permute-start | bytes 786440 | tf_op jit(solution)/shard_map/ppermute | solution.py:45
  43.1 10.2 %collective-permute-start.1 = (f32[2,1,2,16,8,128]{5,4,0,2,3,1:T(8,128)S(1)}, f32[2,1,2,16,8,128]{5,4,0,2,3,1:T(8,128)S(1)}, u32[]{:S(2)}, u32[]{:S(2)}) collective-permute-start(f32[2,1,2,16,8,128]{5,4,0,2,3,1:T(8,128)S(1)} %dynamic-slice_bitcast_fusion.2), channel_id=1, source_target_pairs={{0,16},{16,0},{1,17},{17,1},{2,18},{18,2},{3,19},{19,3},{4,20},{20... | collective-permute-start | bytes 786440 | tf_op jit(solution)/shard_map/ppermute | solution.py:45
  50.9 6.9 %collective-permute-start.4 = (f32[1,2,16,8,128]{4,3,1,2,0:T(8,128)S(1)}, f32[1,2,16,8,128]{4,3,1,2,0:T(8,128)S(1)}, u32[]{:S(2)}, u32[]{:S(2)}) collective-permute-start(f32[1,2,16,8,128]{4,3,1,2,0:T(8,128)S(1)} %dynamic-slice_bitcast_fusion.3), channel_id=1, source_target_pairs={{0,16},{16,0},{1,17},{17,1},{2,18},{18,2},{3,19},{19,3},{4,20},{20... | collective-permute-start | bytes 393224 | tf_op jit(solution)/shard_map/ppermute | solution.py:45
  53.4 6.9 %collective-permute-start.2 = (f32[1,2,16,8,128]{4,3,1,2,0:T(8,128)S(1)}, f32[1,2,16,8,128]{4,3,1,2,0:T(8,128)S(1)}, u32[]{:S(2)}, u32[]{:S(2)}) collective-permute-start(f32[1,2,16,8,128]{4,3,1,2,0:T(8,128)S(1)} %dynamic-slice_bitcast_fusion.4), channel_id=1, source_target_pairs={{0,64},{64,0},{128,192},{192,128},{1,65},{65,1},{129,193},{193,129... | collective-permute-start | bytes 393224 | tf_op jit(solution)/shard_map/ppermute | solution.py:45
  60.3 7.9 %collective-permute-start.5 = (f32[2,8,8,128]{3,2,0,1:T(8,128)S(1)}, f32[2,8,8,128]{3,2,0,1:T(8,128)S(1)}, u32[]{:S(2)}, u32[]{:S(2)}) collective-permute-start(f32[2,8,8,128]{3,2,0,1:T(8,128)S(1)} %dynamic-slice_bitcast_fusion.5), channel_id=1, source_target_pairs={{0,256},{256,0},{1,257},{257,1},{2,258},{258,2},{3,259},{259,3},{4... | collective-permute-start | bytes 196616 | tf_op jit(solution)/shard_map/ppermute | solution.py:45
  63.4 10.1 %collective-permute-start.7 = (f32[2,8,8,128]{3,2,1,0:T(8,128)S(1)}, f32[2,8,8,128]{3,2,1,0:T(8,128)S(1)}, u32[]{:S(2)}, u32[]{:S(2)}) collective-permute-start(f32[2,8,8,128]{3,2,1,0:T(8,128)S(1)} %fusion.51), channel_id=1, source_target_pairs={{0,128},{64,192},{128,0},{192,64},{1,129},{65,193},{129,1},{193,65... | collective-permute-start | bytes 196616 | tf_op jit(solution)/shard_map/ppermute | solution.py:45
  68.3 7.7 %collective-permute-start.6 = (f32[8,8,128]{2,1,0:T(8,128)S(1)}, f32[8,8,128]{2,1,0:T(8,128)S(1)}, u32[]{:S(2)}, u32[]{:S(2)}) collective-permute-start(f32[8,8,128]{2,1,0:T(8,128)S(1)} %dynamic-slice_bitcast_fusion.7), channel_id=1, source_target_pairs={{0,128},{64,192},{128,0},{192,64},{1,129},{65,193},{129,1},{193,65... | collective-permute-start | bytes 98312 | tf_op jit(solution)/shard_map/ppermute | solution.py:45
  73.5 7.3 %collective-permute-start.8 = (f32[8,8,128]{2,1,0:T(8,128)S(1)}, f32[8,8,128]{2,1,0:T(8,128)S(1)}, u32[]{:S(2)}, u32[]{:S(2)}) collective-permute-start(f32[8,8,128]{2,1,0:T(8,128)S(1)} %dynamic-slice_bitcast_fusion.6), channel_id=1, source_target_pairs={{0,256},{256,0},{1,257},{257,1},{2,258},{258,2},{3,259},{259,3},{4... | collective-permute-start | bytes 98312 | tf_op jit(solution)/shard_map/ppermute | solution.py:45
  106.9 5.5 %collective-permute-start.9 = (f32[8]{0:T(128)S(1)}, f32[8]{0:T(128)S(1)}, u32[]{:S(2)}, u32[]{:S(2)}) collective-permute-start(f32[8]{0:T(128)S(1)} %multiply_reduce_fusion.1), channel_id=1, source_target_pairs={{0,16},{16,0},{1,17},{17,1},{2,18},{18,2},{3,19},{19,3},{4,20},{20... | collective-permute-start | bytes 104 | tf_op jit(solution)/shard_map/ppermute | solution.py:94

commit v4 on v1

--- a/solution.py
+++ b/solution.py
@@ -8,6 +8,7 @@
 REF = ("yh", "x", "c")
 DOM = ("yl", "z")
 ALL = REF + DOM
+PLANE = ("yh", "x", "yl")
 
 
 def shift_matrices(moves):
@@ -45,10 +46,10 @@
 
 def reduce_blocks(partial):
     t = partial.reshape(2, 2, 2, 2, 8, 2, 16, 128)
-    t = t.transpose(3, 5, 2, 0, 1, 6, 4, 7)
+    t = t.transpose(3, 0, 1, 2, 5, 6, 4, 7)
     t = halve(t, "c", 2, 1, 0)
-    t = halve_pair(t, ("yl", 2, 1), ("x", 4, 1))
-    t = halve_pair(t, ("yh", 2, 1), ("x", 4, 2))
+    t = t.reshape(-1, *t.shape[-3:])
+    t = jnp.sum(lax.all_to_all(t, PLANE, 0, 0, tiled=True), axis=0)
     return jnp.sum(lax.all_to_all(t, "z", 0, 0, tiled=True), axis=0)
 
 

time: 126 us -> 108 us (0.86); the launches traced: 126 us -> 106 us
  starting transfers between devices: 39.9 us -> 14.3 us
  blocking collectives: 41.1 us -> 62 us
  waiting for transfers between devices: 21.2 us -> 6.86 us
    ppermute x9 -> x1, starting transfers between devices: 28 us -> 2.79 us  [halve(): return keep + lax.ppermute(send, axis, partner(axis, size, bit))]
    all_to_all x0 -> x1, blocking collectives: none -> 21 us  [reduce_blocks(): t = jnp.sum(lax.all_to_all(t, PLANE, 0, 0, tiled=True), axis=0)]
    ppermute x9 -> x1, waiting for transfers between devices: 17.1 us -> 2.39 us  [halve(): return keep + lax.ppermute(send, axis, partner(axis, size, bit))]
  transfers between devices with their start and end apart: 11 -> 3, of which waited for: 8 -> 3; matrix products, arithmetic and copies ran while one was open for 11% -> 12% of each run, Pallas kernels for 0% -> 0%
where the time goes in v4:
time: 108 us; the launch traced here: 106 us
  blocking collectives  62 us (57%)
  starting transfers between devices  14.3 us (13%)
  local copies, waits for them, and re-layouts  11.1 us (10%)
  matrix products  7.88 us (7%)
  waiting for transfers between devices  6.86 us (6%)
  other arithmetic  3.06 us (3%)
    all_to_all x1, blocking collectives, reduce_blocks(): return jnp.sum(lax.all_to_all(t, 'z', 0, 0, tiled=True), axis=0)  25.9 us
    all_to_all x1, blocking collectives, reduce_blocks(): t = jnp.sum(lax.all_to_all(t, PLANE, 0, 0, tiled=True), axis=0)  21 us
    all_to_all x1, blocking collectives, per_device(): lax.all_to_all(row_power, 'z', 0, 0, tiled=True)  15.2 us
    all_to_all x1, starting transfers between devices, gather_rows(): lax.all_to_all(copies, REF, 0, 0, tiled=True).reshape(-1, rows.shape[1])  9.3 us
    reshape x1, local copies, waits for them, and re-layouts, roll_set(): return moved.reshape(offsets.shape[0], images.shape[0], SIDE * SIDE)  6.09 us
    dot_general x1, matrix products, roll_set(): jnp.einsum('snaj,sbj->snab', moved, cols, preferred_element_type=jnp.floa...  4.35 us
    ppermute x1, waiting for transfers between devices, per_device(): row_power = row_power + lax.ppermute(row_power, 'yl', partner('yl', 2, 1))  3.24 us
    ppermute x1, starting transfers between devices, halve(): return keep + lax.ppermute(send, axis, partner(axis, size, bit))  2.79 us
  transfers between devices with their start and end apart: 3, of which 3 were waited for; matrix products, arithmetic and copies ran while one was open for 12% of the time, Pallas kernels for 0%

profile of v4, /device:TPU:6, one launch (start us, length us, event | category | flops | bytes accessed | tf_op | source)
XLA Modules:
  0.0 106.0 jit_solution(13126677421487688347)
XLA Ops:
  0.6 2.0 %broadcast_in_dim.30 = bf16[16,8,4096]{2,1,0:T(8,128)(2,1)} broadcast(bf16[8,4096]{1,0:T(8,128)(2,1)} %param.9), dimensions={1,2} | broadcast | bytes 1114112 | tf_op jit(solution)/shard_map/broadcast_in_dim | solution.py:57
  2.6 9.3 %all-to-all-start = ((bf16[16,8,4096]{2,1,0:T(8,128)(2,1)}), bf16[16,8,4096]{2,1,0:T(8,128)(2,1)S(1)}, u32[]{:S(2)}, u32[]{:S(2)}) async-start(bf16[16,8,4096]{2,1,0:T(8,128)(2,1)} %broadcast_in_dim.30), calls=%async_computation | async-start | bytes 2097152 | tf_op jit(solution)/shard_map/all_to_all | solution.py:58
  12.0 0.5 reshape.155
  12.5 0.1 add_select_fusion
  12.6 4.4 %fusion.5 = bf16[9,32,64,64]{3,2,1,0:T(8,128)(2,1)} fusion(bf16[32,64,64,1]{2,1,0,3:T(8,128)(2,1)S(1)} %reshape.155, s32[9,64]{1,0:T(8,128)S(1)} %get-tuple-element.6, s32[9,64]{1,0:T(8,128)S(1)} %get-tuple-element.7), kind=kOutput, calls=%fused_computation.4 | convolution fusion | flops 304422912 | bytes 2626048 | tf_op jit(solution)/shard_map/snaj,sbj->snab/dot_general | solution.py:25
  17.0 6.1 %reshape.151 = bf16[9,32,4096]{2,1,0:T(8,128)(2,1)S(1)} reshape(bf16[9,32,64,64]{3,2,1,0:T(8,128)(2,1)} %fusion.5) | data formatting | bytes 4718592 | tf_op jit(solution)/shard_map/reshape | solution.py:26
  23.1 0.0 copy-start.1
  23.1 0.0 copy-start.3
  23.1 1.9 %copy.37 = bf16[36,8,32,128]{3,2,1,0:T(8,128)(2,1)} copy(bf16[36,8,32,128]{3,1,2,0:T(8,128)(2,1)S(1)} %bitcast.68) | data formatting | bytes 4718592
  25.0 0.1 copy.20
  25.1 0.1 fusion.28
  25.2 1.2 %all-to-all-done = bf16[16,8,4096]{2,1,0:T(8,128)(2,1)S(1)} async-done(((bf16[16,8,4096]{2,1,0:T(8,128)(2,1)}), bf16[16,8,4096]{2,1,0:T(8,128)(2,1)S(1)}, u32[]{:S(2)}, u32[]{:S(2)}) %all-to-all-start) | async-done | bytes 1048608 | tf_op jit(solution)/shard_map/all_to_all | solution.py:58
  26.4 0.3 multiply_reduce_fusion
  26.7 0.1 mul.62
  26.8 0.9 select_reduce_fusion
  27.7 0.2 exponential_reduce_fusion
  27.9 0.0 copy-start.4
  28.0 0.1 fusion.24
  28.1 0.2 copy.21
  28.3 2.6 %fusion.10 = f32[2,2,2,2,8,2,16,128]{7,4,6,5,3,2,1,0:T(8,128)S(1)} fusion(bf16[2,16,128,32,9,1,1,1,1]{2,1,0,3,4,8,7,6,5:T(8,128)(2,1)} %bitcast.70, bf16[2,2,2,2,8,32,9,1,1]{5,4,3,2,1,0,6,8,7:T(8,128)(2,1)S(1)} %bitcast.71), kind=kOutput, calls=%fused_computation.8 | convolution fusion | flops 301989888 | bytes 4530176 | tf_op jit(solution)/shard_map/psk,spq->kq/dot_general | solution.py:82
  30.9 0.1 dynamic-slice_bitcast_fusion
  31.0 2.8 %collective-permute-start = (f32[2,2,2,2,16,8,128]{6,5,4,3,2,1,0:T(8,128)S(1)}, f32[2,2,2,2,16,8,128]{6,5,4,3,2,1,0:T(8,128)}, u32[]{:S(2)}, u32[]{:S(2)}) collective-permute-start(f32[2,2,2,2,16,8,128]{6,5,4,3,2,1,0:T(8,128)S(1)} %dynamic-slice_bitcast_fusion), channel_id=1, source_target_pairs={{0,32},{32,0},{1,33},{33,1},{2,34},{34,2},{3,35},{35,3},{4,36},{36... | collective-permute-start | bytes 3145736 | tf_op jit(solution)/shard_map/ppermute | solution.py:37
  33.9 2.4 %collective-permute-done = f32[2,2,2,2,16,8,128]{6,5,4,3,2,1,0:T(8,128)} collective-permute-done((f32[2,2,2,2,16,8,128]{6,5,4,3,2,1,0:T(8,128)S(1)}, f32[2,2,2,2,16,8,128]{6,5,4,3,2,1,0:T(8,128)}, u32[]{:S(2)}, u32[]{:S(2)}) %collective-permute-start) | collective-permute-done | bytes 1048608 | tf_op jit(solution)/shard_map/ppermute | solution.py:37
  36.2 1.3 %bitcast_add_fusion = f32[2,2,2,2,16,8,128]{6,5,4,3,2,1,0:T(8,128)S(1)} fusion(f32[2,2,2,2,16,8,128]{6,5,4,3,2,1,0:T(8,128)} %collective-permute-done, f32[2,2,2,2,8,2,16,128]{7,4,6,5,3,2,1,0:T(8,128)S(1)} %fusion.10, s32[]{:T(128)S(6)} %select_n.54), kind=kLoop, calls=%fused_computation.11 | loop fusion | flops 262144 | bytes 3145732 | tf_op jit(solution)/shard_map/add | solution.py:37
  37.6 21.0 %all_to_all.21 = f32[16,16,8,128]{3,2,1,0:T(8,128)S(1)} all-to-all(f32[16,16,8,128]{3,2,1,0:T(8,128)S(1)} %bitcast.69), channel_id=1, replica_groups=mesh['yh'=2,'x'=4,'c'=2,'yl'=2,'z'=16] {'yh','x','yl'}, dimensions={0} | all-to-all | bytes 2097152 | tf_op jit(solution)/shard_map/all_to_all | solution.py:52
  58.6 0.1 reduce_sum.56
  58.6 25.9 %all_to_all.22 = f32[16,8,128]{2,1,0:T(8,128)S(1)} all-to-all(f32[16,8,128]{2,1,0:T(8,128)S(1)} %reduce_sum.56), channel_id=1, replica_groups=mesh['yh'=2,'x'=4,'c'=2,'yl'=2,'z'=16] {'z'}, dimensions={0} | all-to-all | bytes 131072 | tf_op jit(solution)/shard_map/all_to_all | solution.py:53
  84.5 0.1 multiply_reduce_fusion.1
  84.6 2.2 %collective-permute-start.1 = (f32[8]{0:T(128)S(1)}, f32[8]{0:T(128)S(1)}, u32[]{:S(2)}, u32[]{:S(2)}) collective-permute-start(f32[8]{0:T(128)S(1)} %multiply_reduce_fusion.1), channel_id=1, source_target_pairs={{0,16},{16,0},{1,17},{17,1},{2,18},{18,2},{3,19},{19,3},{4,20},{20... | collective-permute-start | bytes 104 | tf_op jit(solution)/shard_map/ppermute | solution.py:85
  86.8 3.2 %collective-permute-done.1 = f32[8]{0:T(128)S(1)} collective-permute-done((f32[8]{0:T(128)S(1)}, f32[8]{0:T(128)S(1)}, u32[]{:S(2)}, u32[]{:S(2)}) %collective-permute-start.1) | collective-permute-done | bytes 64 | tf_op jit(solution)/shard_map/ppermute | solution.py:85
  90.1 15.2 %all_to_all.23 = f32[16,1,8]{2,1,0:T(1,128)S(1)} all-to-all(f32[16,1,8]{2,1,0:T(1,128)S(1)} %broadcast_in_dim.58), channel_id=1, replica_groups=mesh['yh'=2,'x'=4,'c'=2,'yl'=2,'z'=16] {'z'}, dimensions={0} | all-to-all | bytes 1024 | tf_op jit(solution)/shard_map/all_to_all | solution.py:87
  105.3 0.7 divide_convert_fusion
  (15 shorter events, 0.1 us)
Async XLA Ops:
  0.6 11.3 %copy-start = (bf16[32,4096]{1,0:T(8,128)(2,1)S(1)}, bf16[32,4096]{1,0:T(8,128)(2,1)}, u32[]{:S(2)}) copy-start(bf16[32,4096]{1,0:T(8,128)(2,1)} %param.5) | copy-start | bytes 786436
  0.6 11.9 %copy-start.2 = (s32[9,2]{0,1:T(2,128)S(1)}, s32[9,2]{0,1:T(2,128)}, u32[]{:S(2)}) copy-start(s32[9,2]{0,1:T(2,128)} %param.8) | copy-start | bytes 220
  2.6 23.8 %all-to-all-start = ((bf16[16,8,4096]{2,1,0:T(8,128)(2,1)}), bf16[16,8,4096]{2,1,0:T(8,128)(2,1)S(1)}, u32[]{:S(2)}, u32[]{:S(2)}) async-start(bf16[16,8,4096]{2,1,0:T(8,128)(2,1)} %broadcast_in_dim.30), calls=%async_computation | async-start | bytes 2097152 | tf_op jit(solution)/shard_map/all_to_all | solution.py:58
  23.1 2.0 %copy-start.1 = (s32[32,8]{0,1:T(8,128)S(1)}, s32[32,8]{0,1:T(8,128)}, u32[]{:S(2)}) copy-start(s32[32,8]{0,1:T(8,128)} %param.7) | copy-start | bytes 3076
  23.1 3.8 %copy-start.3 = (f32[32]{0:T(128)S(1)}, f32[32]{0:T(128)}, u32[]{:S(2)}) copy-start(f32[32]{0:T(128)} %param.6) | copy-start | bytes 388
  27.9 3.0 %copy-start.4 = (f32[32]{0:T(128)}, f32[32]{0:T(128)S(1)}, u32[]{:S(2)}) copy-start(f32[32]{0:T(128)S(1)} %log_add_fusion) | copy-start | bytes 388
  31.0 5.2 %collective-permute-start = (f32[2,2,2,2,16,8,128]{6,5,4,3,2,1,0:T(8,128)S(1)}, f32[2,2,2,2,16,8,128]{6,5,4,3,2,1,0:T(8,128)}, u32[]{:S(2)}, u32[]{:S(2)}) collective-permute-start(f32[2,2,2,2,16,8,128]{6,5,4,3,2,1,0:T(8,128)S(1)} %dynamic-slice_bitcast_fusion), channel_id=1, source_target_pairs={{0,32},{32,0},{1,33},{33,1},{2,34},{34,2},{3,35},{35,3},{4,36},{36... | collective-permute-start | bytes 3145736 | tf_op jit(solution)/shard_map/ppermute | solution.py:37
  84.6 5.5 %collective-permute-start.1 = (f32[8]{0:T(128)S(1)}, f32[8]{0:T(128)S(1)}, u32[]{:S(2)}, u32[]{:S(2)}) collective-permute-start(f32[8]{0:T(128)S(1)} %multiply_reduce_fusion.1), channel_id=1, source_target_pairs={{0,16},{16,0},{1,17},{17,1},{2,18},{18,2},{3,19},{19,3},{4,20},{20... | collective-permute-start | bytes 104 | tf_op jit(solution)/shard_map/ppermute | solution.py:85

commit v5 on v4

--- a/solution.py
+++ b/solution.py
@@ -8,7 +8,7 @@
 REF = ("yh", "x", "c")
 DOM = ("yl", "z")
 ALL = REF + DOM
-PLANE = ("yh", "x", "yl")
+PLANE = ("yh", "x", "c", "yl")
 
 
 def shift_matrices(moves):
@@ -46,8 +46,7 @@
 
 def reduce_blocks(partial):
     t = partial.reshape(2, 2, 2, 2, 8, 2, 16, 128)
-    t = t.transpose(3, 0, 1, 2, 5, 6, 4, 7)
-    t = halve(t, "c", 2, 1, 0)
+    t = t.transpose(0, 1, 2, 3, 5, 6, 4, 7)
     t = t.reshape(-1, *t.shape[-3:])
     t = jnp.sum(lax.all_to_all(t, PLANE, 0, 0, tiled=True), axis=0)
     return jnp.sum(lax.all_to_all(t, "z", 0, 0, tiled=True), axis=0)

time: 108 us -> 113 us (1.046)
  blocking collectives: 62 us -> 74.6 us
  starting transfers between devices: 14.3 us -> 11.2 us
  waiting for transfers between devices: 6.86 us -> 4.75 us
  other arithmetic: 3.06 us -> 1.78 us
    all_to_all x1, blocking collectives: 21 us -> 33.2 us  [reduce_blocks(): t = jnp.sum(lax.all_to_all(t, PLANE, 0, 0, tiled=True), axis=0)]
    ppermute x1 -> x0, starting transfers between devices: 2.79 us -> none  [halve(): return keep + lax.ppermute(send, axis, partner(axis, size, bit))]
    ppermute x1 -> x0, waiting for transfers between devices: 2.39 us -> none  [halve(): return keep + lax.ppermute(send, axis, partner(axis, size, bit))]
    add x1 -> x0, other arithmetic: 1.34 us -> none  [halve(): return keep + lax.ppermute(send, axis, partner(axis, size, bit))]
  transfers between devices with their start and end apart: 3 -> 2, of which waited for: 3 -> 2; matrix products, arithmetic and copies ran while one was open for 12% -> 12% of each run, Pallas kernels for 0% -> 0%
where the time goes in v5:
time: 113 us; the launch traced here: 112 us
  blocking collectives  74.6 us (66%)
  starting transfers between devices  11.2 us (10%)
  local copies, waits for them, and re-layouts  11 us (10%)
  matrix products  7.88 us (7%)
  waiting for transfers between devices  4.75 us (4%)
  other arithmetic  1.78 us (2%)
    all_to_all x1, blocking collectives, reduce_blocks(): t = jnp.sum(lax.all_to_all(t, PLANE, 0, 0, tiled=True), axis=0)  33.2 us
    all_to_all x1, blocking collectives, reduce_blocks(): return jnp.sum(lax.all_to_all(t, 'z', 0, 0, tiled=True), axis=0)  26.2 us
    all_to_all x1, blocking collectives, per_device(): lax.all_to_all(row_power, 'z', 0, 0, tiled=True)  15.2 us
    all_to_all x1, starting transfers between devices, gather_rows(): lax.all_to_all(copies, REF, 0, 0, tiled=True).reshape(-1, rows.shape[1])  9.3 us
    reshape x1, local copies, waits for them, and re-layouts, roll_set(): return moved.reshape(offsets.shape[0], images.shape[0], SIDE * SIDE)  6.1 us
    dot_general x1, matrix products, roll_set(): jnp.einsum('snaj,sbj->snab', moved, cols, preferred_element_type=jnp.floa...  4.35 us
    ppermute x1, waiting for transfers between devices, per_device(): row_power = row_power + lax.ppermute(row_power, 'yl', partner('yl', 2, 1))  3.51 us
    dot_general x1, matrix products, per_device(): jnp.einsum('psk,spq->kq', weight, stacked, preferred_element_type=jnp.flo...  2.64 us
  transfers between devices with their start and end apart: 2, of which 2 were waited for; matrix products, arithmetic and copies ran while one was open for 12% of the time, Pallas kernels for 0%

profile of v5, /device:TPU:6, one launch (start us, length us, event | category | flops | bytes accessed | tf_op | source)
XLA Modules:
  0.0 112.0 jit_solution(2393194457656966299)
XLA Ops:
  0.6 0.0 copy-start
  0.6 0.0 copy-start.2
  0.6 2.0 %broadcast_in_dim.30 = bf16[16,8,4096]{2,1,0:T(8,128)(2,1)} broadcast(bf16[8,4096]{1,0:T(8,128)(2,1)} %param.9), dimensions={1,2} | broadcast | bytes 1114112 | tf_op jit(solution)/shard_map/broadcast_in_dim | solution.py:56
  2.6 9.3 %all-to-all-start = ((bf16[16,8,4096]{2,1,0:T(8,128)(2,1)}), bf16[16,8,4096]{2,1,0:T(8,128)(2,1)S(1)}, u32[]{:S(2)}, u32[]{:S(2)}) async-start(bf16[16,8,4096]{2,1,0:T(8,128)(2,1)} %broadcast_in_dim.30), calls=%async_computation | async-start | bytes 2097152 | tf_op jit(solution)/shard_map/all_to_all | solution.py:57
  11.9 0.0 copy-done
  12.0 0.5 reshape.155
  12.5 0.0 copy-done.2
  12.5 0.1 add_select_fusion
  12.6 4.4 %fusion.5 = bf16[9,32,64,64]{3,2,1,0:T(8,128)(2,1)} fusion(bf16[32,64,64,1]{2,1,0,3:T(8,128)(2,1)S(1)} %reshape.155, s32[9,64]{1,0:T(8,128)S(1)} %get-tuple-element.6, s32[9,64]{1,0:T(8,128)S(1)} %get-tuple-element.7), kind=kOutput, calls=%fused_computation.4 | convolution fusion | flops 304422912 | bytes 2626048 | tf_op jit(solution)/shard_map/snaj,sbj->snab/dot_general | solution.py:25
  17.0 6.1 %reshape.151 = bf16[9,32,4096]{2,1,0:T(8,128)(2,1)S(1)} reshape(bf16[9,32,64,64]{3,2,1,0:T(8,128)(2,1)} %fusion.5) | data formatting | bytes 4718592 | tf_op jit(solution)/shard_map/reshape | solution.py:26
  23.1 0.0 copy-done.1
  23.1 0.1 copy.17
  23.2 1.9 %copy.32 = bf16[36,8,32,128]{3,2,1,0:T(8,128)(2,1)} copy(bf16[36,8,32,128]{3,1,2,0:T(8,128)(2,1)S(1)} %bitcast.60) | data formatting | bytes 4718592
  25.1 0.1 fusion.25
  25.2 1.2 %all-to-all-done = bf16[16,8,4096]{2,1,0:T(8,128)(2,1)S(1)} async-done(((bf16[16,8,4096]{2,1,0:T(8,128)(2,1)}), bf16[16,8,4096]{2,1,0:T(8,128)(2,1)S(1)}, u32[]{:S(2)}, u32[]{:S(2)}) %all-to-all-start) | async-done | bytes 1048608 | tf_op jit(solution)/shard_map/all_to_all | solution.py:57
  26.4 0.3 multiply_reduce_fusion
  26.7 0.1 mul.62
  26.8 0.0 copy-done.3
  26.8 0.9 select_reduce_fusion
  27.7 0.2 exponential_reduce_fusion
  27.9 0.0 copy-start.4
  28.0 0.1 fusion.21
  28.1 0.2 copy.18
  28.3 2.6 %fusion.8 = f32[2,2,2,2,8,2,16,128,1]{7,4,8,6,5,3,2,1,0:T(8,128)S(1)} fusion(bf16[2,16,128,32,9,1,1,1,1]{2,1,0,3,4,8,7,6,5:T(8,128)(2,1)} %bitcast.61, bf16[2,2,2,2,8,32,9,1,1]{5,4,3,2,1,0,6,8,7:T(8,128)(2,1)S(1)} %bitcast.63), kind=kOutput, calls=%fused_computation.5 | convolution fusion | flops 301989888 | bytes 4530176 | tf_op jit(solution)/shard_map/psk,spq->kq/dot_general | solution.py:81
  30.9 33.2 %all_to_all.21 = f32[32,16,8,128]{3,2,1,0:T(8,128)S(1)} all-to-all(f32[32,16,8,128]{3,2,1,0:T(8,128)S(1)} %bitcast.62), channel_id=1, replica_groups=mesh['yh'=2,'x'=4,'c'=2,'yl'=2,'z'=16] {'yh','x','c','yl'}, dimensions={0} | all-to-all | bytes 4194304 | tf_op jit(solution)/shard_map/all_to_all | solution.py:51
  64.2 0.1 reduce_sum.56
  64.3 26.2 %all_to_all.22 = f32[16,8,128]{2,1,0:T(8,128)S(1)} all-to-all(f32[16,8,128]{2,1,0:T(8,128)S(1)} %reduce_sum.56), channel_id=1, replica_groups=mesh['yh'=2,'x'=4,'c'=2,'yl'=2,'z'=16] {'z'}, dimensions={0} | all-to-all | bytes 131072 | tf_op jit(solution)/shard_map/all_to_all | solution.py:52
  90.5 0.1 multiply_reduce_fusion.1
  90.6 1.9 %collective-permute-start = (f32[8]{0:T(128)S(1)}, f32[8]{0:T(128)S(1)}, u32[]{:S(2)}, u32[]{:S(2)}) collective-permute-start(f32[8]{0:T(128)S(1)} %multiply_reduce_fusion.1), channel_id=1, source_target_pairs={{0,16},{16,0},{1,17},{17,1},{2,18},{18,2},{3,19},{19,3},{4,20},{20... | collective-permute-start | bytes 104 | tf_op jit(solution)/shard_map/ppermute | solution.py:84
  92.5 3.5 %collective-permute-done = f32[8]{0:T(128)S(1)} collective-permute-done((f32[8]{0:T(128)S(1)}, f32[8]{0:T(128)S(1)}, u32[]{:S(2)}, u32[]{:S(2)}) %collective-permute-start) | collective-permute-done | bytes 64 | tf_op jit(solution)/shard_map/ppermute | solution.py:84
  96.0 15.2 %all_to_all.23 = f32[16,1,8]{2,1,0:T(1,128)S(1)} all-to-all(f32[16,1,8]{2,1,0:T(1,128)S(1)} %broadcast_in_dim.58), channel_id=1, replica_groups=mesh['yh'=2,'x'=4,'c'=2,'yl'=2,'z'=16] {'z'}, dimensions={0} | all-to-all | bytes 1024 | tf_op jit(solution)/shard_map/all_to_all | solution.py:86
  111.3 0.7 divide_convert_fusion
  (11 shorter events, 0.1 us)
Async XLA Ops:
  0.6 11.3 %copy-start = (bf16[32,4096]{1,0:T(8,128)(2,1)S(1)}, bf16[32,4096]{1,0:T(8,128)(2,1)}, u32[]{:S(2)}) copy-start(bf16[32,4096]{1,0:T(8,128)(2,1)} %param.5) | copy-start | bytes 786436
  0.6 11.9 %copy-start.2 = (s32[9,2]{0,1:T(2,128)S(1)}, s32[9,2]{0,1:T(2,128)}, u32[]{:S(2)}) copy-start(s32[9,2]{0,1:T(2,128)} %param.8) | copy-start | bytes 220
  2.6 23.8 %all-to-all-start = ((bf16[16,8,4096]{2,1,0:T(8,128)(2,1)}), bf16[16,8,4096]{2,1,0:T(8,128)(2,1)S(1)}, u32[]{:S(2)}, u32[]{:S(2)}) async-start(bf16[16,8,4096]{2,1,0:T(8,128)(2,1)} %broadcast_in_dim.30), calls=%async_computation | async-start | bytes 2097152 | tf_op jit(solution)/shard_map/all_to_all | solution.py:57
  17.0 6.1 %copy-start.1 = (s32[32,8]{0,1:T(8,128)S(1)}, s32[32,8]{0,1:T(8,128)}, u32[]{:S(2)}) copy-start(s32[32,8]{0,1:T(8,128)} %param.7) | copy-start | bytes 3076
  23.2 3.7 %copy-start.3 = (f32[32]{0:T(128)S(1)}, f32[32]{0:T(128)}, u32[]{:S(2)}) copy-start(f32[32]{0:T(128)} %param.6) | copy-start | bytes 388
  27.9 3.0 %copy-start.4 = (f32[32]{0:T(128)}, f32[32]{0:T(128)S(1)}, u32[]{:S(2)}) copy-start(f32[32]{0:T(128)S(1)} %log_add_fusion) | copy-start | bytes 388
  90.6 5.5 %collective-permute-start = (f32[8]{0:T(128)S(1)}, f32[8]{0:T(128)S(1)}, u32[]{:S(2)}, u32[]{:S(2)}) collective-permute-start(f32[8]{0:T(128)S(1)} %multiply_reduce_fusion.1), channel_id=1, source_target_pairs={{0,16},{16,0},{1,17},{17,1},{2,18},{18,2},{3,19},{19,3},{4,20},{20... | collective-permute-start | bytes 104 | tf_op jit(solution)/shard_map/ppermute | solution.py:84

commit v6 on v4

--- a/solution.py
+++ b/solution.py
@@ -54,8 +54,12 @@
 
 
 def gather_rows(rows):
-    copies = jnp.broadcast_to(rows[None], (16, *rows.shape))
-    return lax.all_to_all(copies, REF, 0, 0, tiled=True).reshape(-1, rows.shape[1])
+    copies = jnp.broadcast_to(rows[None], (8, *rows.shape))
+    mine = lax.all_to_all(copies, ("yh", "x"), 0, 0, tiled=True)
+    other = lax.ppermute(mine, "c", partner("c", 2, 1))
+    first = lax.axis_index("c") == 0
+    both = jnp.stack([jnp.where(first, mine, other), jnp.where(first, other, mine)], axis=1)
+    return both.reshape(-1, rows.shape[1])
 
 
 def per_device(particles, inv_noise, candidates, offsets, references):

time: 108 us -> 118 us (1.093)
  waiting for transfers between devices: 6.86 us -> 12.4 us
  starting transfers between devices: 14.3 us -> 16.1 us
    all_to_all x1, waiting for transfers between devices: 1.23 us -> 7.13 us  [gather_rows(): mine = lax.all_to_all(copies, ('yh', 'x'), 0, 0, tiled=True)]
    ppermute x0 -> x1, starting transfers between devices: none -> 1.91 us  [gather_rows(): other = lax.ppermute(mine, 'c', partner('c', 2, 1))]
    all_to_all x1, blocking collectives: 25.9 us -> 27.1 us  [reduce_blocks(): return jnp.sum(lax.all_to_all(t, 'z', 0, 0, tiled=True), axis=0)]
  transfers between devices with their start and end apart: 3 -> 4, of which waited for: 3 -> 3; matrix products, arithmetic and copies ran while one was open for 12% -> 13% of each run, Pallas kernels for 0% -> 0%
where the time goes in v6:
time: 118 us; the launch traced here: 116 us
  blocking collectives  63 us (53%)
  starting transfers between devices  16.1 us (14%)
  waiting for transfers between devices  12.4 us (11%)
  local copies, waits for them, and re-layouts  11.7 us (10%)
  matrix products  7.87 us (7%)
  other arithmetic  3.99 us (3%)
    all_to_all x1, blocking collectives, reduce_blocks(): return jnp.sum(lax.all_to_all(t, 'z', 0, 0, tiled=True), axis=0)  27.1 us
    all_to_all x1, blocking collectives, reduce_blocks(): t = jnp.sum(lax.all_to_all(t, PLANE, 0, 0, tiled=True), axis=0)  20.4 us
    all_to_all x1, blocking collectives, per_device(): lax.all_to_all(row_power, 'z', 0, 0, tiled=True)  15.5 us
    all_to_all x1, starting transfers between devices, gather_rows(): mine = lax.all_to_all(copies, ('yh', 'x'), 0, 0, tiled=True)  9.23 us
    all_to_all x1, waiting for transfers between devices, gather_rows(): mine = lax.all_to_all(copies, ('yh', 'x'), 0, 0, tiled=True)  7.13 us
    reshape x1, local copies, waits for them, and re-layouts, roll_set(): return moved.reshape(offsets.shape[0], images.shape[0], SIDE * SIDE)  6.09 us
    dot_general x1, matrix products, roll_set(): jnp.einsum('snaj,sbj->snab', moved, cols, preferred_element_type=jnp.floa...  4.35 us
    ppermute x1, waiting for transfers between devices, per_device(): row_power = row_power + lax.ppermute(row_power, 'yl', partner('yl', 2, 1))  2.92 us
  transfers between devices with their start and end apart: 4, of which 3 were waited for; matrix products, arithmetic and copies ran while one was open for 13% of the time, Pallas kernels for 0%

profile of v6, /device:TPU:6, one launch (start us, length us, event | category | flops | bytes accessed | tf_op | source)
XLA Modules:
  0.0 115.9 jit_solution(3545579752732195037)
XLA Ops:
  0.6 1.7 %broadcast_in_dim.56 = bf16[8,8,4096]{2,1,0:T(8,128)(2,1)} broadcast(bf16[8,4096]{1,0:T(8,128)(2,1)} %param.9), dimensions={1,2} | broadcast | bytes 589824 | tf_op jit(solution)/shard_map/broadcast_in_dim | solution.py:57
  2.3 9.2 %all-to-all-start = ((bf16[8,8,4096]{2,1,0:T(8,128)(2,1)}), bf16[8,8,4096]{2,1,0:T(8,128)(2,1)S(1)}, u32[]{:S(2)}, u32[]{:S(2)}) async-start(bf16[8,8,4096]{2,1,0:T(8,128)(2,1)} %broadcast_in_dim.56), calls=%async_computation | async-start | bytes 1048576 | tf_op jit(solution)/shard_map/all_to_all | solution.py:58
  11.5 0.8 multiply_bitcast_fusion.1
  12.3 7.1 %all-to-all-done = bf16[8,8,4096]{2,1,0:T(8,128)(2,1)S(1)} async-done(((bf16[8,8,4096]{2,1,0:T(8,128)(2,1)}), bf16[8,8,4096]{2,1,0:T(8,128)(2,1)S(1)}, u32[]{:S(2)}, u32[]{:S(2)}) %all-to-all-start) | async-done | bytes 524320 | tf_op jit(solution)/shard_map/all_to_all | solution.py:58
  19.4 1.9 %collective-permute-start = (bf16[8,8,4096]{2,1,0:T(8,128)(2,1)S(1)}, bf16[8,8,4096]{2,1,0:T(8,128)(2,1)S(1)}, u32[]{:S(2)}, u32[]{:S(2)}) collective-permute-start(bf16[8,8,4096]{2,1,0:T(8,128)(2,1)S(1)} %all-to-all-done), channel_id=1, source_target_pairs={{0,32},{32,0},{1,33},{33,1},{2,34},{34,2},{3,35},{35,3},{4,36},{36... | collective-permute-start | bytes 1572872 | tf_op jit(solution)/shard_map/ppermute | solution.py:59
  21.3 0.1 add_select_fusion
  21.4 1.5 %reshape.155 = bf16[32,64,64,1]{2,1,0,3:T(8,128)(2,1)S(1)} reshape(bf16[32,4096]{1,0:T(8,128)(2,1)} %param.5) | data formatting | bytes 524288 | tf_op jit(solution)/shard_map/reshape | solution.py:21
  22.9 4.3 %fusion.5 = bf16[9,32,64,64]{3,2,1,0:T(8,128)(2,1)} fusion(bf16[32,64,64,1]{2,1,0,3:T(8,128)(2,1)S(1)} %reshape.155, s32[9,64]{1,0:T(8,128)S(1)} %get-tuple-element.8, s32[9,64]{1,0:T(8,128)S(1)} %get-tuple-element.9), kind=kOutput, calls=%fused_computation.4 | convolution fusion | flops 304422912 | bytes 2626048 | tf_op jit(solution)/shard_map/snaj,sbj->snab/dot_general | solution.py:25
  27.2 6.1 %reshape.152 = bf16[9,32,4096]{2,1,0:T(8,128)(2,1)S(1)} reshape(bf16[9,32,64,64]{3,2,1,0:T(8,128)(2,1)} %fusion.5) | data formatting | bytes 4718592 | tf_op jit(solution)/shard_map/reshape | solution.py:26
  33.3 1.9 %copy.41 = bf16[36,8,32,128]{3,2,1,0:T(8,128)(2,1)} copy(bf16[36,8,32,128]{3,1,2,0:T(8,128)(2,1)S(1)} %bitcast.69) | data formatting | bytes 4718592
  35.3 0.1 copy.23
  35.4 0.1 fusion.24
  35.5 0.1 select_bitcast_fusion.1
  35.6 0.3 multiply_reduce_fusion
  35.9 0.1 pad_maximum_fusion
  36.0 0.1 mul.62
  36.1 0.9 fusion.23
  37.0 0.2 exponential_reduce_fusion
  37.2 0.1 fusion.25
  37.3 0.2 copy.25
  37.6 2.6 %fusion.10 = f32[2,2,2,2,8,2,16,128]{7,4,6,5,3,2,1,0:T(8,128)S(1)} fusion(bf16[2,16,128,32,9,1,1,1,1]{2,1,0,3,4,8,7,6,5:T(8,128)(2,1)} %bitcast.71, bf16[2,2,2,2,8,32,9,1,1]{5,4,3,2,1,0,6,8,7:T(8,128)(2,1)S(1)} %bitcast.73), kind=kOutput, calls=%fused_computation.8 | convolution fusion | flops 301989888 | bytes 4530176 | tf_op jit(solution)/shard_map/psk,spq->kq/dot_general | solution.py:86
  40.2 0.1 dynamic-slice_bitcast_fusion
  40.3 2.4 %collective-permute-start.1 = (f32[2,2,2,2,16,8,128]{6,5,4,3,2,1,0:T(8,128)S(1)}, f32[2,2,2,2,16,8,128]{6,5,4,3,2,1,0:T(8,128)}, u32[]{:S(2)}, u32[]{:S(2)}) collective-permute-start(f32[2,2,2,2,16,8,128]{6,5,4,3,2,1,0:T(8,128)S(1)} %dynamic-slice_bitcast_fusion), channel_id=1, source_target_pairs={{0,32},{32,0},{1,33},{33,1},{2,34},{34,2},{3,35},{35,3},{4,36},{36... | collective-permute-start | bytes 3145736 | tf_op jit(solution)/shard_map/ppermute | solution.py:37
  42.8 2.4 %collective-permute-done.1 = f32[2,2,2,2,16,8,128]{6,5,4,3,2,1,0:T(8,128)} collective-permute-done((f32[2,2,2,2,16,8,128]{6,5,4,3,2,1,0:T(8,128)S(1)}, f32[2,2,2,2,16,8,128]{6,5,4,3,2,1,0:T(8,128)}, u32[]{:S(2)}, u32[]{:S(2)}) %collective-permute-start.1) | collective-permute-done | bytes 1048608 | tf_op jit(solution)/shard_map/ppermute | solution.py:37
  45.2 1.3 %bitcast_add_fusion = f32[2,2,2,2,16,8,128]{6,5,4,3,2,1,0:T(8,128)S(1)} fusion(f32[2,2,2,2,16,8,128]{6,5,4,3,2,1,0:T(8,128)} %collective-permute-done.1, f32[2,2,2,2,8,2,16,128]{7,4,6,5,3,2,1,0:T(8,128)S(1)} %fusion.10, s32[]{:T(128)S(6)} %select_n.69), kind=kLoop, calls=%fused_computation.12 | loop fusion | flops 262144 | bytes 3145732 | tf_op jit(solution)/shard_map/add | solution.py:37
  46.5 20.4 %all_to_all.21 = f32[16,16,8,128]{3,2,1,0:T(8,128)S(1)} all-to-all(f32[16,16,8,128]{3,2,1,0:T(8,128)S(1)} %bitcast.70), channel_id=1, replica_groups=mesh['yh'=2,'x'=4,'c'=2,'yl'=2,'z'=16] {'yh','x','yl'}, dimensions={0} | all-to-all | bytes 2097152 | tf_op jit(solution)/shard_map/all_to_all | solution.py:52
  67.0 27.1 %all_to_all.22 = f32[16,8,128]{2,1,0:T(8,128)S(1)} all-to-all(f32[16,8,128]{2,1,0:T(8,128)S(1)} %reduce_sum.56), channel_id=1, replica_groups=mesh['yh'=2,'x'=4,'c'=2,'yl'=2,'z'=16] {'z'}, dimensions={0} | all-to-all | bytes 131072 | tf_op jit(solution)/shard_map/all_to_all | solution.py:53
  94.1 0.1 multiply_reduce_fusion.1
  94.2 2.5 %collective-permute-start.2 = (f32[8]{0:T(128)S(1)}, f32[8]{0:T(128)S(1)}, u32[]{:S(2)}, u32[]{:S(2)}) collective-permute-start(f32[8]{0:T(128)S(1)} %multiply_reduce_fusion.1), channel_id=1, source_target_pairs={{0,16},{16,0},{1,17},{17,1},{2,18},{18,2},{3,19},{19,3},{4,20},{20... | collective-permute-start | bytes 104 | tf_op jit(solution)/shard_map/ppermute | solution.py:89
  96.7 2.9 %collective-permute-done.2 = f32[8]{0:T(128)S(1)} collective-permute-done((f32[8]{0:T(128)S(1)}, f32[8]{0:T(128)S(1)}, u32[]{:S(2)}, u32[]{:S(2)}) %collective-permute-start.2) | collective-permute-done | bytes 64 | tf_op jit(solution)/shard_map/ppermute | solution.py:89
  99.7 15.5 %all_to_all.23 = f32[16,1,8]{2,1,0:T(1,128)S(1)} all-to-all(f32[16,1,8]{2,1,0:T(1,128)S(1)} %broadcast_in_dim.61), channel_id=1, replica_groups=mesh['yh'=2,'x'=4,'c'=2,'yl'=2,'z'=16] {'z'}, dimensions={0} | all-to-all | bytes 1024 | tf_op jit(solution)/shard_map/all_to_all | solution.py:91
  115.2 0.7 divide_convert_fusion
  (15 shorter events, 0.2 us)
Async XLA Ops:
  2.3 17.1 %all-to-all-start = ((bf16[8,8,4096]{2,1,0:T(8,128)(2,1)}), bf16[8,8,4096]{2,1,0:T(8,128)(2,1)S(1)}, u32[]{:S(2)}, u32[]{:S(2)}) async-start(bf16[8,8,4096]{2,1,0:T(8,128)(2,1)} %broadcast_in_dim.56), calls=%async_computation | async-start | bytes 1048576 | tf_op jit(solution)/shard_map/all_to_all | solution.py:58
  19.4 16.1 %collective-permute-start = (bf16[8,8,4096]{2,1,0:T(8,128)(2,1)S(1)}, bf16[8,8,4096]{2,1,0:T(8,128)(2,1)S(1)}, u32[]{:S(2)}, u32[]{:S(2)}) collective-permute-start(bf16[8,8,4096]{2,1,0:T(8,128)(2,1)S(1)} %all-to-all-done), channel_id=1, source_target_pairs={{0,32},{32,0},{1,33},{33,1},{2,34},{34,2},{3,35},{35,3},{4,36},{36... | collective-permute-start | bytes 1572872 | tf_op jit(solution)/shard_map/ppermute | solution.py:59
  33.3 1.9 %copy-start = (s32[32,8]{0,1:T(8,128)S(1)}, s32[32,8]{0,1:T(8,128)}, u32[]{:S(2)}) copy-start(s32[32,8]{0,1:T(8,128)} %param.7) | copy-start | bytes 3076
  35.5 0.7 copy-start.2
  37.2 3.0 %copy-start.1 = (f32[32]{0:T(128)}, f32[32]{0:T(128)S(1)}, u32[]{:S(2)}) copy-start(f32[32]{0:T(128)S(1)} %log_add_fusion) | copy-start | bytes 388
  40.3 4.8 %collective-permute-start.1 = (f32[2,2,2,2,16,8,128]{6,5,4,3,2,1,0:T(8,128)S(1)}, f32[2,2,2,2,16,8,128]{6,5,4,3,2,1,0:T(8,128)}, u32[]{:S(2)}, u32[]{:S(2)}) collective-permute-start(f32[2,2,2,2,16,8,128]{6,5,4,3,2,1,0:T(8,128)S(1)} %dynamic-slice_bitcast_fusion), channel_id=1, source_target_pairs={{0,32},{32,0},{1,33},{33,1},{2,34},{34,2},{3,35},{35,3},{4,36},{36... | collective-permute-start | bytes 3145736 | tf_op jit(solution)/shard_map/ppermute | solution.py:37
  94.2 5.5 %collective-permute-start.2 = (f32[8]{0:T(128)S(1)}, f32[8]{0:T(128)S(1)}, u32[]{:S(2)}, u32[]{:S(2)}) collective-permute-start(f32[8]{0:T(128)S(1)} %multiply_reduce_fusion.1), channel_id=1, source_target_pairs={{0,16},{16,0},{1,17},{17,1},{2,18},{18,2},{3,19},{19,3},{4,20},{20... | collective-permute-start | bytes 104 | tf_op jit(solution)/shard_map/ppermute | solution.py:89

commit v7 on v6

--- a/solution.py
+++ b/solution.py
@@ -26,7 +26,7 @@
     return moved.reshape(offsets.shape[0], images.shape[0], SIDE * SIDE)
 
 
-def partner(axis, size, bit):
+def partner(size, bit):
     return [(i, i ^ bit) for i in range(size)]
 
 
@@ -34,14 +34,7 @@
     mine = (lax.axis_index(axis) // bit) % 2
     keep = lax.dynamic_index_in_dim(t, mine, dim, keepdims=False)
     send = lax.dynamic_index_in_dim(t, 1 - mine, dim, keepdims=False)
-    return keep + lax.ppermute(send, axis, partner(axis, size, bit))
-
-
-def halve_pair(t, first, second):
-    mid = t.shape[2] // 2
-    a = halve(halve(lax.slice_in_dim(t, 0, mid, axis=2), *first, 0), *second, 0)
-    b = halve(halve(lax.slice_in_dim(t, mid, t.shape[2], axis=2), *second, 1), *first, 0)
-    return jnp.concatenate([a, b], axis=0)
+    return keep + lax.ppermute(send, axis, partner(size, bit))
 
 
 def reduce_blocks(partial):
@@ -56,13 +49,13 @@
 def gather_rows(rows):
     copies = jnp.broadcast_to(rows[None], (8, *rows.shape))
     mine = lax.all_to_all(copies, ("yh", "x"), 0, 0, tiled=True)
-    other = lax.ppermute(mine, "c", partner("c", 2, 1))
+    other = lax.ppermute(mine, "c", partner(2, 1))
     first = lax.axis_index("c") == 0
     both = jnp.stack([jnp.where(first, mine, other), jnp.where(first, other, mine)], axis=1)
     return both.reshape(-1, rows.shape[1])
 
 
-def per_device(particles, inv_noise, candidates, offsets, references):
+def step(particles, inv_noise, candidates, offsets, references):
     tile_size = references.shape[0]
     all_classes = tile_size * 16
     stacked = roll_set(particles, offsets, -1)
@@ -86,7 +79,7 @@
     partial = jnp.einsum("psk,spq->kq", weight, stacked, preferred_element_type=jnp.float32)
     shares = reduce_blocks(partial)
     row_power = jnp.sum(shares * shares, axis=1)
-    row_power = row_power + lax.ppermute(row_power, "yl", partner("yl", 2, 1))
+    row_power = row_power + lax.ppermute(row_power, "yl", partner(2, 1))
     row_power = jnp.broadcast_to(row_power[None], (16, row_power.shape[0]))
     row_power = jnp.sum(lax.all_to_all(row_power, "z", 0, 0, tiled=True), axis=0)
     refreshed = (shares / jnp.sqrt(row_power[:, None] / (SIDE * SIDE) + 1e-06)).astype(jnp.bfloat16)
@@ -104,6 +97,4 @@
         P(REF, None),
     )
     out_specs = (P(REF, DOM), P(ALL))
-    return jax.shard_map(
-        per_device, mesh=fine, in_specs=in_specs, out_specs=out_specs, check_vma=False
-    )
+    return jax.shard_map(step, mesh=fine, in_specs=in_specs, out_specs=out_specs, check_vma=False)

time: 118 us -> 118 us (level)
  no operation moved by 1% of the time
where the time goes in v7:
time: 118 us; the launch traced here: 116 us
  blocking collectives  63 us (53%)
  starting transfers between devices  16.1 us (14%)
  waiting for transfers between devices  12.4 us (11%)
  local copies, waits for them, and re-layouts  11.7 us (10%)
  matrix products  7.87 us (7%)
  other arithmetic  3.99 us (3%)
    all_to_all x1, blocking collectives, reduce_blocks(): return jnp.sum(lax.all_to_all(t, 'z', 0, 0, tiled=True), axis=0)  27.1 us
    all_to_all x1, blocking collectives, reduce_blocks(): t = jnp.sum(lax.all_to_all(t, PLANE, 0, 0, tiled=True), axis=0)  20.4 us
    all_to_all x1, blocking collectives, step(): lax.all_to_all(row_power, 'z', 0, 0, tiled=True)  15.5 us
    all_to_all x1, starting transfers between devices, gather_rows(): mine = lax.all_to_all(copies, ('yh', 'x'), 0, 0, tiled=True)  9.23 us
    all_to_all x1, waiting for transfers between devices, gather_rows(): mine = lax.all_to_all(copies, ('yh', 'x'), 0, 0, tiled=True)  7.13 us
    reshape x1, local copies, waits for them, and re-layouts, roll_set(): return moved.reshape(offsets.shape[0], images.shape[0], SIDE * SIDE)  6.09 us
    dot_general x1, matrix products, roll_set(): jnp.einsum('snaj,sbj->snab', moved, cols, preferred_element_type=jnp.floa...  4.35 us
    ppermute x1, waiting for transfers between devices, step(): row_power = row_power + lax.ppermute(row_power, 'yl', partner(2, 1))  2.92 us
  transfers between devices with their start and end apart: 4, of which 3 were waited for; matrix products, arithmetic and copies ran while one was open for 13% of the time, Pallas kernels for 0%

profile of v7, /device:TPU:6, one launch (start us, length us, event | category | flops | bytes accessed | tf_op | source)
XLA Modules:
  0.0 115.9 jit_solution(3545579752732195037)
XLA Ops:
  0.6 1.7 %broadcast_in_dim.56 = bf16[8,8,4096]{2,1,0:T(8,128)(2,1)} broadcast(bf16[8,4096]{1,0:T(8,128)(2,1)} %param.9), dimensions={1,2} | broadcast | bytes 589824 | tf_op jit(solution)/shard_map/broadcast_in_dim | solution.py:50
  2.3 9.2 %all-to-all-start = ((bf16[8,8,4096]{2,1,0:T(8,128)(2,1)}), bf16[8,8,4096]{2,1,0:T(8,128)(2,1)S(1)}, u32[]{:S(2)}, u32[]{:S(2)}) async-start(bf16[8,8,4096]{2,1,0:T(8,128)(2,1)} %broadcast_in_dim.56), calls=%async_computation | async-start | bytes 1048576 | tf_op jit(solution)/shard_map/all_to_all | solution.py:51
  11.5 0.8 multiply_bitcast_fusion.1
  12.3 7.1 %all-to-all-done = bf16[8,8,4096]{2,1,0:T(8,128)(2,1)S(1)} async-done(((bf16[8,8,4096]{2,1,0:T(8,128)(2,1)}), bf16[8,8,4096]{2,1,0:T(8,128)(2,1)S(1)}, u32[]{:S(2)}, u32[]{:S(2)}) %all-to-all-start) | async-done | bytes 524320 | tf_op jit(solution)/shard_map/all_to_all | solution.py:51
  19.4 1.9 %collective-permute-start = (bf16[8,8,4096]{2,1,0:T(8,128)(2,1)S(1)}, bf16[8,8,4096]{2,1,0:T(8,128)(2,1)S(1)}, u32[]{:S(2)}, u32[]{:S(2)}) collective-permute-start(bf16[8,8,4096]{2,1,0:T(8,128)(2,1)S(1)} %all-to-all-done), channel_id=1, source_target_pairs={{0,32},{32,0},{1,33},{33,1},{2,34},{34,2},{3,35},{35,3},{4,36},{36... | collective-permute-start | bytes 1572872 | tf_op jit(solution)/shard_map/ppermute | solution.py:52
  21.3 0.1 add_select_fusion
  21.4 1.5 %reshape.155 = bf16[32,64,64,1]{2,1,0,3:T(8,128)(2,1)S(1)} reshape(bf16[32,4096]{1,0:T(8,128)(2,1)} %param.5) | data formatting | bytes 524288 | tf_op jit(solution)/shard_map/reshape | solution.py:21
  22.9 4.3 %fusion.5 = bf16[9,32,64,64]{3,2,1,0:T(8,128)(2,1)} fusion(bf16[32,64,64,1]{2,1,0,3:T(8,128)(2,1)S(1)} %reshape.155, s32[9,64]{1,0:T(8,128)S(1)} %get-tuple-element.8, s32[9,64]{1,0:T(8,128)S(1)} %get-tuple-element.9), kind=kOutput, calls=%fused_computation.4 | convolution fusion | flops 304422912 | bytes 2626048 | tf_op jit(solution)/shard_map/snaj,sbj->snab/dot_general | solution.py:25
  27.2 6.1 %reshape.152 = bf16[9,32,4096]{2,1,0:T(8,128)(2,1)S(1)} reshape(bf16[9,32,64,64]{3,2,1,0:T(8,128)(2,1)} %fusion.5) | data formatting | bytes 4718592 | tf_op jit(solution)/shard_map/reshape | solution.py:26
  33.3 1.9 %copy.41 = bf16[36,8,32,128]{3,2,1,0:T(8,128)(2,1)} copy(bf16[36,8,32,128]{3,1,2,0:T(8,128)(2,1)S(1)} %bitcast.69) | data formatting | bytes 4718592
  35.3 0.1 copy.23
  35.4 0.1 fusion.24
  35.5 0.1 select_bitcast_fusion.1
  35.6 0.3 multiply_reduce_fusion
  35.9 0.1 pad_maximum_fusion
  36.0 0.1 mul.62
  36.1 0.9 fusion.23
  37.0 0.2 exponential_reduce_fusion
  37.2 0.1 fusion.25
  37.3 0.2 copy.25
  37.6 2.6 %fusion.10 = f32[2,2,2,2,8,2,16,128]{7,4,6,5,3,2,1,0:T(8,128)S(1)} fusion(bf16[2,16,128,32,9,1,1,1,1]{2,1,0,3,4,8,7,6,5:T(8,128)(2,1)} %bitcast.71, bf16[2,2,2,2,8,32,9,1,1]{5,4,3,2,1,0,6,8,7:T(8,128)(2,1)S(1)} %bitcast.73), kind=kOutput, calls=%fused_computation.8 | convolution fusion | flops 301989888 | bytes 4530176 | tf_op jit(solution)/shard_map/psk,spq->kq/dot_general | solution.py:79
  40.2 0.1 dynamic-slice_bitcast_fusion
  40.3 2.4 %collective-permute-start.1 = (f32[2,2,2,2,16,8,128]{6,5,4,3,2,1,0:T(8,128)S(1)}, f32[2,2,2,2,16,8,128]{6,5,4,3,2,1,0:T(8,128)}, u32[]{:S(2)}, u32[]{:S(2)}) collective-permute-start(f32[2,2,2,2,16,8,128]{6,5,4,3,2,1,0:T(8,128)S(1)} %dynamic-slice_bitcast_fusion), channel_id=1, source_target_pairs={{0,32},{32,0},{1,33},{33,1},{2,34},{34,2},{3,35},{35,3},{4,36},{36... | collective-permute-start | bytes 3145736 | tf_op jit(solution)/shard_map/ppermute | solution.py:37
  42.8 2.4 %collective-permute-done.1 = f32[2,2,2,2,16,8,128]{6,5,4,3,2,1,0:T(8,128)} collective-permute-done((f32[2,2,2,2,16,8,128]{6,5,4,3,2,1,0:T(8,128)S(1)}, f32[2,2,2,2,16,8,128]{6,5,4,3,2,1,0:T(8,128)}, u32[]{:S(2)}, u32[]{:S(2)}) %collective-permute-start.1) | collective-permute-done | bytes 1048608 | tf_op jit(solution)/shard_map/ppermute | solution.py:37
  45.2 1.3 %bitcast_add_fusion = f32[2,2,2,2,16,8,128]{6,5,4,3,2,1,0:T(8,128)S(1)} fusion(f32[2,2,2,2,16,8,128]{6,5,4,3,2,1,0:T(8,128)} %collective-permute-done.1, f32[2,2,2,2,8,2,16,128]{7,4,6,5,3,2,1,0:T(8,128)S(1)} %fusion.10, s32[]{:T(128)S(6)} %select_n.69), kind=kLoop, calls=%fused_computation.12 | loop fusion | flops 262144 | bytes 3145732 | tf_op jit(solution)/shard_map/add | solution.py:37
  46.5 20.4 %all_to_all.21 = f32[16,16,8,128]{3,2,1,0:T(8,128)S(1)} all-to-all(f32[16,16,8,128]{3,2,1,0:T(8,128)S(1)} %bitcast.70), channel_id=1, replica_groups=mesh['yh'=2,'x'=4,'c'=2,'yl'=2,'z'=16] {'yh','x','yl'}, dimensions={0} | all-to-all | bytes 2097152 | tf_op jit(solution)/shard_map/all_to_all | solution.py:45
  67.0 27.1 %all_to_all.22 = f32[16,8,128]{2,1,0:T(8,128)S(1)} all-to-all(f32[16,8,128]{2,1,0:T(8,128)S(1)} %reduce_sum.56), channel_id=1, replica_groups=mesh['yh'=2,'x'=4,'c'=2,'yl'=2,'z'=16] {'z'}, dimensions={0} | all-to-all | bytes 131072 | tf_op jit(solution)/shard_map/all_to_all | solution.py:46
  94.1 0.1 multiply_reduce_fusion.1
  94.2 2.5 %collective-permute-start.2 = (f32[8]{0:T(128)S(1)}, f32[8]{0:T(128)S(1)}, u32[]{:S(2)}, u32[]{:S(2)}) collective-permute-start(f32[8]{0:T(128)S(1)} %multiply_reduce_fusion.1), channel_id=1, source_target_pairs={{0,16},{16,0},{1,17},{17,1},{2,18},{18,2},{3,19},{19,3},{4,20},{20... | collective-permute-start | bytes 104 | tf_op jit(solution)/shard_map/ppermute | solution.py:82
  96.7 2.9 %collective-permute-done.2 = f32[8]{0:T(128)S(1)} collective-permute-done((f32[8]{0:T(128)S(1)}, f32[8]{0:T(128)S(1)}, u32[]{:S(2)}, u32[]{:S(2)}) %collective-permute-start.2) | collective-permute-done | bytes 64 | tf_op jit(solution)/shard_map/ppermute | solution.py:82
  99.7 15.5 %all_to_all.23 = f32[16,1,8]{2,1,0:T(1,128)S(1)} all-to-all(f32[16,1,8]{2,1,0:T(1,128)S(1)} %broadcast_in_dim.61), channel_id=1, replica_groups=mesh['yh'=2,'x'=4,'c'=2,'yl'=2,'z'=16] {'z'}, dimensions={0} | all-to-all | bytes 1024 | tf_op jit(solution)/shard_map/all_to_all | solution.py:84
  115.2 0.7 divide_convert_fusion
  (15 shorter events, 0.2 us)
Async XLA Ops:
  2.3 17.1 %all-to-all-start = ((bf16[8,8,4096]{2,1,0:T(8,128)(2,1)}), bf16[8,8,4096]{2,1,0:T(8,128)(2,1)S(1)}, u32[]{:S(2)}, u32[]{:S(2)}) async-start(bf16[8,8,4096]{2,1,0:T(8,128)(2,1)} %broadcast_in_dim.56), calls=%async_computation | async-start | bytes 1048576 | tf_op jit(solution)/shard_map/all_to_all | solution.py:51
  19.4 16.1 %collective-permute-start = (bf16[8,8,4096]{2,1,0:T(8,128)(2,1)S(1)}, bf16[8,8,4096]{2,1,0:T(8,128)(2,1)S(1)}, u32[]{:S(2)}, u32[]{:S(2)}) collective-permute-start(bf16[8,8,4096]{2,1,0:T(8,128)(2,1)S(1)} %all-to-all-done), channel_id=1, source_target_pairs={{0,32},{32,0},{1,33},{33,1},{2,34},{34,2},{3,35},{35,3},{4,36},{36... | collective-permute-start | bytes 1572872 | tf_op jit(solution)/shard_map/ppermute | solution.py:52
  33.3 1.9 %copy-start = (s32[32,8]{0,1:T(8,128)S(1)}, s32[32,8]{0,1:T(8,128)}, u32[]{:S(2)}) copy-start(s32[32,8]{0,1:T(8,128)} %param.7) | copy-start | bytes 3076
  35.5 0.7 copy-start.2
  37.2 3.0 %copy-start.1 = (f32[32]{0:T(128)}, f32[32]{0:T(128)S(1)}, u32[]{:S(2)}) copy-start(f32[32]{0:T(128)S(1)} %log_add_fusion) | copy-start | bytes 388
  40.3 4.8 %collective-permute-start.1 = (f32[2,2,2,2,16,8,128]{6,5,4,3,2,1,0:T(8,128)S(1)}, f32[2,2,2,2,16,8,128]{6,5,4,3,2,1,0:T(8,128)}, u32[]{:S(2)}, u32[]{:S(2)}) collective-permute-start(f32[2,2,2,2,16,8,128]{6,5,4,3,2,1,0:T(8,128)S(1)} %dynamic-slice_bitcast_fusion), channel_id=1, source_target_pairs={{0,32},{32,0},{1,33},{33,1},{2,34},{34,2},{3,35},{35,3},{4,36},{36... | collective-permute-start | bytes 3145736 | tf_op jit(solution)/shard_map/ppermute | solution.py:37
  94.2 5.5 %collective-permute-start.2 = (f32[8]{0:T(128)S(1)}, f32[8]{0:T(128)S(1)}, u32[]{:S(2)}, u32[]{:S(2)}) collective-permute-start(f32[8]{0:T(128)S(1)} %multiply_reduce_fusion.1), channel_id=1, source_target_pairs={{0,16},{16,0},{1,17},{17,1},{2,18},{18,2},{3,19},{19,3},{4,20},{20... | collective-permute-start | bytes 104 | tf_op jit(solution)/shard_map/ppermute | solution.py:82

commit v8 on v4

--- a/solution.py
+++ b/solution.py
@@ -46,11 +46,11 @@
 
 def reduce_blocks(partial):
     t = partial.reshape(2, 2, 2, 2, 8, 2, 16, 128)
-    t = t.transpose(3, 0, 1, 2, 5, 6, 4, 7)
+    t = t.transpose(3, 6, 0, 1, 2, 5, 4, 7)
     t = halve(t, "c", 2, 1, 0)
-    t = t.reshape(-1, *t.shape[-3:])
-    t = jnp.sum(lax.all_to_all(t, PLANE, 0, 0, tiled=True), axis=0)
-    return jnp.sum(lax.all_to_all(t, "z", 0, 0, tiled=True), axis=0)
+    t = jnp.sum(lax.all_to_all(t, "z", 0, 0, tiled=True), axis=0)
+    t = t.reshape(-1, *t.shape[-2:])
+    return jnp.sum(lax.all_to_all(t, PLANE, 0, 0, tiled=True), axis=0)
 
 
 def gather_rows(rows):

time: 108 us -> 140 us (1.30)
  blocking collectives: 62 us -> 94.8 us
    all_to_all x2, blocking collectives: 46.9 us -> 76.2 us  [the longest x1 65.1 us: reduce_blocks(): t = jnp.sum(lax.all_to_all(t, 'z', 0, 0, tiled=True), axis=0)]
    all_to_all x1, blocking collectives: 15.2 us -> 18.6 us  [per_device(): lax.all_to_all(row_power, 'z', 0, 0, tiled=True)]
  transfers between devices with their start and end apart: 3 -> 3, of which waited for: 3 -> 3; matrix products, arithmetic and copies ran while one was open for 12% -> 9% of each run, Pallas kernels for 0% -> 0%
where the time goes in v8:
time: 140 us; the launch traced here: 139 us
  blocking collectives  94.8 us (68%)
  starting transfers between devices  14.6 us (10%)
  local copies, waits for them, and re-layouts  11.2 us (8%)
  matrix products  7.88 us (6%)
  waiting for transfers between devices  6.6 us (5%)
  other arithmetic  3.07 us (2%)
    all_to_all x1, blocking collectives, reduce_blocks(): t = jnp.sum(lax.all_to_all(t, 'z', 0, 0, tiled=True), axis=0)  65.1 us
    all_to_all x1, blocking collectives, per_device(): lax.all_to_all(row_power, 'z', 0, 0, tiled=True)  18.6 us
    all_to_all x1, blocking collectives, reduce_blocks(): return jnp.sum(lax.all_to_all(t, PLANE, 0, 0, tiled=True), axis=0)  11.1 us
    all_to_all x1, starting transfers between devices, gather_rows(): lax.all_to_all(copies, REF, 0, 0, tiled=True).reshape(-1, rows.shape[1])  9.3 us
    reshape x1, local copies, waits for them, and re-layouts, roll_set(): return moved.reshape(offsets.shape[0], images.shape[0], SIDE * SIDE)  6.09 us
    dot_general x1, matrix products, roll_set(): jnp.einsum('snaj,sbj->snab', moved, cols, preferred_element_type=jnp.floa...  4.35 us
    ppermute x1, waiting for transfers between devices, per_device(): row_power = row_power + lax.ppermute(row_power, 'yl', partner('yl', 2, 1))  2.98 us
  transfers between devices with their start and end apart: 3, of which 3 were waited for; matrix products, arithmetic and copies ran while one was open for 9% of the time, Pallas kernels for 0%

profile of v8, /device:TPU:6, one launch (start us, length us, event | category | flops | bytes accessed | tf_op | source)
XLA Modules:
  0.0 138.9 jit_solution(15624970842441804576)
XLA Ops:
  0.6 2.0 %broadcast_in_dim.30 = bf16[16,8,4096]{2,1,0:T(8,128)(2,1)} broadcast(bf16[8,4096]{1,0:T(8,128)(2,1)} %param.9), dimensions={1,2} | broadcast | bytes 1114112 | tf_op jit(solution)/shard_map/broadcast_in_dim | solution.py:57
  2.6 9.3 %all-to-all-start = ((bf16[16,8,4096]{2,1,0:T(8,128)(2,1)}), bf16[16,8,4096]{2,1,0:T(8,128)(2,1)S(1)}, u32[]{:S(2)}, u32[]{:S(2)}) async-start(bf16[16,8,4096]{2,1,0:T(8,128)(2,1)} %broadcast_in_dim.30), calls=%async_computation | async-start | bytes 2097152 | tf_op jit(solution)/shard_map/all_to_all | solution.py:58
  12.0 0.5 reshape.155
  12.5 0.1 add_select_fusion
  12.6 4.4 %fusion.5 = bf16[9,32,64,64]{3,2,1,0:T(8,128)(2,1)} fusion(bf16[32,64,64,1]{2,1,0,3:T(8,128)(2,1)S(1)} %reshape.155, s32[9,64]{1,0:T(8,128)S(1)} %get-tuple-element.6, s32[9,64]{1,0:T(8,128)S(1)} %get-tuple-element.7), kind=kOutput, calls=%fused_computation.4 | convolution fusion | flops 304422912 | bytes 2626048 | tf_op jit(solution)/shard_map/snaj,sbj->snab/dot_general | solution.py:25
  17.0 6.1 %reshape.151 = bf16[9,32,4096]{2,1,0:T(8,128)(2,1)S(1)} reshape(bf16[9,32,64,64]{3,2,1,0:T(8,128)(2,1)} %fusion.5) | data formatting | bytes 4718592 | tf_op jit(solution)/shard_map/reshape | solution.py:26
  23.1 0.0 copy-start.3
  23.1 1.9 %copy.45 = bf16[36,8,32,128]{3,2,1,0:T(8,128)(2,1)} copy(bf16[36,8,32,128]{3,1,2,0:T(8,128)(2,1)S(1)} %bitcast.68) | data formatting | bytes 4718592
  25.0 0.1 copy.27
  25.1 0.1 fusion.28
  25.2 1.2 all-to-all-done
  26.4 0.3 multiply_reduce_fusion
  26.7 0.1 mul.62
  26.8 0.9 select_reduce_fusion
  27.7 0.2 exponential_reduce_fusion
  27.9 0.0 copy-start.4
  28.0 0.1 fusion.24
  28.1 0.2 copy.28
  28.3 2.6 %fusion.10 = f32[2,2,2,2,8,2,16,128]{7,4,6,5,3,2,1,0:T(8,128)S(1)} fusion(bf16[2,16,128,32,9,1,1,1,1]{2,1,0,3,4,8,7,6,5:T(8,128)(2,1)} %bitcast.69, bf16[2,2,2,2,8,32,9,1,1]{5,4,3,2,1,0,6,8,7:T(8,128)(2,1)S(1)} %bitcast.70), kind=kOutput, calls=%fused_computation.8 | convolution fusion | flops 301989888 | bytes 4530176 | tf_op jit(solution)/shard_map/psk,spq->kq/dot_general | solution.py:82
  30.9 0.1 dynamic-slice_bitcast_fusion
  31.0 2.8 %collective-permute-start = (f32[16,2,2,2,2,8,128]{6,5,0,4,3,2,1:T(8,128)S(1)}, f32[16,2,2,2,2,8,128]{6,5,0,4,3,2,1:T(8,128)}, u32[]{:S(2)}, u32[]{:S(2)}) collective-permute-start(f32[16,2,2,2,2,8,128]{6,5,0,4,3,2,1:T(8,128)S(1)} %dynamic-slice_bitcast_fusion), channel_id=1, source_target_pairs={{0,32},{32,0},{1,33},{33,1},{2,34},{34,2},{3,35},{35,3},{4,36},{36... | collective-permute-start | bytes 3145736 | tf_op jit(solution)/shard_map/ppermute | solution.py:37
  33.9 2.4 %collective-permute-done = f32[16,2,2,2,2,8,128]{6,5,0,4,3,2,1:T(8,128)} collective-permute-done((f32[16,2,2,2,2,8,128]{6,5,0,4,3,2,1:T(8,128)S(1)}, f32[16,2,2,2,2,8,128]{6,5,0,4,3,2,1:T(8,128)}, u32[]{:S(2)}, u32[]{:S(2)}) %collective-permute-start) | collective-permute-done | bytes 1048608 | tf_op jit(solution)/shard_map/ppermute | solution.py:37
  36.2 1.3 bitcast_add_fusion
  37.6 0.1 copy.32
  37.7 65.1 %all_to_all.21 = f32[16,2,2,2,2,8,128]{6,5,4,3,2,1,0:T(8,128)S(1)} all-to-all(f32[16,2,2,2,2,8,128]{6,5,4,3,2,1,0:T(8,128)S(1)} %copy.32), channel_id=1, replica_groups=mesh['yh'=2,'x'=4,'c'=2,'yl'=2,'z'=16] {'z'}, dimensions={0} | all-to-all | bytes 2097152 | tf_op jit(solution)/shard_map/all_to_all | solution.py:51
  102.8 0.1 reduce_sum.56
  102.9 11.1 %all_to_all.22 = f32[16,8,128]{2,1,0:T(8,128)S(1)} all-to-all(f32[16,8,128]{2,1,0:T(8,128)S(1)} %bitcast.71), channel_id=1, replica_groups=mesh['yh'=2,'x'=4,'c'=2,'yl'=2,'z'=16] {'yh','x','yl'}, dimensions={0} | all-to-all | bytes 131072 | tf_op jit(solution)/shard_map/all_to_all | solution.py:53
  114.0 0.1 multiply_reduce_fusion.1
  114.1 2.5 %collective-permute-start.1 = (f32[8]{0:T(128)S(1)}, f32[8]{0:T(128)S(1)}, u32[]{:S(2)}, u32[]{:S(2)}) collective-permute-start(f32[8]{0:T(128)S(1)} %multiply_reduce_fusion.1), channel_id=1, source_target_pairs={{0,16},{16,0},{1,17},{17,1},{2,18},{18,2},{3,19},{19,3},{4,20},{20... | collective-permute-start | bytes 104 | tf_op jit(solution)/shard_map/ppermute | solution.py:85
  116.6 3.0 %collective-permute-done.1 = f32[8]{0:T(128)S(1)} collective-permute-done((f32[8]{0:T(128)S(1)}, f32[8]{0:T(128)S(1)}, u32[]{:S(2)}, u32[]{:S(2)}) %collective-permute-start.1) | collective-permute-done | bytes 64 | tf_op jit(solution)/shard_map/ppermute | solution.py:85
  119.6 18.6 %all_to_all.23 = f32[16,1,8]{2,1,0:T(1,128)S(1)} all-to-all(f32[16,1,8]{2,1,0:T(1,128)S(1)} %broadcast_in_dim.58), channel_id=1, replica_groups=mesh['yh'=2,'x'=4,'c'=2,'yl'=2,'z'=16] {'z'}, dimensions={0} | all-to-all | bytes 1024 | tf_op jit(solution)/shard_map/all_to_all | solution.py:87
  138.2 0.7 divide_convert_fusion
  (16 shorter events, 0.1 us)
Async XLA Ops:
  0.6 11.3 %copy-start = (bf16[32,4096]{1,0:T(8,128)(2,1)S(1)}, bf16[32,4096]{1,0:T(8,128)(2,1)}, u32[]{:S(2)}) copy-start(bf16[32,4096]{1,0:T(8,128)(2,1)} %param.5) | copy-start | bytes 786436
  0.6 11.9 %copy-start.2 = (s32[9,2]{0,1:T(2,128)S(1)}, s32[9,2]{0,1:T(2,128)}, u32[]{:S(2)}) copy-start(s32[9,2]{0,1:T(2,128)} %param.8) | copy-start | bytes 220
  2.6 23.8 %all-to-all-start = ((bf16[16,8,4096]{2,1,0:T(8,128)(2,1)}), bf16[16,8,4096]{2,1,0:T(8,128)(2,1)S(1)}, u32[]{:S(2)}, u32[]{:S(2)}) async-start(bf16[16,8,4096]{2,1,0:T(8,128)(2,1)} %broadcast_in_dim.30), calls=%async_computation | async-start | bytes 2097152 | tf_op jit(solution)/shard_map/all_to_all | solution.py:58
  23.1 2.0 %copy-start.1 = (s32[32,8]{0,1:T(8,128)S(1)}, s32[32,8]{0,1:T(8,128)}, u32[]{:S(2)}) copy-start(s32[32,8]{0,1:T(8,128)} %param.7) | copy-start | bytes 3076
  23.1 3.8 %copy-start.3 = (f32[32]{0:T(128)S(1)}, f32[32]{0:T(128)}, u32[]{:S(2)}) copy-start(f32[32]{0:T(128)} %param.6) | copy-start | bytes 388
  27.9 3.0 %copy-start.4 = (f32[32]{0:T(128)}, f32[32]{0:T(128)S(1)}, u32[]{:S(2)}) copy-start(f32[32]{0:T(128)S(1)} %log_add_fusion) | copy-start | bytes 388
  31.0 5.2 %collective-permute-start = (f32[16,2,2,2,2,8,128]{6,5,0,4,3,2,1:T(8,128)S(1)}, f32[16,2,2,2,2,8,128]{6,5,0,4,3,2,1:T(8,128)}, u32[]{:S(2)}, u32[]{:S(2)}) collective-permute-start(f32[16,2,2,2,2,8,128]{6,5,0,4,3,2,1:T(8,128)S(1)} %dynamic-slice_bitcast_fusion), channel_id=1, source_target_pairs={{0,32},{32,0},{1,33},{33,1},{2,34},{34,2},{3,35},{35,3},{4,36},{36... | collective-permute-start | bytes 3145736 | tf_op jit(solution)/shard_map/ppermute | solution.py:37
  114.1 5.5 %collective-permute-start.1 = (f32[8]{0:T(128)S(1)}, f32[8]{0:T(128)S(1)}, u32[]{:S(2)}, u32[]{:S(2)}) collective-permute-start(f32[8]{0:T(128)S(1)} %multiply_reduce_fusion.1), channel_id=1, source_target_pairs={{0,16},{16,0},{1,17},{17,1},{2,18},{18,2},{3,19},{19,3},{4,20},{20... | collective-permute-start | bytes 104 | tf_op jit(solution)/shard_map/ppermute | solution.py:85

commit v9 on v4

--- a/solution.py
+++ b/solution.py
@@ -44,10 +44,18 @@
     return jnp.concatenate([a, b], axis=0)
 
 
-def reduce_blocks(partial):
-    t = partial.reshape(2, 2, 2, 2, 8, 2, 16, 128)
-    t = t.transpose(3, 0, 1, 2, 5, 6, 4, 7)
-    t = halve(t, "c", 2, 1, 0)
+def class_half(weight, stacked, core):
+    w = weight.reshape(*weight.shape[:2], 2, 2, 2, 2, 8)
+    w = lax.dynamic_index_in_dim(w, core, 5, keepdims=False)
+    half = jnp.einsum("psabci,spyzj->abciyzj", w, stacked.reshape(*stacked.shape[:2], 2, 16, 128),
+                      preferred_element_type=jnp.float32)
+    return half.transpose(0, 1, 2, 4, 5, 3, 6)
+
+
+def reduce_blocks(weight, stacked):
+    mine = lax.axis_index("c")
+    sent = lax.ppermute(class_half(weight, stacked, 1 - mine), "c", partner("c", 2, 1))
+    t = class_half(weight, stacked, mine) + sent
     t = t.reshape(-1, *t.shape[-3:])
     t = jnp.sum(lax.all_to_all(t, PLANE, 0, 0, tiled=True), axis=0)
     return jnp.sum(lax.all_to_all(t, "z", 0, 0, tiled=True), axis=0)
@@ -79,8 +87,7 @@
     weight = jnp.where(
         permitted_mask[:, None, :], jnp.exp(masked - evidence[:, None, None]), 0.0
     ).astype(jnp.bfloat16)
-    partial = jnp.einsum("psk,spq->kq", weight, stacked, preferred_element_type=jnp.float32)
-    shares = reduce_blocks(partial)
+    shares = reduce_blocks(weight, stacked)
     row_power = jnp.sum(shares * shares, axis=1)
     row_power = row_power + lax.ppermute(row_power, "yl", partner("yl", 2, 1))
     row_power = jnp.broadcast_to(row_power[None], (16, row_power.shape[0]))

time: 108 us -> 112 us (1.037)
  local copies, waits for them, and re-layouts: 11.1 us -> 16.2 us
  other arithmetic: 3.06 us -> 1.73 us
  blocking collectives: 62 us -> 63.2 us
    another operation x0 -> x1, local copies, waits for them, and re-layouts: none -> 7.12 us  [class_half(): stacked.reshape(*stacked.shape[:2], 2, 16, 128)]
    unnamed x12 -> x13, local copies, waits for them, and re-layouts: 2.03 us -> 0.11 us
    add x1 -> x0, other arithmetic: 1.34 us -> none  [halve(): return keep + lax.ppermute(send, axis, partner(axis, size, bit))]
    all_to_all x1, waiting for transfers between devices: 1.23 us -> 0.01 us  [gather_rows(): lax.all_to_all(copies, REF, 0, 0, tiled=True).reshape(-1, rows.shape[1])]
    all_to_all x1, blocking collectives: 21 us -> 22.1 us  [reduce_blocks(): t = jnp.sum(lax.all_to_all(t, PLANE, 0, 0, tiled=True), axis=0)]
    dot_general x1 -> x2, matrix products: 2.64 us -> 3.71 us  [class_half(): jnp.einsum('psabci,spyzj->abciyzj', w, stacked.reshape(*stacked.shape[:2]...]
  transfers between devices with their start and end apart: 3 -> 3, of which waited for: 3 -> 2; matrix products, arithmetic and copies ran while one was open for 12% -> 17% of each run, Pallas kernels for 0% -> 0%
where the time goes in v9:
time: 112 us; the launch traced here: 110 us
  blocking collectives  63.2 us (56%)
  local copies, waits for them, and re-layouts  16.2 us (14%)
  starting transfers between devices  13.4 us (12%)
  matrix products  8.94 us (8%)
  waiting for transfers between devices  5.86 us (5%)
  other arithmetic  1.73 us (2%)
    all_to_all x1, blocking collectives, reduce_blocks(): return jnp.sum(lax.all_to_all(t, 'z', 0, 0, tiled=True), axis=0)  25.9 us
    all_to_all x1, blocking collectives, reduce_blocks(): t = jnp.sum(lax.all_to_all(t, PLANE, 0, 0, tiled=True), axis=0)  22.1 us
    all_to_all x1, blocking collectives, per_device(): lax.all_to_all(row_power, 'z', 0, 0, tiled=True)  15.2 us
    all_to_all x1, starting transfers between devices, gather_rows(): lax.all_to_all(copies, REF, 0, 0, tiled=True).reshape(-1, rows.shape[1])  9.3 us
    another operation x1, local copies, waits for them, and re-layouts, class_half(): stacked.reshape(*stacked.shape[:2], 2, 16, 128)  7.12 us
    reshape x1, local copies, waits for them, and re-layouts, roll_set(): return moved.reshape(offsets.shape[0], images.shape[0], SIDE * SIDE)  6.09 us
    dot_general x1, matrix products, roll_set(): jnp.einsum('snaj,sbj->snab', moved, cols, preferred_element_type=jnp.floa...  4.35 us
    dot_general x2, matrix products, class_half(): jnp.einsum('psabci,spyzj->abciyzj', w, stacked.reshape(*stacked.shape[:2]...  3.71 us
  transfers between devices with their start and end apart: 3, of which 2 were waited for; matrix products, arithmetic and copies ran while one was open for 17% of the time, Pallas kernels for 0%

profile of v9, /device:TPU:6, one launch (start us, length us, event | category | flops | bytes accessed | tf_op | source)
XLA Modules:
  0.0 110.2 jit_solution(2875998646753169371)
XLA Ops:
  0.6 1.9 %broadcast_in_dim.26 = bf16[16,8,4096]{2,1,0:T(8,128)(2,1)} broadcast(bf16[8,4096]{1,0:T(8,128)(2,1)} %param.9), dimensions={1,2} | broadcast | bytes 1114112 | tf_op jit(solution)/shard_map/broadcast_in_dim | solution.py:65
  2.6 9.3 %all-to-all-start = ((bf16[16,8,4096]{2,1,0:T(8,128)(2,1)}), bf16[16,8,4096]{2,1,0:T(8,128)(2,1)S(1)}, u32[]{:S(2)}, u32[]{:S(2)}) async-start(bf16[16,8,4096]{2,1,0:T(8,128)(2,1)} %broadcast_in_dim.26), calls=%async_computation | async-start | bytes 2097152 | tf_op jit(solution)/shard_map/all_to_all | solution.py:66
  11.9 0.5 reshape.157
  12.5 0.1 add_select_fusion
  12.5 4.3 %fusion.5 = bf16[9,32,64,64]{3,2,1,0:T(8,128)(2,1)} fusion(bf16[32,64,64,1]{2,1,0,3:T(8,128)(2,1)S(1)} %reshape.157, s32[9,64]{1,0:T(8,128)S(1)} %get-tuple-element.8, s32[9,64]{1,0:T(8,128)S(1)} %get-tuple-element.9), kind=kOutput, calls=%fused_computation.4 | convolution fusion | flops 304422912 | bytes 2626048 | tf_op jit(solution)/shard_map/snaj,sbj->snab/dot_general | solution.py:25
  16.9 6.1 %reshape.152 = bf16[9,32,4096]{2,1,0:T(8,128)(2,1)S(1)} reshape(bf16[9,32,64,64]{3,2,1,0:T(8,128)(2,1)} %fusion.5) | data formatting | bytes 4718592 | tf_op jit(solution)/shard_map/reshape | solution.py:26
  23.0 0.0 copy-start.2
  23.0 0.0 copy-start.4
  23.0 7.1 %reshape_reshape.4 = bf16[9,32,2,16,128]{4,3,2,1,0:T(8,128)(2,1)} reshape(bf16[9,32,64,64]{3,2,1,0:T(8,128)(2,1)} %fusion.5) | data formatting | bytes 4718592 | tf_op jit(solution)/shard_map/reshape;reshape | solution.py:50
  30.1 0.1 copy.24
  30.2 0.1 fusion.36
  30.3 0.0 all-to-all-done
  30.3 0.3 multiply_reduce_fusion
  30.6 0.1 mul.58
  30.7 0.9 fusion.46
  31.6 0.2 exponential_reduce_fusion
  31.8 0.0 copy-start.5
  31.9 0.1 fusion.37
  32.0 0.2 copy.25
  32.2 0.1 constant_dynamic-slice_fusion.1
  32.3 2.7 %fusion.15 = f32[2,2,2,2,16,8,128]{6,5,4,3,2,1,0:T(8,128)S(1)} fusion(bf16[9,32,2,16,128,1,1,1]{4,3,2,1,0,7,6,5:T(8,128)(2,1)} %bitcast.65, bf16[32,9,2,2,2,1,8]{0,6,5,4,3,2,1:T(8,128)(2,1)S(1)} %get-tuple-element.3), kind=kOutput, calls=%fused_computation.11 | convolution fusion | flops 150994944 | bytes 3444736 | tf_op jit(solution)/shard_map/psabci,spyzj->abciyzj/dot_general | solution.py:50
  35.0 2.0 %collective-permute-start = (f32[2,2,2,2,16,8,128]{6,5,4,3,2,1,0:T(8,128)S(1)}, f32[2,2,2,2,16,8,128]{6,5,4,3,2,1,0:T(8,128)S(1)}, u32[]{:S(2)}, u32[]{:S(2)}) collective-permute-start(f32[2,2,2,2,16,8,128]{6,5,4,3,2,1,0:T(8,128)S(1)} %fusion.15), channel_id=1, source_target_pairs={{0,32},{32,0},{1,33},{33,1},{2,34},{34,2},{3,35},{35,3},{4,36},{36... | collective-permute-start | bytes 3145736 | tf_op jit(solution)/shard_map/ppermute | solution.py:57
  37.1 2.5 %collective-permute-done = f32[2,2,2,2,16,8,128]{6,5,4,3,2,1,0:T(8,128)S(1)} collective-permute-done((f32[2,2,2,2,16,8,128]{6,5,4,3,2,1,0:T(8,128)S(1)}, f32[2,2,2,2,16,8,128]{6,5,4,3,2,1,0:T(8,128)S(1)}, u32[]{:S(2)}, u32[]{:S(2)}) %collective-permute-start) | collective-permute-done | bytes 1048608 | tf_op jit(solution)/shard_map/ppermute | solution.py:57
  39.6 1.0 fusion.18
  40.6 22.1 %all_to_all.21 = f32[16,16,8,128]{3,2,1,0:T(8,128)S(1)} all-to-all(f32[16,16,8,128]{3,2,1,0:T(8,128)S(1)} %bitcast.68), channel_id=1, replica_groups=mesh['yh'=2,'x'=4,'c'=2,'yl'=2,'z'=16] {'yh','x','yl'}, dimensions={0} | all-to-all | bytes 2097152 | tf_op jit(solution)/shard_map/all_to_all | solution.py:60
  62.7 0.1 reduce_sum.56
  62.8 25.9 %all_to_all.22 = f32[16,8,128]{2,1,0:T(8,128)S(1)} all-to-all(f32[16,8,128]{2,1,0:T(8,128)S(1)} %reduce_sum.56), channel_id=1, replica_groups=mesh['yh'=2,'x'=4,'c'=2,'yl'=2,'z'=16] {'z'}, dimensions={0} | all-to-all | bytes 131072 | tf_op jit(solution)/shard_map/all_to_all | solution.py:61
  88.7 0.1 multiply_reduce_fusion.1
  88.8 2.1 %collective-permute-start.1 = (f32[8]{0:T(128)S(1)}, f32[8]{0:T(128)S(1)}, u32[]{:S(2)}, u32[]{:S(2)}) collective-permute-start(f32[8]{0:T(128)S(1)} %multiply_reduce_fusion.1), channel_id=1, source_target_pairs={{0,16},{16,0},{1,17},{17,1},{2,18},{18,2},{3,19},{19,3},{4,20},{20... | collective-permute-start | bytes 104 | tf_op jit(solution)/shard_map/ppermute | solution.py:92
  90.9 3.3 %collective-permute-done.1 = f32[8]{0:T(128)S(1)} collective-permute-done((f32[8]{0:T(128)S(1)}, f32[8]{0:T(128)S(1)}, u32[]{:S(2)}, u32[]{:S(2)}) %collective-permute-start.1) | collective-permute-done | bytes 64 | tf_op jit(solution)/shard_map/ppermute | solution.py:92
  94.3 15.2 %all_to_all.23 = f32[16,1,8]{2,1,0:T(1,128)S(1)} all-to-all(f32[16,1,8]{2,1,0:T(1,128)S(1)} %broadcast_in_dim.29), channel_id=1, replica_groups=mesh['yh'=2,'x'=4,'c'=2,'yl'=2,'z'=16] {'z'}, dimensions={0} | all-to-all | bytes 1024 | tf_op jit(solution)/shard_map/all_to_all | solution.py:94
  109.5 0.7 divide_convert_fusion
  (17 shorter events, 0.1 us)
Async XLA Ops:
  0.6 11.3 %copy-start.1 = (bf16[32,4096]{1,0:T(8,128)(2,1)S(1)}, bf16[32,4096]{1,0:T(8,128)(2,1)}, u32[]{:S(2)}) copy-start(bf16[32,4096]{1,0:T(8,128)(2,1)} %param.5) | copy-start | bytes 786436
  0.6 11.8 %copy-start.3 = (s32[9,2]{0,1:T(2,128)S(1)}, s32[9,2]{0,1:T(2,128)}, u32[]{:S(2)}) copy-start(s32[9,2]{0,1:T(2,128)} %param.8) | copy-start | bytes 220
  2.6 27.7 %all-to-all-start = ((bf16[16,8,4096]{2,1,0:T(8,128)(2,1)}), bf16[16,8,4096]{2,1,0:T(8,128)(2,1)S(1)}, u32[]{:S(2)}, u32[]{:S(2)}) async-start(bf16[16,8,4096]{2,1,0:T(8,128)(2,1)} %broadcast_in_dim.26), calls=%async_computation | async-start | bytes 2097152 | tf_op jit(solution)/shard_map/all_to_all | solution.py:66
  23.0 7.1 %copy-start.2 = (s32[32,8]{0,1:T(8,128)S(1)}, s32[32,8]{0,1:T(8,128)}, u32[]{:S(2)}) copy-start(s32[32,8]{0,1:T(8,128)} %param.7) | copy-start | bytes 3076
  23.0 7.7 %copy-start.4 = (f32[32]{0:T(128)S(1)}, f32[32]{0:T(128)}, u32[]{:S(2)}) copy-start(f32[32]{0:T(128)} %param.6) | copy-start | bytes 388
  31.8 3.2 %copy-start.5 = (f32[32]{0:T(128)}, f32[32]{0:T(128)S(1)}, u32[]{:S(2)}) copy-start(f32[32]{0:T(128)S(1)} %log_add_fusion) | copy-start | bytes 388
  32.3 7.3 %copy-start = (bf16[9,32,2,16,128]{4,3,2,1,0:T(8,128)(2,1)S(1)}, bf16[9,32,2,16,128]{4,3,2,1,0:T(8,128)(2,1)}, u32[]{:S(2)}) copy-start(bf16[9,32,2,16,128]{4,3,2,1,0:T(8,128)(2,1)} %reshape_reshape.4) | copy-start | bytes 7077892
  35.0 4.6 %collective-permute-start = (f32[2,2,2,2,16,8,128]{6,5,4,3,2,1,0:T(8,128)S(1)}, f32[2,2,2,2,16,8,128]{6,5,4,3,2,1,0:T(8,128)S(1)}, u32[]{:S(2)}, u32[]{:S(2)}) collective-permute-start(f32[2,2,2,2,16,8,128]{6,5,4,3,2,1,0:T(8,128)S(1)} %fusion.15), channel_id=1, source_target_pairs={{0,32},{32,0},{1,33},{33,1},{2,34},{34,2},{3,35},{35,3},{4,36},{36... | collective-permute-start | bytes 3145736 | tf_op jit(solution)/shard_map/ppermute | solution.py:57
  88.8 5.5 %collective-permute-start.1 = (f32[8]{0:T(128)S(1)}, f32[8]{0:T(128)S(1)}, u32[]{:S(2)}, u32[]{:S(2)}) collective-permute-start(f32[8]{0:T(128)S(1)} %multiply_reduce_fusion.1), channel_id=1, source_target_pairs={{0,16},{16,0},{1,17},{17,1},{2,18},{18,2},{3,19},{19,3},{4,20},{20... | collective-permute-start | bytes 104 | tf_op jit(solution)/shard_map/ppermute | solution.py:92

commit v10 on v4

--- a/solution.py
+++ b/solution.py
@@ -50,7 +50,8 @@
     t = halve(t, "c", 2, 1, 0)
     t = t.reshape(-1, *t.shape[-3:])
     t = jnp.sum(lax.all_to_all(t, PLANE, 0, 0, tiled=True), axis=0)
-    return jnp.sum(lax.all_to_all(t, "z", 0, 0, tiled=True), axis=0)
+    moved = lax.all_to_all(t.astype(jnp.bfloat16), "z", 0, 0, tiled=True)
+    return jnp.sum(moved.astype(jnp.float32), axis=0)
 
 
 def gather_rows(rows):

time: 108 us -> 107 us (level)
  no operation moved by 1% of the time
where the time goes in v10:
time: 107 us; the launch traced here: 106 us
  blocking collectives  61.7 us (58%)
  starting transfers between devices  14.3 us (13%)
  local copies, waits for them, and re-layouts  11.1 us (10%)
  matrix products  7.88 us (7%)
  waiting for transfers between devices  6.86 us (6%)
  other arithmetic  3.06 us (3%)
    all_to_all x1, blocking collectives, reduce_blocks(): moved = lax.all_to_all(t.astype(jnp.bfloat16), 'z', 0, 0, tiled=True)  25.7 us
    all_to_all x1, blocking collectives, reduce_blocks(): t = jnp.sum(lax.all_to_all(t, PLANE, 0, 0, tiled=True), axis=0)  21 us
    all_to_all x1, blocking collectives, per_device(): lax.all_to_all(row_power, 'z', 0, 0, tiled=True)  15 us
    all_to_all x1, starting transfers between devices, gather_rows(): lax.all_to_all(copies, REF, 0, 0, tiled=True).reshape(-1, rows.shape[1])  9.3 us
    reshape x1, local copies, waits for them, and re-layouts, roll_set(): return moved.reshape(offsets.shape[0], images.shape[0], SIDE * SIDE)  6.09 us
    dot_general x1, matrix products, roll_set(): jnp.einsum('snaj,sbj->snab', moved, cols, preferred_element_type=jnp.floa...  4.35 us
    ppermute x1, waiting for transfers between devices, per_device(): row_power = row_power + lax.ppermute(row_power, 'yl', partner('yl', 2, 1))  3.24 us
    ppermute x1, starting transfers between devices, halve(): return keep + lax.ppermute(send, axis, partner(axis, size, bit))  2.79 us
  transfers between devices with their start and end apart: 3, of which 3 were waited for; matrix products, arithmetic and copies ran while one was open for 12% of the time, Pallas kernels for 0%

profile of v10, /device:TPU:6, one launch (start us, length us, event | category | flops | bytes accessed | tf_op | source)
XLA Modules:
  0.0 105.6 jit_solution(10379342769889098772)
XLA Ops:
  0.6 2.0 %broadcast_in_dim.30 = bf16[16,8,4096]{2,1,0:T(8,128)(2,1)} broadcast(bf16[8,4096]{1,0:T(8,128)(2,1)} %param.9), dimensions={1,2} | broadcast | bytes 1114112 | tf_op jit(solution)/shard_map/broadcast_in_dim | solution.py:58
  2.6 9.3 %all-to-all-start = ((bf16[16,8,4096]{2,1,0:T(8,128)(2,1)}), bf16[16,8,4096]{2,1,0:T(8,128)(2,1)S(1)}, u32[]{:S(2)}, u32[]{:S(2)}) async-start(bf16[16,8,4096]{2,1,0:T(8,128)(2,1)} %broadcast_in_dim.30), calls=%async_computation | async-start | bytes 2097152 | tf_op jit(solution)/shard_map/all_to_all | solution.py:59
  12.0 0.5 reshape.155
  12.5 0.1 add_select_fusion
  12.6 4.4 %fusion.5 = bf16[9,32,64,64]{3,2,1,0:T(8,128)(2,1)} fusion(bf16[32,64,64,1]{2,1,0,3:T(8,128)(2,1)S(1)} %reshape.155, s32[9,64]{1,0:T(8,128)S(1)} %get-tuple-element.6, s32[9,64]{1,0:T(8,128)S(1)} %get-tuple-element.7), kind=kOutput, calls=%fused_computation.4 | convolution fusion | flops 304422912 | bytes 2626048 | tf_op jit(solution)/shard_map/snaj,sbj->snab/dot_general | solution.py:25
  17.0 6.1 %reshape.151 = bf16[9,32,4096]{2,1,0:T(8,128)(2,1)S(1)} reshape(bf16[9,32,64,64]{3,2,1,0:T(8,128)(2,1)} %fusion.5) | data formatting | bytes 4718592 | tf_op jit(solution)/shard_map/reshape | solution.py:26
  23.1 0.0 copy-start.1
  23.1 0.0 copy-start.3
  23.1 1.9 %copy.37 = bf16[36,8,32,128]{3,2,1,0:T(8,128)(2,1)} copy(bf16[36,8,32,128]{3,1,2,0:T(8,128)(2,1)S(1)} %bitcast.68) | data formatting | bytes 4718592
  25.0 0.1 copy.20
  25.1 0.1 fusion.28
  25.2 1.2 %all-to-all-done = bf16[16,8,4096]{2,1,0:T(8,128)(2,1)S(1)} async-done(((bf16[16,8,4096]{2,1,0:T(8,128)(2,1)}), bf16[16,8,4096]{2,1,0:T(8,128)(2,1)S(1)}, u32[]{:S(2)}, u32[]{:S(2)}) %all-to-all-start) | async-done | bytes 1048608 | tf_op jit(solution)/shard_map/all_to_all | solution.py:59
  26.4 0.3 multiply_reduce_fusion
  26.7 0.1 mul.62
  26.8 0.9 select_reduce_fusion
  27.7 0.2 exponential_reduce_fusion
  27.9 0.0 copy-start.4
  28.0 0.1 fusion.24
  28.1 0.2 copy.21
  28.3 2.6 %fusion.10 = f32[2,2,2,2,8,2,16,128]{7,4,6,5,3,2,1,0:T(8,128)S(1)} fusion(bf16[2,16,128,32,9,1,1,1,1]{2,1,0,3,4,8,7,6,5:T(8,128)(2,1)} %bitcast.70, bf16[2,2,2,2,8,32,9,1,1]{5,4,3,2,1,0,6,8,7:T(8,128)(2,1)S(1)} %bitcast.71), kind=kOutput, calls=%fused_computation.8 | convolution fusion | flops 301989888 | bytes 4530176 | tf_op jit(solution)/shard_map/psk,spq->kq/dot_general | solution.py:83
  30.9 0.1 dynamic-slice_bitcast_fusion
  31.0 2.8 %collective-permute-start = (f32[2,2,2,2,16,8,128]{6,5,4,3,2,1,0:T(8,128)S(1)}, f32[2,2,2,2,16,8,128]{6,5,4,3,2,1,0:T(8,128)}, u32[]{:S(2)}, u32[]{:S(2)}) collective-permute-start(f32[2,2,2,2,16,8,128]{6,5,4,3,2,1,0:T(8,128)S(1)} %dynamic-slice_bitcast_fusion), channel_id=1, source_target_pairs={{0,32},{32,0},{1,33},{33,1},{2,34},{34,2},{3,35},{35,3},{4,36},{36... | collective-permute-start | bytes 3145736 | tf_op jit(solution)/shard_map/ppermute | solution.py:37
  33.9 2.4 %collective-permute-done = f32[2,2,2,2,16,8,128]{6,5,4,3,2,1,0:T(8,128)} collective-permute-done((f32[2,2,2,2,16,8,128]{6,5,4,3,2,1,0:T(8,128)S(1)}, f32[2,2,2,2,16,8,128]{6,5,4,3,2,1,0:T(8,128)}, u32[]{:S(2)}, u32[]{:S(2)}) %collective-permute-start) | collective-permute-done | bytes 1048608 | tf_op jit(solution)/shard_map/ppermute | solution.py:37
  36.2 1.3 %bitcast_add_fusion = f32[2,2,2,2,16,8,128]{6,5,4,3,2,1,0:T(8,128)S(1)} fusion(f32[2,2,2,2,16,8,128]{6,5,4,3,2,1,0:T(8,128)} %collective-permute-done, f32[2,2,2,2,8,2,16,128]{7,4,6,5,3,2,1,0:T(8,128)S(1)} %fusion.10, s32[]{:T(128)S(6)} %select_n.54), kind=kLoop, calls=%fused_computation.11 | loop fusion | flops 262144 | bytes 3145732 | tf_op jit(solution)/shard_map/add | solution.py:37
  37.6 21.0 %all_to_all.21 = f32[16,16,8,128]{3,2,1,0:T(8,128)S(1)} all-to-all(f32[16,16,8,128]{3,2,1,0:T(8,128)S(1)} %bitcast.69), channel_id=1, replica_groups=mesh['yh'=2,'x'=4,'c'=2,'yl'=2,'z'=16] {'yh','x','yl'}, dimensions={0} | all-to-all | bytes 2097152 | tf_op jit(solution)/shard_map/all_to_all | solution.py:52
  58.6 0.1 reduce_sum.56
  58.6 25.7 %all_to_all.22 = bf16[16,8,128]{2,1,0:T(8,128)(2,1)S(1)} all-to-all(bf16[16,8,128]{2,1,0:T(8,128)(2,1)S(1)} %reduce_sum.56), channel_id=1, replica_groups=mesh['yh'=2,'x'=4,'c'=2,'yl'=2,'z'=16] {'z'}, dimensions={0} | all-to-all | bytes 65536 | tf_op jit(solution)/shard_map/all_to_all | solution.py:53
  84.3 0.1 multiply_reduce_fusion.1
  84.4 2.2 %collective-permute-start.1 = (f32[8]{0:T(128)S(1)}, f32[8]{0:T(128)S(1)}, u32[]{:S(2)}, u32[]{:S(2)}) collective-permute-start(f32[8]{0:T(128)S(1)} %multiply_reduce_fusion.1), channel_id=1, source_target_pairs={{0,16},{16,0},{1,17},{17,1},{2,18},{18,2},{3,19},{19,3},{4,20},{20... | collective-permute-start | bytes 104 | tf_op jit(solution)/shard_map/ppermute | solution.py:86
  86.7 3.2 %collective-permute-done.1 = f32[8]{0:T(128)S(1)} collective-permute-done((f32[8]{0:T(128)S(1)}, f32[8]{0:T(128)S(1)}, u32[]{:S(2)}, u32[]{:S(2)}) %collective-permute-start.1) | collective-permute-done | bytes 64 | tf_op jit(solution)/shard_map/ppermute | solution.py:86
  89.9 15.0 %all_to_all.23 = f32[16,1,8]{2,1,0:T(1,128)S(1)} all-to-all(f32[16,1,8]{2,1,0:T(1,128)S(1)} %broadcast_in_dim.58), channel_id=1, replica_groups=mesh['yh'=2,'x'=4,'c'=2,'yl'=2,'z'=16] {'z'}, dimensions={0} | all-to-all | bytes 1024 | tf_op jit(solution)/shard_map/all_to_all | solution.py:88
  104.9 0.7 divide_convert_fusion
  (15 shorter events, 0.1 us)
Async XLA Ops:
  0.6 11.3 %copy-start = (bf16[32,4096]{1,0:T(8,128)(2,1)S(1)}, bf16[32,4096]{1,0:T(8,128)(2,1)}, u32[]{:S(2)}) copy-start(bf16[32,4096]{1,0:T(8,128)(2,1)} %param.5) | copy-start | bytes 786436
  0.6 11.9 %copy-start.2 = (s32[9,2]{0,1:T(2,128)S(1)}, s32[9,2]{0,1:T(2,128)}, u32[]{:S(2)}) copy-start(s32[9,2]{0,1:T(2,128)} %param.8) | copy-start | bytes 220
  2.6 23.8 %all-to-all-start = ((bf16[16,8,4096]{2,1,0:T(8,128)(2,1)}), bf16[16,8,4096]{2,1,0:T(8,128)(2,1)S(1)}, u32[]{:S(2)}, u32[]{:S(2)}) async-start(bf16[16,8,4096]{2,1,0:T(8,128)(2,1)} %broadcast_in_dim.30), calls=%async_computation | async-start | bytes 2097152 | tf_op jit(solution)/shard_map/all_to_all | solution.py:59
  23.1 2.0 %copy-start.1 = (s32[32,8]{0,1:T(8,128)S(1)}, s32[32,8]{0,1:T(8,128)}, u32[]{:S(2)}) copy-start(s32[32,8]{0,1:T(8,128)} %param.7) | copy-start | bytes 3076
  23.1 3.8 %copy-start.3 = (f32[32]{0:T(128)S(1)}, f32[32]{0:T(128)}, u32[]{:S(2)}) copy-start(f32[32]{0:T(128)} %param.6) | copy-start | bytes 388
  27.9 3.0 %copy-start.4 = (f32[32]{0:T(128)}, f32[32]{0:T(128)S(1)}, u32[]{:S(2)}) copy-start(f32[32]{0:T(128)S(1)} %log_add_fusion) | copy-start | bytes 388
  31.0 5.2 %collective-permute-start = (f32[2,2,2,2,16,8,128]{6,5,4,3,2,1,0:T(8,128)S(1)}, f32[2,2,2,2,16,8,128]{6,5,4,3,2,1,0:T(8,128)}, u32[]{:S(2)}, u32[]{:S(2)}) collective-permute-start(f32[2,2,2,2,16,8,128]{6,5,4,3,2,1,0:T(8,128)S(1)} %dynamic-slice_bitcast_fusion), channel_id=1, source_target_pairs={{0,32},{32,0},{1,33},{33,1},{2,34},{34,2},{3,35},{35,3},{4,36},{36... | collective-permute-start | bytes 3145736 | tf_op jit(solution)/shard_map/ppermute | solution.py:37
  84.4 5.5 %collective-permute-start.1 = (f32[8]{0:T(128)S(1)}, f32[8]{0:T(128)S(1)}, u32[]{:S(2)}, u32[]{:S(2)}) collective-permute-start(f32[8]{0:T(128)S(1)} %multiply_reduce_fusion.1), channel_id=1, source_target_pairs={{0,16},{16,0},{1,17},{17,1},{2,18},{18,2},{3,19},{19,3},{4,20},{20... | collective-permute-start | bytes 104 | tf_op jit(solution)/shard_map/ppermute | solution.py:86

commit v11 on v2

--- a/solution.py
+++ b/solution.py
@@ -8,7 +8,7 @@
 REF = ("yh", "x", "c")
 DOM = ("yl", "z")
 ALL = REF + DOM
-SPREAD = ("yh", "x", "yl", "z")
+PLANE = ("yh", "x")
 
 
 def shift_matrices(moves):
@@ -48,8 +48,9 @@
     t = partial.reshape(2, 2, 2, 2, 8, 2, 16, 128)
     t = t.transpose(3, 0, 1, 2, 5, 6, 4, 7)
     t = halve(t, "c", 2, 1, 0)
-    t = t.reshape(-1, *t.shape[-2:])
-    return jnp.sum(lax.all_to_all(t, SPREAD, 0, 0, tiled=True), axis=0)
+    t = t.reshape(-1, 32, *t.shape[-2:])
+    t = jnp.sum(lax.all_to_all(t, PLANE, 0, 0, tiled=True), axis=0)
+    return jnp.sum(lax.all_to_all(t, DOM, 0, 0, tiled=True), axis=0)
 
 
 def gather_rows(rows):

time: 133 us -> 107 us (0.80)
  blocking collectives: 92.4 us -> 66.8 us
    all_to_all x1 -> x2, blocking collectives: 74.6 us -> 50.5 us  [the longest x1 29.3 us: reduce_blocks(): return jnp.sum(lax.all_to_all(t, DOM, 0, 0, tiled=True), axis=0)]
    all_to_all x1, blocking collectives: 17.8 us -> 16.3 us  [per_device(): lax.all_to_all(row_power, DOM, 0, 0, tiled=True)]
  transfers between devices with their start and end apart: 2 -> 2, of which waited for: 2 -> 2; matrix products, arithmetic and copies ran while one was open for 10% -> 13% of each run, Pallas kernels for 0% -> 0%
where the time goes in v11:
time: 107 us; the launch traced here: 105 us
  blocking collectives  66.8 us (62%)
  starting transfers between devices  12.1 us (11%)
  local copies, waits for them, and re-layouts  11.1 us (10%)
  matrix products  7.88 us (7%)
  waiting for transfers between devices  3.62 us (3%)
  other arithmetic  3.09 us (3%)
    all_to_all x1, blocking collectives, reduce_blocks(): return jnp.sum(lax.all_to_all(t, DOM, 0, 0, tiled=True), axis=0)  29.3 us
    all_to_all x1, blocking collectives, reduce_blocks(): t = jnp.sum(lax.all_to_all(t, PLANE, 0, 0, tiled=True), axis=0)  21.2 us
    all_to_all x1, blocking collectives, per_device(): lax.all_to_all(row_power, DOM, 0, 0, tiled=True)  16.3 us
    all_to_all x1, starting transfers between devices, gather_rows(): lax.all_to_all(copies, REF, 0, 0, tiled=True).reshape(-1, rows.shape[1])  9.3 us
    reshape x1, local copies, waits for them, and re-layouts, roll_set(): return moved.reshape(offsets.shape[0], images.shape[0], SIDE * SIDE)  6.09 us
    dot_general x1, matrix products, roll_set(): jnp.einsum('snaj,sbj->snab', moved, cols, preferred_element_type=jnp.floa...  4.35 us
    ppermute x1, starting transfers between devices, halve(): return keep + lax.ppermute(send, axis, partner(axis, size, bit))  2.79 us
    dot_general x1, matrix products, per_device(): jnp.einsum('psk,spq->kq', weight, stacked, preferred_element_type=jnp.flo...  2.64 us
  transfers between devices with their start and end apart: 2, of which 2 were waited for; matrix products, arithmetic and copies ran while one was open for 13% of the time, Pallas kernels for 0%

profile of v11, /device:TPU:6, one launch (start us, length us, event | category | flops | bytes accessed | tf_op | source)
XLA Modules:
  0.0 105.4 jit_solution(1457294207818578620)
XLA Ops:
  0.6 2.0 %broadcast_in_dim.30 = bf16[16,8,4096]{2,1,0:T(8,128)(2,1)} broadcast(bf16[8,4096]{1,0:T(8,128)(2,1)} %param.9), dimensions={1,2} | broadcast | bytes 1114112 | tf_op jit(solution)/shard_map/broadcast_in_dim | solution.py:57
  2.6 9.3 %all-to-all-start = ((bf16[16,8,4096]{2,1,0:T(8,128)(2,1)}), bf16[16,8,4096]{2,1,0:T(8,128)(2,1)S(1)}, u32[]{:S(2)}, u32[]{:S(2)}) async-start(bf16[16,8,4096]{2,1,0:T(8,128)(2,1)} %broadcast_in_dim.30), calls=%async_computation | async-start | bytes 2097152 | tf_op jit(solution)/shard_map/all_to_all | solution.py:58
  12.0 0.5 reshape.155
  12.5 0.0 copy-done.2
  12.5 0.1 add_select_fusion
  12.6 4.4 %fusion.5 = bf16[9,32,64,64]{3,2,1,0:T(8,128)(2,1)} fusion(bf16[32,64,64,1]{2,1,0,3:T(8,128)(2,1)S(1)} %reshape.155, s32[9,64]{1,0:T(8,128)S(1)} %get-tuple-element.6, s32[9,64]{1,0:T(8,128)S(1)} %get-tuple-element.7), kind=kOutput, calls=%fused_computation.4 | convolution fusion | flops 304422912 | bytes 2626048 | tf_op jit(solution)/shard_map/snaj,sbj->snab/dot_general | solution.py:25
  17.0 6.1 %reshape.151 = bf16[9,32,4096]{2,1,0:T(8,128)(2,1)S(1)} reshape(bf16[9,32,64,64]{3,2,1,0:T(8,128)(2,1)} %fusion.5) | data formatting | bytes 4718592 | tf_op jit(solution)/shard_map/reshape | solution.py:26
  23.1 0.0 copy-start.1
  23.1 0.0 copy-start.3
  23.1 1.9 %copy.37 = bf16[36,8,32,128]{3,2,1,0:T(8,128)(2,1)} copy(bf16[36,8,32,128]{3,1,2,0:T(8,128)(2,1)S(1)} %bitcast.68) | data formatting | bytes 4718592
  25.0 0.1 copy.20
  25.1 0.1 fusion.28
  25.2 1.2 %all-to-all-done = bf16[16,8,4096]{2,1,0:T(8,128)(2,1)S(1)} async-done(((bf16[16,8,4096]{2,1,0:T(8,128)(2,1)}), bf16[16,8,4096]{2,1,0:T(8,128)(2,1)S(1)}, u32[]{:S(2)}, u32[]{:S(2)}) %all-to-all-start) | async-done | bytes 1048608 | tf_op jit(solution)/shard_map/all_to_all | solution.py:58
  26.4 0.3 multiply_reduce_fusion
  26.7 0.1 mul.62
  26.8 0.9 select_reduce_fusion
  27.7 0.2 exponential_reduce_fusion
  27.9 0.0 copy-start.4
  28.0 0.1 fusion.24
  28.1 0.2 copy.21
  28.3 2.6 %fusion.10 = f32[2,2,2,2,8,2,16,128]{7,4,6,5,3,2,1,0:T(8,128)S(1)} fusion(bf16[2,16,128,32,9,1,1,1,1]{2,1,0,3,4,8,7,6,5:T(8,128)(2,1)} %bitcast.70, bf16[2,2,2,2,8,32,9,1,1]{5,4,3,2,1,0,6,8,7:T(8,128)(2,1)S(1)} %bitcast.71), kind=kOutput, calls=%fused_computation.8 | convolution fusion | flops 301989888 | bytes 4530176 | tf_op jit(solution)/shard_map/psk,spq->kq/dot_general | solution.py:82
  30.9 0.1 dynamic-slice_bitcast_fusion
  31.0 2.8 %collective-permute-start = (f32[2,2,2,2,16,8,128]{6,5,4,3,2,1,0:T(8,128)S(1)}, f32[2,2,2,2,16,8,128]{6,5,4,3,2,1,0:T(8,128)}, u32[]{:S(2)}, u32[]{:S(2)}) collective-permute-start(f32[2,2,2,2,16,8,128]{6,5,4,3,2,1,0:T(8,128)S(1)} %dynamic-slice_bitcast_fusion), channel_id=1, source_target_pairs={{0,32},{32,0},{1,33},{33,1},{2,34},{34,2},{3,35},{35,3},{4,36},{36... | collective-permute-start | bytes 3145736 | tf_op jit(solution)/shard_map/ppermute | solution.py:37
  33.9 2.4 %collective-permute-done = f32[2,2,2,2,16,8,128]{6,5,4,3,2,1,0:T(8,128)} collective-permute-done((f32[2,2,2,2,16,8,128]{6,5,4,3,2,1,0:T(8,128)S(1)}, f32[2,2,2,2,16,8,128]{6,5,4,3,2,1,0:T(8,128)}, u32[]{:S(2)}, u32[]{:S(2)}) %collective-permute-start) | collective-permute-done | bytes 1048608 | tf_op jit(solution)/shard_map/ppermute | solution.py:37
  36.2 1.3 %bitcast_add_fusion = f32[2,2,2,2,16,8,128]{6,5,4,3,2,1,0:T(8,128)S(1)} fusion(f32[2,2,2,2,16,8,128]{6,5,4,3,2,1,0:T(8,128)} %collective-permute-done, f32[2,2,2,2,8,2,16,128]{7,4,6,5,3,2,1,0:T(8,128)S(1)} %fusion.10, s32[]{:T(128)S(6)} %select_n.54), kind=kLoop, calls=%fused_computation.11 | loop fusion | flops 262144 | bytes 3145732 | tf_op jit(solution)/shard_map/add | solution.py:37
  37.6 21.2 %all_to_all.21 = f32[8,32,8,128]{3,2,1,0:T(8,128)S(1)} all-to-all(f32[8,32,8,128]{3,2,1,0:T(8,128)S(1)} %bitcast.69), channel_id=1, replica_groups=mesh['yh'=2,'x'=4,'c'=2,'yl'=2,'z'=16] {'yh','x'}, dimensions={0} | all-to-all | bytes 2097152 | tf_op jit(solution)/shard_map/all_to_all | solution.py:52
  58.8 0.1 reduce_sum.56
  58.8 29.3 %all_to_all.22 = f32[32,8,128]{2,1,0:T(8,128)S(1)} all-to-all(f32[32,8,128]{2,1,0:T(8,128)S(1)} %reduce_sum.56), channel_id=1, replica_groups=mesh['yh'=2,'x'=4,'c'=2,'yl'=2,'z'=16] {'yl','z'}, dimensions={0} | all-to-all | bytes 262144 | tf_op jit(solution)/shard_map/all_to_all | solution.py:53
  88.2 0.1 multiply_reduce_fusion.1
  88.3 16.3 %all_to_all.23 = f32[32,1,8]{2,1,0:T(1,128)S(1)} all-to-all(f32[32,1,8]{2,1,0:T(1,128)S(1)} %broadcast_in_dim.58), channel_id=1, replica_groups=mesh['yh'=2,'x'=4,'c'=2,'yl'=2,'z'=16] {'yl','z'}, dimensions={0} | all-to-all | bytes 2048 | tf_op jit(solution)/shard_map/all_to_all | solution.py:86
  104.7 0.1 reduce_sum.59
  104.7 0.7 divide_convert_fusion
  (12 shorter events, 0.1 us)
Async XLA Ops:
  0.6 11.3 %copy-start = (bf16[32,4096]{1,0:T(8,128)(2,1)S(1)}, bf16[32,4096]{1,0:T(8,128)(2,1)}, u32[]{:S(2)}) copy-start(bf16[32,4096]{1,0:T(8,128)(2,1)} %param.5) | copy-start | bytes 786436
  0.6 11.9 %copy-start.2 = (s32[9,2]{0,1:T(2,128)S(1)}, s32[9,2]{0,1:T(2,128)}, u32[]{:S(2)}) copy-start(s32[9,2]{0,1:T(2,128)} %param.8) | copy-start | bytes 220
  2.6 23.8 %all-to-all-start = ((bf16[16,8,4096]{2,1,0:T(8,128)(2,1)}), bf16[16,8,4096]{2,1,0:T(8,128)(2,1)S(1)}, u32[]{:S(2)}, u32[]{:S(2)}) async-start(bf16[16,8,4096]{2,1,0:T(8,128)(2,1)} %broadcast_in_dim.30), calls=%async_computation | async-start | bytes 2097152 | tf_op jit(solution)/shard_map/all_to_all | solution.py:58
  23.1 2.0 %copy-start.1 = (s32[32,8]{0,1:T(8,128)S(1)}, s32[32,8]{0,1:T(8,128)}, u32[]{:S(2)}) copy-start(s32[32,8]{0,1:T(8,128)} %param.7) | copy-start | bytes 3076
  23.1 3.8 %copy-start.3 = (f32[32]{0:T(128)S(1)}, f32[32]{0:T(128)}, u32[]{:S(2)}) copy-start(f32[32]{0:T(128)} %param.6) | copy-start | bytes 388
  27.9 3.0 %copy-start.4 = (f32[32]{0:T(128)}, f32[32]{0:T(128)S(1)}, u32[]{:S(2)}) copy-start(f32[32]{0:T(128)S(1)} %log_add_fusion) | copy-start | bytes 388
  31.0 5.2 %collective-permute-start = (f32[2,2,2,2,16,8,128]{6,5,4,3,2,1,0:T(8,128)S(1)}, f32[2,2,2,2,16,8,128]{6,5,4,3,2,1,0:T(8,128)}, u32[]{:S(2)}, u32[]{:S(2)}) collective-permute-start(f32[2,2,2,2,16,8,128]{6,5,4,3,2,1,0:T(8,128)S(1)} %dynamic-slice_bitcast_fusion), channel_id=1, source_target_pairs={{0,32},{32,0},{1,33},{33,1},{2,34},{34,2},{3,35},{35,3},{4,36},{36... | collective-permute-start | bytes 3145736 | tf_op jit(solution)/shard_map/ppermute | solution.py:37

commit v12 on v11

--- a/solution.py
+++ b/solution.py
@@ -8,7 +8,7 @@
 REF = ("yh", "x", "c")
 DOM = ("yl", "z")
 ALL = REF + DOM
-PLANE = ("yh", "x")
+PLANE = ("yh", "x", "c")
 
 
 def shift_matrices(moves):
@@ -46,8 +46,7 @@
 
 def reduce_blocks(partial):
     t = partial.reshape(2, 2, 2, 2, 8, 2, 16, 128)
-    t = t.transpose(3, 0, 1, 2, 5, 6, 4, 7)
-    t = halve(t, "c", 2, 1, 0)
+    t = t.transpose(0, 1, 2, 3, 5, 6, 4, 7)
     t = t.reshape(-1, 32, *t.shape[-2:])
     t = jnp.sum(lax.all_to_all(t, PLANE, 0, 0, tiled=True), axis=0)
     return jnp.sum(lax.all_to_all(t, DOM, 0, 0, tiled=True), axis=0)

time: 107 us -> 112 us (1.047); the launches traced: 105 us -> 112 us
  blocking collectives: 66.8 us -> 80 us
  starting transfers between devices: 12.1 us -> 9.3 us
  waiting for transfers between devices: 3.62 us -> 1.23 us
  other arithmetic: 3.09 us -> 1.8 us
    all_to_all x1, blocking collectives: 21.2 us -> 32.4 us  [reduce_blocks(): t = jnp.sum(lax.all_to_all(t, PLANE, 0, 0, tiled=True), axis=0)]
    ppermute x1 -> x0, starting transfers between devices: 2.79 us -> none  [halve(): return keep + lax.ppermute(send, axis, partner(axis, size, bit))]
    ppermute x1 -> x0, waiting for transfers between devices: 2.39 us -> none  [halve(): return keep + lax.ppermute(send, axis, partner(axis, size, bit))]
    all_to_all x1, blocking collectives: 29.3 us -> 31.2 us  [reduce_blocks(): return jnp.sum(lax.all_to_all(t, DOM, 0, 0, tiled=True), axis=0)]
    add x1 -> x0, other arithmetic: 1.34 us -> none  [halve(): return keep + lax.ppermute(send, axis, partner(axis, size, bit))]
  transfers between devices with their start and end apart: 2 -> 1, of which waited for: 2 -> 1; matrix products, arithmetic and copies ran while one was open for 13% -> 12% of each run, Pallas kernels for 0% -> 0%
where the time goes in v12:
time: 112 us
  blocking collectives  80 us (71%)
  local copies, waits for them, and re-layouts  11 us (10%)
  starting transfers between devices  9.3 us (8%)
  matrix products  7.88 us (7%)
  other arithmetic  1.8 us (2%)
  waiting for transfers between devices  1.23 us (1%)
    all_to_all x1, blocking collectives, reduce_blocks(): t = jnp.sum(lax.all_to_all(t, PLANE, 0, 0, tiled=True), axis=0)  32.4 us
    all_to_all x1, blocking collectives, reduce_blocks(): return jnp.sum(lax.all_to_all(t, DOM, 0, 0, tiled=True), axis=0)  31.2 us
    all_to_all x1, blocking collectives, per_device(): lax.all_to_all(row_power, DOM, 0, 0, tiled=True)  16.3 us
    all_to_all x1, starting transfers between devices, gather_rows(): lax.all_to_all(copies, REF, 0, 0, tiled=True).reshape(-1, rows.shape[1])  9.3 us
    reshape x1, local copies, waits for them, and re-layouts, roll_set(): return moved.reshape(offsets.shape[0], images.shape[0], SIDE * SIDE)  6.1 us
    dot_general x1, matrix products, roll_set(): jnp.einsum('snaj,sbj->snab', moved, cols, preferred_element_type=jnp.floa...  4.35 us
    dot_general x1, matrix products, per_device(): jnp.einsum('psk,spq->kq', weight, stacked, preferred_element_type=jnp.flo...  2.64 us
  transfers between devices with their start and end apart: 1, of which 1 were waited for; matrix products, arithmetic and copies ran while one was open for 12% of the time, Pallas kernels for 0%

profile of v12, /device:TPU:6, one launch (start us, length us, event | category | flops | bytes accessed | tf_op | source)
XLA Modules:
  0.0 112.0 jit_solution(6507082858752878241)
XLA Ops:
  0.6 0.0 copy-start
  0.6 0.0 copy-start.2
  0.6 2.0 %broadcast_in_dim.30 = bf16[16,8,4096]{2,1,0:T(8,128)(2,1)} broadcast(bf16[8,4096]{1,0:T(8,128)(2,1)} %param.9), dimensions={1,2} | broadcast | bytes 1114112 | tf_op jit(solution)/shard_map/broadcast_in_dim | solution.py:56
  2.6 9.3 %all-to-all-start = ((bf16[16,8,4096]{2,1,0:T(8,128)(2,1)}), bf16[16,8,4096]{2,1,0:T(8,128)(2,1)S(1)}, u32[]{:S(2)}, u32[]{:S(2)}) async-start(bf16[16,8,4096]{2,1,0:T(8,128)(2,1)} %broadcast_in_dim.30), calls=%async_computation | async-start | bytes 2097152 | tf_op jit(solution)/shard_map/all_to_all | solution.py:57
  11.9 0.0 copy-done
  12.0 0.5 reshape.155
  12.5 0.0 copy-done.2
  12.5 0.1 add_select_fusion
  12.6 4.4 %fusion.5 = bf16[9,32,64,64]{3,2,1,0:T(8,128)(2,1)} fusion(bf16[32,64,64,1]{2,1,0,3:T(8,128)(2,1)S(1)} %reshape.155, s32[9,64]{1,0:T(8,128)S(1)} %get-tuple-element.6, s32[9,64]{1,0:T(8,128)S(1)} %get-tuple-element.7), kind=kOutput, calls=%fused_computation.4 | convolution fusion | flops 304422912 | bytes 2626048 | tf_op jit(solution)/shard_map/snaj,sbj->snab/dot_general | solution.py:25
  17.0 6.1 %reshape.151 = bf16[9,32,4096]{2,1,0:T(8,128)(2,1)S(1)} reshape(bf16[9,32,64,64]{3,2,1,0:T(8,128)(2,1)} %fusion.5) | data formatting | bytes 4718592 | tf_op jit(solution)/shard_map/reshape | solution.py:26
  23.1 0.0 copy-done.1
  23.1 0.1 copy.17
  23.2 1.9 %copy.32 = bf16[36,8,32,128]{3,2,1,0:T(8,128)(2,1)} copy(bf16[36,8,32,128]{3,1,2,0:T(8,128)(2,1)S(1)} %bitcast.60) | data formatting | bytes 4718592
  25.1 0.1 fusion.25
  25.2 1.2 %all-to-all-done = bf16[16,8,4096]{2,1,0:T(8,128)(2,1)S(1)} async-done(((bf16[16,8,4096]{2,1,0:T(8,128)(2,1)}), bf16[16,8,4096]{2,1,0:T(8,128)(2,1)S(1)}, u32[]{:S(2)}, u32[]{:S(2)}) %all-to-all-start) | async-done | bytes 1048608 | tf_op jit(solution)/shard_map/all_to_all | solution.py:57
  26.4 0.3 multiply_reduce_fusion
  26.7 0.1 mul.62
  26.8 0.0 copy-done.3
  26.8 0.9 select_reduce_fusion
  27.7 0.2 exponential_reduce_fusion
  27.9 0.0 copy-start.4
  28.0 0.1 fusion.21
  28.1 0.2 copy.18
  28.3 2.6 %fusion.8 = f32[2,2,2,2,8,2,16,128,1]{7,4,8,6,5,3,2,1,0:T(8,128)S(1)} fusion(bf16[2,16,128,32,9,1,1,1,1]{2,1,0,3,4,8,7,6,5:T(8,128)(2,1)} %bitcast.61, bf16[2,2,2,2,8,32,9,1,1]{5,4,3,2,1,0,6,8,7:T(8,128)(2,1)S(1)} %bitcast.63), kind=kOutput, calls=%fused_computation.5 | convolution fusion | flops 301989888 | bytes 4530176 | tf_op jit(solution)/shard_map/psk,spq->kq/dot_general | solution.py:81
  30.9 0.0 copy-done.4
  30.9 32.4 %all_to_all.21 = f32[16,32,8,128]{3,2,1,0:T(8,128)S(1)} all-to-all(f32[16,32,8,128]{3,2,1,0:T(8,128)S(1)} %bitcast.62), channel_id=1, replica_groups=mesh['yh'=2,'x'=4,'c'=2,'yl'=2,'z'=16] {'yh','x','c'}, dimensions={0} | all-to-all | bytes 4194304 | tf_op jit(solution)/shard_map/all_to_all | solution.py:51
  63.4 0.1 reduce_sum.56
  63.5 31.2 %all_to_all.22 = f32[32,8,128]{2,1,0:T(8,128)S(1)} all-to-all(f32[32,8,128]{2,1,0:T(8,128)S(1)} %reduce_sum.56), channel_id=1, replica_groups=mesh['yh'=2,'x'=4,'c'=2,'yl'=2,'z'=16] {'yl','z'}, dimensions={0} | all-to-all | bytes 262144 | tf_op jit(solution)/shard_map/all_to_all | solution.py:52
  94.7 0.1 multiply_reduce_fusion.1
  94.9 16.3 %all_to_all.23 = f32[32,1,8]{2,1,0:T(1,128)S(1)} all-to-all(f32[32,1,8]{2,1,0:T(1,128)S(1)} %broadcast_in_dim.58), channel_id=1, replica_groups=mesh['yh'=2,'x'=4,'c'=2,'yl'=2,'z'=16] {'yl','z'}, dimensions={0} | all-to-all | bytes 2048 | tf_op jit(solution)/shard_map/all_to_all | solution.py:85
  111.2 0.1 reduce_sum.59
  111.3 0.7 divide_convert_fusion
  (8 shorter events, 0.1 us)
Async XLA Ops:
  0.6 11.3 %copy-start = (bf16[32,4096]{1,0:T(8,128)(2,1)S(1)}, bf16[32,4096]{1,0:T(8,128)(2,1)}, u32[]{:S(2)}) copy-start(bf16[32,4096]{1,0:T(8,128)(2,1)} %param.5) | copy-start | bytes 786436
  0.6 11.9 %copy-start.2 = (s32[9,2]{0,1:T(2,128)S(1)}, s32[9,2]{0,1:T(2,128)}, u32[]{:S(2)}) copy-start(s32[9,2]{0,1:T(2,128)} %param.8) | copy-start | bytes 220
  2.6 23.8 %all-to-all-start = ((bf16[16,8,4096]{2,1,0:T(8,128)(2,1)}), bf16[16,8,4096]{2,1,0:T(8,128)(2,1)S(1)}, u32[]{:S(2)}, u32[]{:S(2)}) async-start(bf16[16,8,4096]{2,1,0:T(8,128)(2,1)} %broadcast_in_dim.30), calls=%async_computation | async-start | bytes 2097152 | tf_op jit(solution)/shard_map/all_to_all | solution.py:57
  17.0 6.1 %copy-start.1 = (s32[32,8]{0,1:T(8,128)S(1)}, s32[32,8]{0,1:T(8,128)}, u32[]{:S(2)}) copy-start(s32[32,8]{0,1:T(8,128)} %param.7) | copy-start | bytes 3076
  23.2 3.7 %copy-start.3 = (f32[32]{0:T(128)S(1)}, f32[32]{0:T(128)}, u32[]{:S(2)}) copy-start(f32[32]{0:T(128)} %param.6) | copy-start | bytes 388
  27.9 3.0 %copy-start.4 = (f32[32]{0:T(128)}, f32[32]{0:T(128)S(1)}, u32[]{:S(2)}) copy-start(f32[32]{0:T(128)S(1)} %log_add_fusion) | copy-start | bytes 388
